TPU v7x, 512 devices: a whole 4x8x8 slice. The times are simulated.
512 devices in a mesh: dp: 32 (over y, z_lo, core), seq: 16 (over x, z_hi).
Axes of the slice: x: 4, y: 8, z: 8 (z_hi: 4, z_lo: 2; z = z_hi * 2 + z_lo), core: 2. Of those that a mesh axis runs over, the one named last changes fastest.
Arguments:
- query_rows: bfloat16 [32, 2048, 2048], P('dp', 'seq'), may hold values from -6 to 6
- key_rows: bfloat16 [32, 2048, 2048], P('dp', 'seq'), may hold values from -0.5 to 0.5
- value_rows: bfloat16 [32, 2048, 2048], P('dp', 'seq'), may hold values from -6 to 6
- doc_starts: int32 [32, 2048], P('dp', 'seq'), may hold values 0 or 1
- decay_rates: int32 [16], replicated, may hold values from 1 to 100
- out_gain: float32 [2048], replicated, may hold values from 0.1 to 1.9
- cotangent: bfloat16 [32, 2048, 2048], P('dp', 'seq'), may hold values from -6 to 6
Outputs:
- normed: bfloat16 [32, 2048, 2048], P('dp', 'seq')
- grad_query: bfloat16 [32, 2048, 2048], P('dp', 'seq')
- grad_key: bfloat16 [32, 2048, 2048], P('dp', 'seq')
- grad_value: bfloat16 [32, 2048, 2048], P('dp', 'seq')
- grad_gain: float32 [2048], P('dp')
All inputs are finite; a program needn't handle non-finite values. No bound on the sum of `doc_starts` on one device may be relied on, other than what follows from the above.
Results may differ from a plain program's by a relative error of at most 0.00085.
Values may be sent and summed in bfloat16 or wider, within the bound.
No kernel may reach another device: no remote copies, remote signals or barrier semaphores. Data moves between devices by JAX's collectives and lax.ppermute only.
A program may use at most 64 MiB of HBM per device.

v0:
```python
import math

import jax
import jax.numpy as jnp
from jax import lax
from jax.sharding import PartitionSpec as P

E = 128


highest = lax.Precision.HIGHEST
epsilon = 1e-05


def prefix(part, axis, combine, identity, reverse):
    count = lax.axis_size(axis)
    place = lax.axis_index(axis)
    ahead = count - 1 - place if reverse else place
    gathered = jax.tree.map(lambda a: lax.all_gather(a, axis), part)
    state = jax.tree.map(lambda a, e: jnp.zeros_like(a) + jnp.asarray(e, a.dtype), part, identity)

    def one(hop, state):
        source = count - 1 - hop if reverse else hop
        return combine(
            state, jax.tree.map(lambda a: lax.dynamic_index_in_dim(a, source, 0, False), gathered)
        )

    return lax.fori_loop(0, ahead, one, state)


def block_terms(log_decay, marks):
    length = marks.shape[0]
    counted = jnp.cumsum(marks, dtype=jnp.int32)
    places = jnp.arange(length, dtype=jnp.float32)
    offsets = places[:, None] - places[None, :]
    inside = (counted[:, None] == counted[None, :]) & (offsets >= 0.0)
    weights = jnp.where(
        inside[None], jnp.exp2(log_decay[:, None, None] * jnp.maximum(offsets, 0.0)[None]), 0.0
    )
    fresh = (counted == 0).astype(jnp.float32)
    entry = fresh[:, None] * jnp.exp2(log_decay[None, :] * (places[:, None] + 1.0))
    latest = counted[length - 1]
    tail = jnp.where(
        (counted == latest)[:, None],
        jnp.exp2(log_decay[None, :] * (length - 1.0 - places)[:, None]),
        0.0,
    )
    through = (latest == 0).astype(jnp.float32) * jnp.exp2(log_decay * length)
    return (weights, entry, tail, through)


def state_sum(key_block, value_block, tail):
    return jnp.einsum("jhe,jhf->hef", key_block * tail[:, :, None], value_block, precision=highest)


def out_sum(query_block, key_block, value_block, state_in, weights, entry):
    scores = jnp.einsum("ihe,jhe->hij", query_block, key_block, precision=highest) * weights
    inner = jnp.einsum("hij,jhe->ihe", scores, value_block, precision=highest)
    carried = jnp.einsum("ihe,hef->ihf", query_block, state_in, precision=highest)
    return inner + entry[:, :, None] * carried


def run_chain(through, terms, start, backward):

    def advance(accum, item):
        factor, term = item
        return (factor[:, None, None] * accum + term, accum)

    return lax.scan(advance, start, (through, terms), reverse=backward)


def combine(earlier, later):
    return (earlier[0] * later[0], later[1] + later[0][:, None, None] * earlier[1])


def ahead_state(factor, state):
    result = prefix(
        (factor, state), "seq", combine, (jnp.ones_like(factor), jnp.zeros_like(state)), False
    )
    return result[1]


def behind_grad(factor, state):
    result = prefix(
        (factor, state), "seq", combine, (jnp.ones_like(factor), jnp.zeros_like(state)), True
    )
    return result[1]


def forward_local(query_seq, key_seq, value_seq, marks, log_decay, link):
    length, heads, width = query_seq.shape
    block = math.gcd(length, 512)
    count = length // block
    query_blocks = query_seq.astype(jnp.float32).reshape(count, block, heads, width)
    key_blocks = key_seq.astype(jnp.float32).reshape(count, block, heads, width)
    value_blocks = value_seq.astype(jnp.float32).reshape(count, block, heads, width)
    weights, entry, tail, through = jax.vmap(block_terms, (None, 0))(
        log_decay, marks.reshape(count, block)
    )

    def states_of(key_part, value_part):
        return jax.vmap(state_sum)(key_part, value_part, tail)

    states, state_back = jax.vjp(states_of, key_blocks, value_blocks)
    empty = jnp.zeros((heads, width, width), jnp.float32)
    own_state = run_chain(through, states, empty, False)[0]
    own_factor = jnp.prod(through, axis=0)
    device_in = link(own_factor, own_state)
    block_in = run_chain(through, states, device_in, False)[1]

    def outs_of(query_part, key_part, value_part, state_part):
        return jax.vmap(out_sum)(query_part, key_part, value_part, state_part, weights, entry)

    outs, out_back = jax.vjp(outs_of, query_blocks, key_blocks, value_blocks, block_in)
    saved = (through, own_factor, state_back, out_back, block, count)
    return (outs.reshape(length, heads * width), saved)


def backward_local(grad_rows, saved, link, heads, width):
    through, own_factor, state_back, out_back, block, count = saved
    length = grad_rows.shape[0]
    grad_blocks = grad_rows.reshape(count, block, heads, width)
    grad_q_part, grad_k_part, grad_v_part, grad_state = out_back(grad_blocks)
    empty = jnp.zeros((heads, width, width), jnp.float32)
    own_grad = run_chain(through, grad_state, empty, True)[0]
    device_out = link(own_factor, own_grad)
    block_out = run_chain(through, grad_state, device_out, True)[1]
    extra_key, extra_value = state_back(block_out)
    flat = (length, heads * width)
    return (
        grad_q_part.reshape(flat),
        (grad_k_part + extra_key).reshape(flat),
        (grad_v_part + extra_value).reshape(flat),
    )


def normalize(mixed, out_gain, cotangent):

    def apply(attn, gain_vec):
        scale = lax.rsqrt(jnp.mean(attn * attn, axis=-1, keepdims=True) + epsilon)
        return attn * scale * gain_vec

    result, back = jax.vjp(apply, mixed, out_gain)
    grad_out, gain_part = back(cotangent.astype(jnp.float32))
    return (result.astype(jnp.bfloat16), grad_out, gain_part)


def per_device(query_rows, key_rows, value_rows, doc_starts, decay_rates, out_gain, cotangent):
    local_tokens = query_rows.shape[1]
    total = local_tokens * lax.axis_size("seq")
    log_decay = -decay_rates.astype(jnp.float32) / total
    heads = query_rows.shape[2] // E
    shaped = (local_tokens, heads, E)
    outs, saved = forward_local(
        query_rows[0].reshape(shaped),
        key_rows[0].reshape(shaped),
        value_rows[0].reshape(shaped),
        doc_starts[0],
        log_decay,
        ahead_state,
    )
    normed, grad_out, gain_part = normalize(outs[None], out_gain, cotangent)
    grads = backward_local(grad_out[0], saved, behind_grad, heads, E)
    grad_query = grads[0][None].astype(jnp.bfloat16)
    grad_key = grads[1][None].astype(jnp.bfloat16)
    grad_value = grads[2][None].astype(jnp.bfloat16)
    summed = lax.psum(gain_part, "seq")
    grad_gain = lax.psum_scatter(summed, "dp", scatter_dimension=0, tiled=True)
    return (normed, grad_query, grad_key, grad_value, grad_gain)


def solution(mesh):
    return jax.shard_map(
        per_device,
        mesh=mesh,
        in_specs=(
            P("dp", "seq", None),
            P("dp", "seq", None),
            P("dp", "seq", None),
            P("dp", "seq"),
            P(),
            P(),
            P("dp", "seq", None),
        ),
        out_specs=(
            P("dp", "seq", None),
            P("dp", "seq", None),
            P("dp", "seq", None),
            P("dp", "seq", None),
            P("dp"),
        ),
        check_vma=False,
    )
```

profile of v0, /device:TPU:1, one launch (start us, length us, event | category | flops | bytes accessed | tf_op | source)
XLA Modules:
  0.0 518.3 jit_solution(9662311050770830135)
XLA Ops:
  15.2 2.3 convolution_add_fusion.2
  17.6 46.0 %all-reduce = f32[256]{0:T(256)S(1)} all-reduce(f32[256]{0:T(256)S(1)} %get-tuple-element.232), channel_id=3, replica_groups=mesh['dp'=32,'seq'=16] {'seq'}, use_global_device_ids=true, to_apply=%add | all-reduce | flops 256 | bytes 2048
  65.0 1.5 convolution_multiply_fusion.1
  66.5 165.6 %all-gather.7.cloned.1.call-done = f32[256,128,128]{2,1,0:T(8,128)} async-done(((f32[16,128,128]{2,1,0:T(8,128)}), f32[256,128,128]{2,1,0:T(8,128)}) %all-gather.7.cloned.1.call-update) | async-done | bytes 16777232 | tf_op jit(solution)/shard_map/all_gather | solution.py:19
  233.3 3.4 multiply_reduce_fusion
  236.7 1.6 copy.43
  239.7 2.7 add_add_fusion
  242.4 1.5 copy.46
  243.9 2.7 fusion.4
  246.7 2.5 copy.52
  255.7 55.1 %all-reduce.1 = f32[2048]{0:T(1024)S(1)} all-reduce(f32[2048]{0:T(1024)S(1)} %get-tuple-element.204), channel_id=4, replica_groups=mesh['dp'=32,'seq'=16] {'dp'}, use_global_device_ids=true, to_apply=%region_9.10.clone | all-reduce | flops 2048 | bytes 16384
  310.9 66.8 %psum.8 = f32[64]{0:T(128)} all-reduce(f32[64]{0:T(128)S(1)} %dynamic-slice.5), channel_id=1, replica_groups=mesh['dp'=32,'seq'=16] {'seq'}, use_global_device_ids=true, to_apply=%region_8.9 | all-reduce | flops 64 | bytes 512 | tf_op jit(solution)/shard_map/psum | solution.py:167
  377.7 3.4 fusion.40
  381.2 99.2 %all-gather.5.cloned.1.call-done = f32[16,16,128,128]{3,2,1,0:T(8,128)} async-done(((f32[1,16,128,128]{3,2,1,0:T(8,128)}), f32[16,16,128,128]{3,2,1,0:T(8,128)}) %all-gather.5.cloned.1.call-update) | async-done | bytes 16777232 | tf_op jit(solution)/shard_map/all_gather | solution.py:19
  480.5 22.4 %while.17 = (s32[]{:T(128)}, f32[16,128,128]{2,1,0:T(8,128)S(1)}, s32[]{:T(128)}, f32[16,16,128,128]{3,2,1,0:T(8,128)}, f32[16,16]{1,0:T(8,128)S(1)}, /*index=5*/s32[]{:T(128)}, s32[]{:T(128)}, s32[]{:T(128)}, s32[]{:T(128)}) while((s32[]{:T(128)}, f32[16,128,128]{2,1,0:T(8,128)S(1)}, s32[]{:T(128)}, f32[16,16,128,128]{3,2,1,0:T(8,128)}, ...), condition=%wide.region_6.7_spmd, body=%wide.region_5.6_spmd.sunk | while | flops 524294 | bytes 3146075 | solution.py:28
  480.5 1.4 bitcast_add_fusion.5
  482.0 1.4 bitcast_add_fusion.5
  483.5 1.4 bitcast_add_fusion.5
  485.0 1.4 bitcast_add_fusion.5
  486.5 1.4 bitcast_add_fusion.5
  488.0 1.4 bitcast_add_fusion.5
  489.5 1.4 bitcast_add_fusion.5
  491.0 1.4 bitcast_add_fusion.5
  492.5 1.4 bitcast_add_fusion.5
  494.0 1.4 bitcast_add_fusion.5
  495.4 1.4 bitcast_add_fusion.5
  496.9 1.4 bitcast_add_fusion.5
  498.4 1.4 bitcast_add_fusion.5
  499.9 1.4 bitcast_add_fusion.5
  501.4 1.4 bitcast_add_fusion.5
  504.1 3.5 fusion.8
  507.6 1.8 fusion.6
  (57 shorter events, 20.0 us)
Async XLA Ops:
  7.2 225.0 %all-gather.7.cloned.1.call-start = ((), (), s32[]{:S(2)}) async-start(), calls=%async_computation.1 | async-start | bytes 17825792 | tf_op jit(solution)/shard_map/all_gather | solution.py:19
  11.2 227.0 %copy-start.3 = (f32[2048]{0:T(1024)S(1)}, f32[2048]{0:T(1024)}, u32[]{:S(2)}) copy-start(f32[2048]{0:T(1024)} %param.16) | copy-start | bytes 24580
  17.6 462.8 %all-gather.5.cloned.1.call-start = ((), (), s32[]{:S(2)}) async-start(), calls=%async_computation | async-start | bytes 17825792 | tf_op jit(solution)/shard_map/all_gather | solution.py:19
  64.9 171.8 %copy-start.2 = (bf16[16,8,16,128]{3,2,1,0:T(8,128)(2,1)}, bf16[16,8,16,128]{3,2,1,0:T(8,128)(2,1)S(1)}, u32[]{:S(2)}) copy-start(bf16[16,8,16,128]{3,2,1,0:T(8,128)(2,1)S(1)} %copy.62) | copy-start | bytes 1572868
  252.4 1.1 copy-start
  381.2 126.4 %copy-start.1 = (f32[16,128,128]{2,1,0:T(8,128)S(1)}, f32[16,128,128]{2,1,0:T(8,128)}, u32[]{:S(2)}) copy-start(f32[16,128,128]{2,1,0:T(8,128)} %copy-done) | copy-start | bytes 3145732
Sparse Core Ops, SparseCore 0:
  17.7 214.4 all-gather.6
  249.3 230.9 all-gather.4
where the time goes:
time: 520 us; the launch traced here: 518 us
  waiting for transfers between devices  265 us (51%)
  blocking collectives  168 us (32%)
  other arithmetic  28.4 us (5%)
  matrix products  24.6 us (5%)
  between operations  16.2 us (3%)
  local copies, waits for them, and re-layouts  15.8 us (3%)
    all_gather x2, waiting for transfers between devices, prefix(): gathered = jax.tree.map(lambda a: lax.all_gather(a, axis), part)  265 us
    unnamed x2, blocking collectives  101 us
    psum x1, blocking collectives, per_device(): summed = lax.psum(gain_part, 'seq')  66.8 us
    add x15, other arithmetic, combine(): later[1] + later[0][:, None, None] * earlier[1]  21.7 us
  transfers between devices with their start and end apart: 2, of which 2 were waited for; matrix products, arithmetic and copies ran while one was open for 2% of the time, Pallas kernels for 0%

commit v1 on v0

--- a/solution.py
+++ b/solution.py
@@ -12,20 +12,32 @@
 epsilon = 1e-05
 
 
-def prefix(part, axis, combine, identity, reverse):
-    count = lax.axis_size(axis)
-    place = lax.axis_index(axis)
-    ahead = count - 1 - place if reverse else place
-    gathered = jax.tree.map(lambda a: lax.all_gather(a, axis), part)
-    state = jax.tree.map(lambda a, e: jnp.zeros_like(a) + jnp.asarray(e, a.dtype), part, identity)
+def pack(factor, state):
+    heads, width, _ = state.shape
+    rows = jnp.broadcast_to(factor[:, None, None], (heads, 8, width))
+    return jnp.concatenate([state, rows], axis=1)
 
-    def one(hop, state):
-        source = count - 1 - hop if reverse else hop
-        return combine(
-            state, jax.tree.map(lambda a: lax.dynamic_index_in_dim(a, source, 0, False), gathered)
-        )
 
-    return lax.fori_loop(0, ahead, one, state)
+def scan_exclusive(factor, state, reverse):
+    count = lax.axis_size("seq")
+    width = state.shape[1]
+    run_factor, run_state = factor, state
+    out_factor, out_state = jnp.ones_like(factor), jnp.zeros_like(state)
+    distance = 1
+    while distance < count:
+        if reverse:
+            pairs = [(i, i - distance) for i in range(distance, count)]
+        else:
+            pairs = [(i, i + distance) for i in range(count - distance)]
+        got = lax.ppermute(pack(run_factor, run_state), "seq", pairs)
+        got_state, got_factor = got[:, :width], got[:, width, 0]
+        out_state = out_state + out_factor[:, None, None] * got_state
+        out_factor = out_factor * got_factor
+        if distance * 2 < count:
+            run_state = run_state + run_factor[:, None, None] * got_state
+            run_factor = run_factor * got_factor
+        distance *= 2
+    return out_state
 
 
 def block_terms(log_decay, marks):
@@ -69,22 +81,12 @@
     return lax.scan(advance, start, (through, terms), reverse=backward)
 
 
-def combine(earlier, later):
-    return (earlier[0] * later[0], later[1] + later[0][:, None, None] * earlier[1])
-
-
 def ahead_state(factor, state):
-    result = prefix(
-        (factor, state), "seq", combine, (jnp.ones_like(factor), jnp.zeros_like(state)), False
-    )
-    return result[1]
+    return scan_exclusive(factor, state, False)
 
 
 def behind_grad(factor, state):
-    result = prefix(
-        (factor, state), "seq", combine, (jnp.ones_like(factor), jnp.zeros_like(state)), True
-    )
-    return result[1]
+    return scan_exclusive(factor, state, True)
 
 
 def forward_local(query_seq, key_seq, value_seq, marks, log_decay, link):
@@ -164,8 +166,9 @@
     grad_query = grads[0][None].astype(jnp.bfloat16)
     grad_key = grads[1][None].astype(jnp.bfloat16)
     grad_value = grads[2][None].astype(jnp.bfloat16)
-    summed = lax.psum(gain_part, "seq")
-    grad_gain = lax.psum_scatter(summed, "dp", scatter_dimension=0, tiled=True)
+    summed = lax.psum(gain_part, ("dp", "seq"))
+    share = summed.shape[-1] // lax.axis_size("dp")
+    grad_gain = lax.dynamic_slice_in_dim(summed, lax.axis_index("dp") * share, share)
     return (normed, grad_query, grad_key, grad_value, grad_gain)
 
 

time: 520 us -> 499 us (0.960)
  blocking collectives: 168 us -> 108 us
  starting transfers between devices: 0.08 us -> 57.6 us
  waiting for transfers between devices: 265 us -> 283 us
  between operations: 16.2 us -> 1.78 us
  other arithmetic: 28.4 us -> 16.4 us
  matrix products: 24.6 us -> 17.2 us
    ppermute x0 -> x8, waiting for transfers between devices: none -> 283 us  [scan_exclusive(): got = lax.ppermute(pack(run_factor, run_state), 'seq', pairs)]
    all_gather x2 -> x0, waiting for transfers between devices: 265 us -> none  [prefix(): gathered = jax.tree.map(lambda a: lax.all_gather(a, axis), part)]
    unnamed x2 -> x0, blocking collectives: 101 us -> none
    ppermute x0 -> x8, starting transfers between devices: none -> 57.6 us  [scan_exclusive(): got = lax.ppermute(pack(run_factor, run_state), 'seq', pairs)]
    psum x1, blocking collectives: 66.8 us -> 108 us  [per_device(): summed = lax.psum(gain_part, ('dp', 'seq'))]
    add x15 -> x8, other arithmetic: 21.7 us -> 5.72 us  [the longest x2 3.5 us: scan_exclusive(): out_state = out_state + out_factor[:, None, None] * got_state]
  transfers between devices with their start and end apart: 2 -> 8, of which waited for: 2 -> 7; matrix products, arithmetic and copies ran while one was open for 2% -> 2% of each run, Pallas kernels for 0% -> 0%
where the time goes in v1:
time: 499 us; the launch traced here: 498 us
  waiting for transfers between devices  283 us (57%)
  blocking collectives  108 us (22%)
  starting transfers between devices  57.6 us (12%)
  matrix products  17.2 us (3%)
  other arithmetic  16.4 us (3%)
  local copies, waits for them, and re-layouts  13.5 us (3%)
    ppermute x8, waiting for transfers between devices, scan_exclusive(): got = lax.ppermute(pack(run_factor, run_state), 'seq', pairs)  283 us
    psum x1, blocking collectives, per_device(): summed = lax.psum(gain_part, ('dp', 'seq'))  108 us
    ppermute x8, starting transfers between devices, scan_exclusive(): got = lax.ppermute(pack(run_factor, run_state), 'seq', pairs)  57.6 us
  transfers between devices with their start and end apart: 8, of which 7 were waited for; matrix products, arithmetic and copies ran while one was open for 2% of the time, Pallas kernels for 0%

profile of v1, /device:TPU:1, one launch (start us, length us, event | category | flops | bytes accessed | tf_op | source)
XLA Modules:
  0.0 497.9 jit_solution(8573685035798244976)
XLA Ops:
  5.0 1.3 convolution_add_fusion.2
  7.5 6.7 %collective-permute-start = (f32[16,136,128]{2,1,0:T(8,128)}, f32[16,136,128]{2,1,0:T(8,128)S(1)}, u32[]{:S(2)}, u32[]{:S(2)}) collective-permute-start(f32[16,136,128]{2,1,0:T(8,128)} %pad_maximum_fusion.1), channel_id=1, source_target_pairs={{0,1},{1,2},{2,3},{3,4},{4,5},{5,6},{6,7},{7,8},{8,9},{9,10},{10,1... | collective-permute-start | bytes 3342344 | tf_op jit(solution)/shard_map/ppermute | solution.py:32
  14.3 22.9 %collective-permute-done = f32[16,136,128]{2,1,0:T(8,128)S(1)} collective-permute-done((f32[16,136,128]{2,1,0:T(8,128)}, f32[16,136,128]{2,1,0:T(8,128)S(1)}, u32[]{:S(2)}, u32[]{:S(2)}) %collective-permute-start) | collective-permute-done | bytes 1114144 | tf_op jit(solution)/shard_map/ppermute | solution.py:32
  37.7 35.3 %collective-permute-start.1 = (f32[16,136,128]{2,1,0:T(8,128)S(1)}, f32[16,136,128]{2,1,0:T(8,128)S(1)}, u32[]{:S(2)}, u32[]{:S(2)}) collective-permute-start(f32[16,136,128]{2,1,0:T(8,128)S(1)} %pad_maximum_fusion.2), channel_id=1, source_target_pairs={{0,2},{1,3},{2,4},{3,5},{4,6},{5,7},{6,8},{7,9},{8,10},{9,11},{10,... | collective-permute-start | bytes 3342344 | tf_op jit(solution)/shard_map/ppermute | solution.py:32
  73.0 29.5 %collective-permute-done.1 = f32[16,136,128]{2,1,0:T(8,128)S(1)} collective-permute-done((f32[16,136,128]{2,1,0:T(8,128)S(1)}, f32[16,136,128]{2,1,0:T(8,128)S(1)}, u32[]{:S(2)}, u32[]{:S(2)}) %collective-permute-start.1) | collective-permute-done | bytes 1114144 | tf_op jit(solution)/shard_map/ppermute | solution.py:32
  103.9 3.9 collective-permute-start.2
  107.8 12.4 %collective-permute-done.2 = f32[16,136,128]{2,1,0:T(8,128)S(1)} collective-permute-done((f32[16,136,128]{2,1,0:T(8,128)S(1)}, f32[16,136,128]{2,1,0:T(8,128)S(1)}, u32[]{:S(2)}, u32[]{:S(2)}) %collective-permute-start.2) | collective-permute-done | bytes 1114144 | tf_op jit(solution)/shard_map/ppermute | solution.py:32
  122.5 6.3 %collective-permute-start.3 = (f32[16,136,128]{2,1,0:T(8,128)}, f32[16,136,128]{2,1,0:T(8,128)}, u32[]{:S(2)}, u32[]{:S(2)}) collective-permute-start(f32[16,136,128]{2,1,0:T(8,128)} %pad_maximum_fusion.4), channel_id=1, source_target_pairs={{0,8},{1,9},{2,10},{3,11},{4,12},{5,13},{6,14},{7,15},{16,24},{17,... | collective-permute-start | bytes 3342344 | tf_op jit(solution)/shard_map/ppermute | solution.py:32
  129.9 1.2 convolution_bitcast_fusion.4
  131.1 20.1 %collective-permute-done.3 = f32[16,136,128]{2,1,0:T(8,128)} collective-permute-done((f32[16,136,128]{2,1,0:T(8,128)}, f32[16,136,128]{2,1,0:T(8,128)}, u32[]{:S(2)}, u32[]{:S(2)}) %collective-permute-start.3) | collective-permute-done | bytes 1114144 | tf_op jit(solution)/shard_map/ppermute | solution.py:32
  151.2 1.6 fusion.13
  152.8 2.0 multiply_reduce_fusion
  154.8 1.6 copy.45
  156.9 1.6 add_add_fusion
  158.6 1.5 copy.48
  160.1 1.2 fusion
  161.4 1.3 collective-permute-start.4
  162.7 80.2 %collective-permute-done.4 = f32[16,136,128]{2,1,0:T(8,128)S(1)} collective-permute-done((f32[16,136,128]{2,1,0:T(8,128)S(1)}, f32[16,136,128]{2,1,0:T(8,128)S(1)}, u32[]{:S(2)}, u32[]{:S(2)}) %collective-permute-start.4) | collective-permute-done | bytes 1114144 | tf_op jit(solution)/shard_map/ppermute | solution.py:32
  243.5 1.3 collective-permute-start.5
  244.8 74.5 %collective-permute-done.5 = f32[16,136,128]{2,1,0:T(8,128)S(1)} collective-permute-done((f32[16,136,128]{2,1,0:T(8,128)S(1)}, f32[16,136,128]{2,1,0:T(8,128)S(1)}, u32[]{:S(2)}, u32[]{:S(2)}) %collective-permute-start.5) | collective-permute-done | bytes 1114144 | tf_op jit(solution)/shard_map/ppermute | solution.py:32
  321.7 1.3 collective-permute-start.6
  322.9 43.6 %collective-permute-done.6 = f32[16,136,128]{2,1,0:T(8,128)} collective-permute-done((f32[16,136,128]{2,1,0:T(8,128)}, f32[16,136,128]{2,1,0:T(8,128)}, u32[]{:S(2)}, u32[]{:S(2)}) %collective-permute-start.6) | collective-permute-done | bytes 1114144 | tf_op jit(solution)/shard_map/ppermute | solution.py:32
  366.6 1.4 multiply_add_fusion
  370.2 1.5 collective-permute-start.7
  371.7 1.2 convolution_multiply_fusion
  374.1 2.0 fusion.5
  376.1 2.0 copy.57
  378.2 108.3 %psum.7 = f32[2048]{0:T(1024)S(1)} all-reduce(f32[2048]{0:T(1024)S(1)} %get-tuple-element.64), channel_id=1, replica_groups=mesh['dp'=32,'seq'=16] {'dp','seq'}, use_global_device_ids=true, to_apply=%region_4.5 | all-reduce | flops 2048 | bytes 16384 | tf_op jit(solution)/shard_map/psum | solution.py:169
  487.0 1.8 convolution_bitcast_fusion.2
  490.4 1.9 fusion.12
  492.4 2.3 fusion.6
  494.7 1.2 fusion.7
  (88 shorter events, 21.0 us)
Async XLA Ops:
  0.6 4.1 copy-start.16
  0.6 4.2 copy-start.19
  7.5 29.7 %collective-permute-start = (f32[16,136,128]{2,1,0:T(8,128)}, f32[16,136,128]{2,1,0:T(8,128)S(1)}, u32[]{:S(2)}, u32[]{:S(2)}) collective-permute-start(f32[16,136,128]{2,1,0:T(8,128)} %pad_maximum_fusion.1), channel_id=1, source_target_pairs={{0,1},{1,2},{2,3},{3,4},{4,5},{5,6},{6,7},{7,8},{8,9},{9,10},{10,1... | collective-permute-start | bytes 3342344 | tf_op jit(solution)/shard_map/ppermute | solution.py:32
  37.1 65.6 %copy-start.7 = (f32[16,136,128]{2,1,0:T(8,128)}, f32[16,136,128]{2,1,0:T(8,128)S(1)}, u32[]{:S(2)}) copy-start(f32[16,136,128]{2,1,0:T(8,128)S(1)} %collective-permute-done) | copy-start | bytes 3342340
  37.7 64.8 %collective-permute-start.1 = (f32[16,136,128]{2,1,0:T(8,128)S(1)}, f32[16,136,128]{2,1,0:T(8,128)S(1)}, u32[]{:S(2)}, u32[]{:S(2)}) collective-permute-start(f32[16,136,128]{2,1,0:T(8,128)S(1)} %pad_maximum_fusion.2), channel_id=1, source_target_pairs={{0,2},{1,3},{2,4},{3,5},{4,6},{5,7},{6,8},{7,9},{8,10},{9,11},{10,... | collective-permute-start | bytes 3342344 | tf_op jit(solution)/shard_map/ppermute | solution.py:32
  102.5 1.0 copy-start.11
  103.9 16.3 %collective-permute-start.2 = (f32[16,136,128]{2,1,0:T(8,128)S(1)}, f32[16,136,128]{2,1,0:T(8,128)S(1)}, u32[]{:S(2)}, u32[]{:S(2)}) collective-permute-start(f32[16,136,128]{2,1,0:T(8,128)S(1)} %pad_maximum_fusion.3), channel_id=1, source_target_pairs={{0,4},{1,5},{2,6},{3,7},{4,8},{5,9},{6,10},{7,11},{8,12},{9,13},{1... | collective-permute-start | bytes 3342344 | tf_op jit(solution)/shard_map/ppermute | solution.py:32
  120.2 1.0 copy-start.13
  121.5 7.4 %copy-start.17 = (bf16[1,128,2048]{2,1,0:T(8,128)(2,1)S(1)}, bf16[1,128,2048]{2,1,0:T(8,128)(2,1)}, u32[]{:S(2)}) copy-start(bf16[1,128,2048]{2,1,0:T(8,128)(2,1)} %param.7) | copy-start | bytes 1572868
  122.5 28.6 %collective-permute-start.3 = (f32[16,136,128]{2,1,0:T(8,128)}, f32[16,136,128]{2,1,0:T(8,128)}, u32[]{:S(2)}, u32[]{:S(2)}) collective-permute-start(f32[16,136,128]{2,1,0:T(8,128)} %pad_maximum_fusion.4), channel_id=1, source_target_pairs={{0,8},{1,9},{2,10},{3,11},{4,12},{5,13},{6,14},{7,15},{16,24},{17,... | collective-permute-start | bytes 3342344 | tf_op jit(solution)/shard_map/ppermute | solution.py:32
  129.2 30.9 %copy-start.2 = (bf16[1,128,2048]{1,2,0:T(8,128)(2,1)}, bf16[1,128,2048]{1,2,0:T(8,128)(2,1)S(1)}, u32[]{:S(2)}) copy-start(bf16[1,128,2048]{1,2,0:T(8,128)(2,1)S(1)} %copy.64) | copy-start | bytes 1572868
  129.3 21.9 %copy-start.14 = (f32[16,136,128]{2,1,0:T(8,128)S(1)}, f32[16,136,128]{2,1,0:T(8,128)}, u32[]{:S(2)}) copy-start(f32[16,136,128]{2,1,0:T(8,128)} %copy-done.13) | copy-start | bytes 3342340
  129.8 1.2 copy-start.3
  129.9 21.3 %copy-start.8 = (f32[16,136,128]{2,1,0:T(8,128)S(1)}, f32[16,136,128]{2,1,0:T(8,128)}, u32[]{:S(2)}) copy-start(f32[16,136,128]{2,1,0:T(8,128)} %copy-done.7) | copy-start | bytes 3342340
  129.9 21.3 %copy-start.12 = (f32[16,136,128]{2,1,0:T(8,128)S(1)}, f32[16,136,128]{2,1,0:T(8,128)}, u32[]{:S(2)}) copy-start(f32[16,136,128]{2,1,0:T(8,128)} %copy-done.11) | copy-start | bytes 3342340
  152.8 2.0 copy-start
  154.8 1.6 copy-start.15
  154.8 1.6 copy-start.18
  161.4 81.5 %collective-permute-start.4 = (f32[16,136,128]{2,1,0:T(8,128)S(1)}, f32[16,136,128]{2,1,0:T(8,128)S(1)}, u32[]{:S(2)}, u32[]{:S(2)}) collective-permute-start(f32[16,136,128]{2,1,0:T(8,128)S(1)} %pad_maximum_fusion), channel_id=1, source_target_pairs={{1,0},{2,1},{3,2},{4,3},{5,4},{6,5},{7,6},{8,7},{9,8},{10,9},{11,1... | collective-permute-start | bytes 3342344 | tf_op jit(solution)/shard_map/ppermute | solution.py:32
  242.9 76.5 %copy-start.5 = (f32[16,136,128]{2,1,0:T(8,128)}, f32[16,136,128]{2,1,0:T(8,128)S(1)}, u32[]{:S(2)}) copy-start(f32[16,136,128]{2,1,0:T(8,128)S(1)} %collective-permute-done.4) | copy-start | bytes 3342340
  243.5 75.8 %collective-permute-start.5 = (f32[16,136,128]{2,1,0:T(8,128)S(1)}, f32[16,136,128]{2,1,0:T(8,128)S(1)}, u32[]{:S(2)}, u32[]{:S(2)}) collective-permute-start(f32[16,136,128]{2,1,0:T(8,128)S(1)} %pad_maximum_fusion.5), channel_id=1, source_target_pairs={{2,0},{3,1},{4,2},{5,3},{6,4},{7,5},{8,6},{9,7},{10,8},{11,9},{12,... | collective-permute-start | bytes 3342344 | tf_op jit(solution)/shard_map/ppermute | solution.py:32
  319.3 1.0 copy-start.9
  321.7 44.9 %collective-permute-start.6 = (f32[16,136,128]{2,1,0:T(8,128)}, f32[16,136,128]{2,1,0:T(8,128)}, u32[]{:S(2)}, u32[]{:S(2)}) collective-permute-start(f32[16,136,128]{2,1,0:T(8,128)} %pad_maximum_fusion.6), channel_id=1, source_target_pairs={{4,0},{5,1},{6,2},{7,3},{8,4},{9,5},{10,6},{11,7},{12,8},{13,9},{1... | collective-permute-start | bytes 3342344 | tf_op jit(solution)/shard_map/ppermute | solution.py:32
  370.2 119.8 %collective-permute-start.7 = (f32[16,136,128]{2,1,0:T(8,128)}, f32[16,136,128]{2,1,0:T(8,128)}, u32[]{:S(2)}, u32[]{:S(2)}) collective-permute-start(f32[16,136,128]{2,1,0:T(8,128)} %pad_maximum_fusion.7), channel_id=1, source_target_pairs={{8,0},{9,1},{10,2},{11,3},{12,4},{13,5},{14,6},{15,7},{24,16},{25,... | collective-permute-start | bytes 3342344 | tf_op jit(solution)/shard_map/ppermute | solution.py:32
  372.9 1.2 copy-start.1
  487.0 1.8 copy-start.4
  488.8 1.2 copy-start.6
  488.9 1.6 copy-start.10

commit v2 on v0

v2 whole, which is shorter than its diff:
```python
import jax
import jax.numpy as jnp
from jax import lax
from jax.sharding import PartitionSpec as P

E = 128
CHUNK = 128


highest = lax.Precision.HIGHEST
epsilon = 1e-05


def block_terms(log_decay, marks):
    length = marks.shape[0]
    counted = jnp.cumsum(marks, dtype=jnp.int32)
    places = jnp.arange(length, dtype=jnp.float32)
    offsets = places[:, None] - places[None, :]
    inside = (counted[:, None] == counted[None, :]) & (offsets >= 0.0)
    weights = jnp.where(
        inside[None], jnp.exp2(log_decay[:, None, None] * jnp.maximum(offsets, 0.0)[None]), 0.0
    )
    fresh = (counted == 0).astype(jnp.float32)
    entry = fresh[:, None] * jnp.exp2(log_decay[None, :] * (places[:, None] + 1.0))
    latest = counted[length - 1]
    tail = jnp.where(
        (counted == latest)[:, None],
        jnp.exp2(log_decay[None, :] * (length - 1.0 - places)[:, None]),
        0.0,
    )
    return (weights, entry, tail)


def state_sum(key_block, value_block, tail):
    return jnp.einsum("jhe,jhf->hef", key_block * tail[:, :, None], value_block, precision=highest)


def out_sum(query_block, key_block, value_block, state_in, weights, entry):
    scores = jnp.einsum("ihe,jhe->hij", query_block, key_block, precision=highest) * weights
    inner = jnp.einsum("hij,jhe->ihe", scores, value_block, precision=highest)
    carried = jnp.einsum("ihe,hef->ihf", query_block, state_in, precision=highest)
    return inner + entry[:, :, None] * carried


def chunk_mixing(log_decay, marks, count, length):
    starts = jnp.cumsum(jnp.sum(marks.reshape(count, length), axis=1), dtype=jnp.int32)
    chunk = jnp.arange(count)
    before = jnp.where(chunk >= 1, starts[jnp.maximum(chunk - 1, 0)], 0)
    clear = (chunk[None, :] < chunk[:, None]) & (before[:, None] - starts[None, :] == 0)
    gap = jnp.maximum(chunk[:, None] - chunk[None, :] - 1, 0).astype(jnp.float32)
    return jnp.where(clear[None], jnp.exp2(log_decay[:, None, None] * (length * gap)[None]), 0.0)


def local_attention(query_seq, key_seq, value_seq, marks, log_decay):
    tokens, heads, width = query_seq.shape
    length = CHUNK
    count = tokens // length

    def split(rows):
        return rows.reshape(count, length, heads, width)

    query_blocks, key_blocks, value_blocks = split(query_seq), split(key_seq), split(value_seq)
    weights, entry, tail = jax.vmap(block_terms, (None, 0))(log_decay, marks.reshape(count, length))
    states = jax.vmap(state_sum)(key_blocks, value_blocks, tail)
    mixing = chunk_mixing(log_decay, marks, count, length)
    block_in = jnp.einsum("hcd,dhef->chef", mixing, states, precision=highest)
    outs = jax.vmap(out_sum)(query_blocks, key_blocks, value_blocks, block_in, weights, entry)
    return outs.reshape(tokens, heads * width)


def per_device(query_rows, key_rows, value_rows, doc_starts, decay_rates, out_gain, cotangent):
    count = lax.axis_size("seq")
    place = lax.axis_index("seq")
    local_tokens, features = query_rows.shape[1], query_rows.shape[2]
    tokens = local_tokens * count
    heads = features // E // count
    width = heads * E
    log_decay = lax.dynamic_slice_in_dim(-decay_rates.astype(jnp.float32) / tokens, place * heads, heads)
    gain = lax.dynamic_slice_in_dim(out_gain, place * width, width)

    stacked = jnp.stack([query_rows[0], key_rows[0], value_rows[0], cotangent[0]])
    stacked = stacked.reshape(4, local_tokens, count, width)
    moved = lax.all_to_all(stacked, "seq", 2, 1, tiled=True).reshape(4, tokens, heads, E)
    marks = lax.all_gather(doc_starts[0], "seq", tiled=True)

    query_seq, key_seq, value_seq = (moved[i].astype(jnp.float32) for i in range(3))
    grad_rows = moved[3].astype(jnp.float32).reshape(tokens, width)
    attn, back = jax.vjp(
        lambda q, k, v: local_attention(q, k, v, marks, log_decay), query_seq, key_seq, value_seq
    )
    stats = jnp.stack([jnp.sum(attn * attn, axis=-1), jnp.sum(attn * gain * grad_rows, axis=-1)])
    totals = lax.psum(stats, "seq")
    scale = lax.rsqrt(totals[0] / features + epsilon)[:, None]
    normed = attn * scale * gain
    grad_attn = gain * grad_rows * scale - attn * (scale**3 * (totals[1] / features)[:, None])
    gain_part = jnp.sum(grad_rows * attn * scale, axis=0)
    grad_q, grad_k, grad_v = back(grad_attn)

    outs = jnp.stack(
        [normed, grad_q.reshape(tokens, width), grad_k.reshape(tokens, width), grad_v.reshape(tokens, width)]
    ).astype(jnp.bfloat16)
    outs = outs.reshape(4, count, local_tokens, width)
    returned = lax.all_to_all(outs, "seq", 1, 3, tiled=True).reshape(4, 1, local_tokens, features)

    gain_seq = jnp.sum(lax.all_gather(gain_part, "dp"), axis=0)
    gain_all = lax.all_gather(gain_seq, "seq", tiled=True)
    share = features // lax.axis_size("dp")
    grad_gain = lax.dynamic_slice_in_dim(gain_all, lax.axis_index("dp") * share, share)
    return (returned[0], returned[1], returned[2], returned[3], grad_gain)


def solution(mesh):
    return jax.shard_map(
        per_device,
        mesh=mesh,
        in_specs=(
            P("dp", "seq", None),
            P("dp", "seq", None),
            P("dp", "seq", None),
            P("dp", "seq"),
            P(),
            P(),
            P("dp", "seq", None),
        ),
        out_specs=(
            P("dp", "seq", None),
            P("dp", "seq", None),
            P("dp", "seq", None),
            P("dp", "seq", None),
            P("dp"),
        ),
        check_vma=False,
    )
```

time: 520 us -> 338 us (0.65)
  waiting for transfers between devices: 265 us -> 0.01 us
  blocking collectives: 168 us -> 249 us
  other arithmetic: 28.4 us -> 5.35 us
  starting transfers between devices: 0.08 us -> 18 us
  between operations: 16.2 us -> 1.6 us
  local copies, waits for them, and re-layouts: 15.8 us -> 29.9 us
    all_gather x2 -> x0, waiting for transfers between devices: 265 us -> none  [prefix(): gathered = jax.tree.map(lambda a: lax.all_gather(a, axis), part)]
    all_gather x0 -> x3, blocking collectives: none -> 186 us  [the longest x1 77.8 us: per_device(): gain_seq = jnp.sum(lax.all_gather(gain_part, 'dp'), axis=0)]
    unnamed x2 -> x0, blocking collectives: 101 us -> none
    add x15 -> x0, other arithmetic: 21.7 us -> none  [combine(): later[1] + later[0][:, None, None] * earlier[1]]
    all_to_all x0 -> x2, starting transfers between devices: none -> 18 us  [the longest x1 13.6 us: per_device(): lax.all_to_all(stacked, 'seq', 2, 1, tiled=True)]
    unnamed x18 -> x32, local copies, waits for them, and re-layouts: 9.12 us -> 11.8 us
  transfers between devices with their start and end apart: 2 -> 2, of which waited for: 2 -> 0; matrix products, arithmetic and copies ran while one was open for 2% -> 2% of each run, Pallas kernels for 0% -> 0%
where the time goes in v2:
time: 338 us; the launch traced here: 333 us
  blocking collectives  249 us (74%)
  local copies, waits for them, and re-layouts  29.9 us (9%)
  matrix products  29.7 us (9%)
  starting transfers between devices  18 us (5%)
  other arithmetic  5.35 us (2%)
    all_gather x1, blocking collectives, per_device(): gain_seq = jnp.sum(lax.all_gather(gain_part, 'dp'), axis=0)  77.8 us
    all_gather x1, blocking collectives, per_device(): marks = lax.all_gather(doc_starts[0], 'seq', tiled=True)  72.9 us
    psum x1, blocking collectives, per_device(): totals = lax.psum(stats, 'seq')  63.1 us
    all_gather x1, blocking collectives, per_device(): gain_all = lax.all_gather(gain_seq, 'seq', tiled=True)  35.1 us
    all_to_all x1, starting transfers between devices, per_device(): lax.all_to_all(stacked, 'seq', 2, 1, tiled=True)  13.6 us
    unnamed x32, local copies, waits for them, and re-layouts  11.8 us
    dot_general x3, matrix products, out_sum(): inner = jnp.einsum('hij,jhe->ihe', scores, value_block, precision=highest)  8.88 us
    dot_general x3, matrix products, out_sum(): jnp.einsum('ihe,hef->ihf', query_block, state_in, precision=highest)  7.95 us
  transfers between devices with their start and end apart: 2, of which 0 were waited for; matrix products, arithmetic and copies ran while one was open for 2% of the time, Pallas kernels for 0%

profile of v2, /device:TPU:1, one launch (start us, length us, event | category | flops | bytes accessed | tf_op | source)
XLA Modules:
  0.0 333.5 jit_solution(796169840298171184)
XLA Ops:
  0.7 1.4 copy.57
  2.1 1.3 copy.58
  5.4 1.5 pad_maximum_fusion
  6.9 2.6 copy.61
  9.5 13.6 %all-to-all-start = ((bf16[4,128,16,128]{3,1,0,2:T(8,128)(2,1)}), bf16[4,128,16,128]{3,1,0,2:T(8,128)(2,1)}, u32[]{:S(2)}, u32[]{:S(2)}) async-start(bf16[4,128,16,128]{3,1,0,2:T(8,128)(2,1)} %copy.61), calls=%async_computation | async-start | bytes 4194304 | tf_op jit(solution)/shard_map/all_to_all | solution.py:83
  23.1 72.9 %all-gather = s32[1,2048]{1,0:T(1,128)S(1)} all-gather(s32[1,128]{1,0:T(1,128)S(1)} %copy-done.10), channel_id=2, replica_groups=mesh['dp'=32,'seq'=16] {'seq'}, dimensions={1}, use_global_device_ids=true | all-gather | bytes 8704 | tf_op jit(solution)/shard_map/all_gather | solution.py:84
  101.1 1.7 copy.106
  102.8 1.3 fusion.26
  104.6 1.6 convolution_bitcast_fusion.1
  107.3 1.1 fusion.1
  108.4 1.3 fusion.24
  109.6 63.1 %psum.7 = f32[2,2048]{1,0:T(2,128)S(1)} all-reduce(f32[2,2048]{1,0:T(2,128)S(1)} %pad_maximum_fusion.2), channel_id=1, replica_groups=mesh['dp'=32,'seq'=16] {'seq'}, use_global_device_ids=true, to_apply=%region_5.6 | all-reduce | flops 4096 | bytes 32768 | tf_op jit(solution)/shard_map/psum | solution.py:92
  172.8 4.7 %fusion.18 = f32[16,128,128]{1,2,0:T(8,128)} fusion(f32[16,128,128]{2,1,0:T(8,128)} %copy-done.6, f32[16,1,128,128]{2,3,0,1:T(8,128)S(1)} %get-tuple-element.25, f32[16,128]{1,0:T(8,128)S(1)} %fusion.36, f32[16,128]{1,0:T(8,128)S(1)} %bitcast.199, f32[128]{0:T(128)S(1)} %dynamic_slice.10, bf16[4,16,128,1,128]{4,2,1,3,0:T(8,128)(2,1)S(1)} %bitcast.183), kind=kOutput, calls=%fused_computation.37 | convolution fusion | flops 403963904 | bytes 3686912 | tf_op jit(solution)/shard_map/transpose(jvp(vmap(hij,jhe->ihe)))/dot_general | solution.py:40
  177.5 3.9 %fusion.22 = f32[16,128,128]{2,1,0:T(8,128)} fusion(f32[16,128,128]{2,0,1:T(8,128)S(1)} %copy-done.2, f32[16,128]{1,0:T(8,128)S(1)} %get-tuple-element.23, f32[16,1,128,128]{2,3,0,1:T(8,128)S(1)} %get-tuple-element.25, f32[16,128]{1,0:T(8,128)S(1)} %fusion.36, f32[16,128]{1,0:T(8,128)S(1)} %bitcast.200, f32[128]{0:T(128)S(1)} %dynamic_slice.10, ...), kind=kOutput, calls=%fused_computation.41 | convolution fusion | flops 404226048 | bytes 3695104 | tf_op jit(solution)/shard_map/transpose(jvp(vmap(ihe,hef->ihf)))/dot_general | solution.py:41
  181.4 1.1 fusion.17
  182.6 2.9 select_multiply_fusion
  185.5 3.0 convolution_bitcast_fusion.3
  188.4 2.6 copy.74
  191.1 3.2 convolution_bitcast_fusion
  194.3 2.6 copy.78
  196.8 2.1 fusion.4
  199.0 2.3 fusion.8
  202.1 1.0 fusion.10
  203.4 1.4 copy.81
  204.8 4.4 %all-to-all-start.1 = ((bf16[4,16,128,128]{3,2,0,1:T(8,128)(2,1)}), bf16[4,16,128,128]{3,2,0,1:T(8,128)(2,1)}, u32[]{:S(2)}, u32[]{:S(2)}) async-start(bf16[4,16,128,128]{3,2,0,1:T(8,128)(2,1)} %copy.81), calls=%async_computation.1 | async-start | bytes 4194304 | tf_op jit(solution)/shard_map/all_to_all | solution.py:103
  209.7 77.8 %all-gather.2 = f32[32,1,128]{2,1,0:T(1,128)S(1)} all-gather(f32[1,1,128]{2,1,0:T(1,128)S(1)} %bitcast.211), channel_id=3, replica_groups=mesh['dp'=32,'seq'=16] {'dp'}, dimensions={0}, use_global_device_ids=true | all-gather | bytes 16896 | tf_op jit(solution)/shard_map/all_gather | solution.py:105
  287.5 35.1 %all-gather.3 = f32[16,1,128]{2,1,0:T(1,128)S(1)} all-gather(f32[1,1,128]{2,1,0:T(1,128)S(1)} %bitcast.213), channel_id=1, replica_groups=mesh['dp'=32,'seq'=16] {'seq'}, dimensions={0}, use_global_device_ids=true | all-gather | bytes 8704 | tf_op jit(solution)/shard_map/all_gather | solution.py:106
  323.2 3.0 copy.82
  326.2 1.2 fusion.68
  327.4 2.0 copy.86
  329.4 2.0 copy.85
  331.5 1.0 copy.84
  (55 shorter events, 10.9 us)
Async XLA Ops:
  0.6 2.7 copy-start.8
  0.6 3.7 %copy-start.9 = (bf16[1,128,2048]{2,1,0:T(8,128)(2,1)S(1)}, bf16[1,128,2048]{2,1,0:T(8,128)(2,1)}, u32[]{:S(2)}) copy-start(bf16[1,128,2048]{2,1,0:T(8,128)(2,1)} %param.13) | copy-start | bytes 1572868
  9.5 13.6 %copy-start.10 = (s32[1,128]{1,0:T(1,128)S(1)}, s32[1,128]{1,0:T(1,128)}, u32[]{:S(2)}) copy-start(s32[1,128]{1,0:T(1,128)} %param.10) | copy-start | bytes 1540
  9.5 88.0 %copy-start.11 = (s32[16]{0:T(128)S(1)}, s32[16]{0:T(128)}, u32[]{:S(2)}) copy-start(s32[16]{0:T(128)} %param.11) | copy-start | bytes 196
  9.5 91.6 %all-to-all-start = ((bf16[4,128,16,128]{3,1,0,2:T(8,128)(2,1)}), bf16[4,128,16,128]{3,1,0,2:T(8,128)(2,1)}, u32[]{:S(2)}, u32[]{:S(2)}) async-start(bf16[4,128,16,128]{3,1,0,2:T(8,128)(2,1)} %copy.61), calls=%async_computation | async-start | bytes 4194304 | tf_op jit(solution)/shard_map/all_to_all | solution.py:83
  104.6 3.7 %copy-start.6 = (f32[16,128,128]{2,1,0:T(8,128)}, f32[16,128,128]{2,1,0:T(8,128)S(1)}, u32[]{:S(2)}) copy-start(f32[16,128,128]{2,1,0:T(8,128)S(1)} %select_multiply_fusion.1) | copy-start | bytes 3145732
  106.3 1.0 copy-start.1
  172.7 4.7 %copy-start.2 = (f32[16,128,128]{2,0,1:T(8,128)S(1)}, f32[16,128,128]{2,0,1:T(8,128)}, u32[]{:S(2)}) copy-start(f32[16,128,128]{2,0,1:T(8,128)} %copy-done.1) | copy-start | bytes 3145732
  196.8 2.1 copy-start
  196.8 2.1 copy-start.5
  199.0 2.3 copy-start.3
  199.0 2.3 copy-start.4
  202.1 1.1 copy-start.7
  204.8 118.3 %all-to-all-start.1 = ((bf16[4,16,128,128]{3,2,0,1:T(8,128)(2,1)}), bf16[4,16,128,128]{3,2,0,1:T(8,128)(2,1)}, u32[]{:S(2)}, u32[]{:S(2)}) async-start(bf16[4,16,128,128]{3,2,0,1:T(8,128)(2,1)} %copy.81), calls=%async_computation.1 | async-start | bytes 4194304 | tf_op jit(solution)/shard_map/all_to_all | solution.py:103

commit v3 on v2

--- a/solution.py
+++ b/solution.py
@@ -68,6 +68,27 @@
     return outs.reshape(tokens, heads * width)
 
 
+def butterfly_sum(part, axis):
+    count = lax.axis_size(axis)
+    if count & (count - 1):
+        return lax.psum(part, axis)
+    distance = 1
+    while distance < count:
+        part = part + lax.ppermute(part, axis, [(i, i ^ distance) for i in range(count)])
+        distance *= 2
+    return part
+
+
+def exact_pieces(values):
+    pieces = []
+    rest = values
+    for _ in range(3):
+        piece = lax.reduce_precision(rest, exponent_bits=8, mantissa_bits=7)
+        pieces.append(piece)
+        rest = rest - piece
+    return jnp.stack(pieces).astype(jnp.bfloat16)
+
+
 def per_device(query_rows, key_rows, value_rows, doc_starts, decay_rates, out_gain, cotangent):
     count = lax.axis_size("seq")
     place = lax.axis_index("seq")
@@ -78,10 +99,18 @@
     log_decay = lax.dynamic_slice_in_dim(-decay_rates.astype(jnp.float32) / tokens, place * heads, heads)
     gain = lax.dynamic_slice_in_dim(out_gain, place * width, width)
 
+    mark_rows = local_tokens // width
+    extra = -(-max(mark_rows, 1) // 8) * 8
     stacked = jnp.stack([query_rows[0], key_rows[0], value_rows[0], cotangent[0]])
     stacked = stacked.reshape(4, local_tokens, count, width)
-    moved = lax.all_to_all(stacked, "seq", 2, 1, tiled=True).reshape(4, tokens, heads, E)
-    marks = lax.all_gather(doc_starts[0], "seq", tiled=True)
+    side = jnp.zeros((4, extra, count, width), jnp.bfloat16)
+    side = side.at[0, :mark_rows].set(
+        jnp.broadcast_to(doc_starts[0].astype(jnp.bfloat16).reshape(mark_rows, 1, width), (mark_rows, count, width))
+    )
+    moved = lax.all_to_all(jnp.concatenate([stacked, side], axis=1), "seq", 2, 1, tiled=True)
+    moved = moved.reshape(4, count, local_tokens + extra, width)
+    marks = moved[0, :, local_tokens:local_tokens + mark_rows].reshape(tokens).astype(jnp.int32)
+    moved = moved[:, :, :local_tokens].reshape(4, tokens, heads, E)
 
     query_seq, key_seq, value_seq = (moved[i].astype(jnp.float32) for i in range(3))
     grad_rows = moved[3].astype(jnp.float32).reshape(tokens, width)
@@ -89,24 +118,27 @@
         lambda q, k, v: local_attention(q, k, v, marks, log_decay), query_seq, key_seq, value_seq
     )
     stats = jnp.stack([jnp.sum(attn * attn, axis=-1), jnp.sum(attn * gain * grad_rows, axis=-1)])
-    totals = lax.psum(stats, "seq")
+    totals = butterfly_sum(stats, "seq")
     scale = lax.rsqrt(totals[0] / features + epsilon)[:, None]
     normed = attn * scale * gain
     grad_attn = gain * grad_rows * scale - attn * (scale**3 * (totals[1] / features)[:, None])
     gain_part = jnp.sum(grad_rows * attn * scale, axis=0)
+    gain_total = butterfly_sum(gain_part, "dp")
     grad_q, grad_k, grad_v = back(grad_attn)
 
     outs = jnp.stack(
         [normed, grad_q.reshape(tokens, width), grad_k.reshape(tokens, width), grad_v.reshape(tokens, width)]
     ).astype(jnp.bfloat16)
     outs = outs.reshape(4, count, local_tokens, width)
-    returned = lax.all_to_all(outs, "seq", 1, 3, tiled=True).reshape(4, 1, local_tokens, features)
-
-    gain_seq = jnp.sum(lax.all_gather(gain_part, "dp"), axis=0)
-    gain_all = lax.all_gather(gain_seq, "seq", tiled=True)
+    tail = jnp.zeros((4, count, 8, width), jnp.bfloat16)
+    tail = tail.at[:3, :, 0].set(jnp.broadcast_to(exact_pieces(gain_total)[:, None], (3, count, width)))
+    returned = lax.all_to_all(jnp.concatenate([outs, tail], axis=2), "seq", 1, 3, tiled=True)
+    returned = returned.reshape(4, local_tokens + 8, features)
+    gain_all = jnp.sum(returned[:3, local_tokens].astype(jnp.float32), axis=0)
     share = features // lax.axis_size("dp")
     grad_gain = lax.dynamic_slice_in_dim(gain_all, lax.axis_index("dp") * share, share)
-    return (returned[0], returned[1], returned[2], returned[3], grad_gain)
+    results = returned[:, None, :local_tokens]
+    return (results[0], results[1], results[2], results[3], grad_gain)
 
 
 def solution(mesh):

time: 338 us -> 236 us (0.70)
  blocking collectives: 249 us -> 0 us
  waiting for transfers between devices: 0.01 us -> 103 us
  starting transfers between devices: 18 us -> 71.8 us
  local copies, waits for them, and re-layouts: 29.9 us -> 25.2 us
  matrix products: 29.7 us -> 26.1 us
    all_gather x3 -> x0, blocking collectives: 186 us -> none  [the longest x1 77.8 us: per_device(): gain_seq = jnp.sum(lax.all_gather(gain_part, 'dp'), axis=0)]
    all_to_all x2, waiting for transfers between devices: 0.01 us -> 95.2 us  [the longest x1 53.2 us: per_device(): lax.all_to_all(jnp.concatenate([outs, tail], axis=2), 'seq', 1, 3, tiled=...]
    psum x1 -> x0, blocking collectives: 63.1 us -> none  [per_device(): totals = lax.psum(stats, 'seq')]
    ppermute x0 -> x9, starting transfers between devices: none -> 54.5 us  [butterfly_sum(): lax.ppermute(part, axis, [(i, i ^ distance) for i in range(count)])]
    unnamed x32 -> x16, local copies, waits for them, and re-layouts: 11.8 us -> 3.19 us
    ppermute x0 -> x9, waiting for transfers between devices: none -> 7.44 us  [butterfly_sum(): lax.ppermute(part, axis, [(i, i ^ distance) for i in range(count)])]
    concatenate x0 -> x2, local copies, waits for them, and re-layouts: none -> 7.37 us  [the longest x1 5.81 us: per_device(): jnp.concatenate([stacked, side], axis=1)]
    another operation x4, local copies, waits for them, and re-layouts: 6.68 us -> 2.87 us
  transfers between devices with their start and end apart: 2 -> 11, of which waited for: 0 -> 9; matrix products, arithmetic and copies ran while one was open for 2% -> 5% of each run, Pallas kernels for 0% -> 0%
where the time goes in v3:
time: 236 us; the launch traced here: 234 us
  waiting for transfers between devices  103 us (44%)
  starting transfers between devices  71.8 us (30%)
  matrix products  26.1 us (11%)
  local copies, waits for them, and re-layouts  25.2 us (11%)
  other arithmetic  6.81 us (3%)
    ppermute x9, starting transfers between devices, butterfly_sum(): lax.ppermute(part, axis, [(i, i ^ distance) for i in range(count)])  54.5 us
    all_to_all x1, waiting for transfers between devices, per_device(): lax.all_to_all(jnp.concatenate([outs, tail], axis=2), 'seq', 1, 3, tiled=...  53.2 us
    all_to_all x1, waiting for transfers between devices, per_device(): lax.all_to_all(jnp.concatenate([stacked, side], axis=1), 'seq', 2, 1, til...  42 us
    all_to_all x1, starting transfers between devices, per_device(): lax.all_to_all(jnp.concatenate([stacked, side], axis=1), 'seq', 2, 1, til...  13.6 us
    dot_general x3, matrix products, out_sum(): jnp.einsum('ihe,hef->ihf', query_block, state_in, precision=highest)  7.93 us
    dot_general x3, matrix products, out_sum(): inner = jnp.einsum('hij,jhe->ihe', scores, value_block, precision=highest)  7.7 us
    ppermute x9, waiting for transfers between devices, butterfly_sum(): lax.ppermute(part, axis, [(i, i ^ distance) for i in range(count)])  7.44 us
    concatenate x1, local copies, waits for them, and re-layouts, per_device(): jnp.concatenate([stacked, side], axis=1)  5.81 us
  transfers between devices with their start and end apart: 11, of which 9 were waited for; matrix products, arithmetic and copies ran while one was open for 5% of the time, Pallas kernels for 0%

profile of v3, /device:TPU:1, one launch (start us, length us, event | category | flops | bytes accessed | tf_op | source)
XLA Modules:
  0.0 234.2 jit_solution(1335335673783393429)
XLA Ops:
  1.4 1.3 copy.40
  2.7 1.3 copy.41
  5.0 2.3 fusion.2
  7.4 5.8 %copy.44 = bf16[4,136,16,128]{3,1,0,2:T(8,128)(2,1)} copy(bf16[4,136,16,128]{1,3,2,0:T(8,128)(2,1)} %fusion.2) | data formatting | bytes 4456448 | tf_op jit(solution)/shard_map/concatenate | solution.py:110
  13.2 13.6 %all-to-all-start = ((bf16[4,136,16,128]{3,1,0,2:T(8,128)(2,1)}), bf16[4,136,16,128]{3,1,0,2:T(8,128)(2,1)}, u32[]{:S(2)}, u32[]{:S(2)}) async-start(bf16[4,136,16,128]{3,1,0,2:T(8,128)(2,1)} %copy.44), calls=%async_computation | async-start | bytes 4456448 | tf_op jit(solution)/shard_map/all_to_all | solution.py:110
  30.2 42.0 %all-to-all-done = bf16[4,136,16,128]{3,1,0,2:T(8,128)(2,1)} async-done(((bf16[4,136,16,128]{3,1,0,2:T(8,128)(2,1)}), bf16[4,136,16,128]{3,1,0,2:T(8,128)(2,1)}, u32[]{:S(2)}, u32[]{:S(2)}) %all-to-all-start) | async-done | bytes 2228256 | tf_op jit(solution)/shard_map/all_to_all | solution.py:110
  72.3 1.8 copy.79
  76.0 1.3 fusion.30
  77.8 1.6 convolution_bitcast_fusion.1
  81.8 5.2 %collective-permute-start = (f32[2,2048]{1,0:T(2,128)S(1)}, f32[2,2048]{1,0:T(2,128)S(1)}, u32[]{:S(2)}, u32[]{:S(2)}) collective-permute-start(f32[2,2048]{1,0:T(2,128)S(1)} %pad_maximum_fusion.1), channel_id=1, source_target_pairs={{0,1},{1,0},{2,3},{3,2},{4,5},{5,4},{6,7},{7,6},{8,9},{9,8},{10,11... | collective-permute-start | bytes 49160 | tf_op jit(solution)/shard_map/ppermute | solution.py:77
  88.1 8.8 %collective-permute-start.1 = (f32[2,2048]{1,0:T(2,128)S(1)}, f32[2,2048]{1,0:T(2,128)S(1)}, u32[]{:S(2)}, u32[]{:S(2)}) collective-permute-start(f32[2,2048]{1,0:T(2,128)S(1)} %fusion.77), channel_id=1, source_target_pairs={{0,2},{1,3},{2,0},{3,1},{4,6},{5,7},{6,4},{7,5},{8,10},{9,11},{10,... | collective-permute-start | bytes 49160 | tf_op jit(solution)/shard_map/ppermute | solution.py:77
  98.0 3.2 %collective-permute-start.2 = (f32[2,2048]{1,0:T(2,128)S(1)}, f32[2,2048]{1,0:T(2,128)S(1)}, u32[]{:S(2)}, u32[]{:S(2)}) collective-permute-start(f32[2,2048]{1,0:T(2,128)S(1)} %fusion.88), channel_id=1, source_target_pairs={{0,4},{1,5},{2,6},{3,7},{4,0},{5,1},{6,2},{7,3},{8,12},{9,13},{10,... | collective-permute-start | bytes 49160 | tf_op jit(solution)/shard_map/ppermute | solution.py:77
  102.5 5.2 %collective-permute-start.3 = (f32[2,2048]{1,0:T(2,128)S(1)}, f32[2,2048]{1,0:T(2,128)S(1)}, u32[]{:S(2)}, u32[]{:S(2)}) collective-permute-start(f32[2,2048]{1,0:T(2,128)S(1)} %add.101), channel_id=1, source_target_pairs={{0,8},{1,9},{2,10},{3,11},{4,12},{5,13},{6,14},{7,15},{8,0},{9,1},... | collective-permute-start | bytes 49160 | tf_op jit(solution)/shard_map/ppermute | solution.py:77
  109.0 3.5 %fusion.22 = f32[16,128,128]{1,2,0:T(8,128)} fusion(f32[16,128,128]{2,1,0:T(8,128)S(1)} %select_multiply_fusion.1, f32[16,1,128,128]{2,3,0,1:T(8,128)S(1)} %get-tuple-element.42, f32[16,128]{1,0:T(8,128)S(1)} %fusion.43, f32[16,128]{1,0:T(8,128)S(1)} %bitcast.202, f32[128]{0:T(128)S(1)} %dynamic_slice.10, bf16[4,16,136,128]{3,2,1,0:T(8,128)(2,1)S(1)} %bitcast.190), kind=kOutput, calls=%fused_computation.42 | convolution fusion | flops 403963904 | bytes 3686912 | tf_op jit(solution)/shard_map/transpose(jvp(vmap(hij,jhe->ihe)))/dot_general | solution.py:40
  112.5 3.9 %fusion.26 = f32[16,128,128]{2,1,0:T(8,128)} fusion(f32[16,128,128]{2,0,1:T(8,128)S(1)} %convolution_bitcast_fusion.1, f32[16,128]{1,0:T(8,128)S(1)} %get-tuple-element.37, f32[16,1,128,128]{2,3,0,1:T(8,128)S(1)} %get-tuple-element.42, f32[16,128]{1,0:T(8,128)S(1)} %fusion.43, f32[16,128]{1,0:T(8,128)S(1)} %bitcast.203, f32[128]{0:T(128)S(1)} %dynamic_slice.10, ...), kind=kOutput, calls=%fused_computation.46 | convolution fusion | flops 404226048 | bytes 3695104 | tf_op jit(solution)/shard_map/transpose(jvp(vmap(ihe,hef->ihf)))/dot_general | solution.py:41
  116.9 3.0 %select_multiply_fusion = f32[16,128,128]{2,1,0:T(8,128)} fusion(f32[128,128]{1,0:T(8,128)S(1)} %multiply_exponential_fusion, s32[16,128]{1,0:T(8,128)S(1)} %reduce_window_sum.18, pred[128,128]{1,0:T(8,128)(4,1)S(1)} %fusion.41, bf16[4,16,136,128]{3,2,1,0:T(8,128)(2,1)S(1)} %bitcast.193, f32[16,1,128,128]{2,3,0,1:T(8,128)S(1)} %get-tuple-element.42, ...), kind=kOutput, calls=%fused_computation.12 | convolution fusion | flops 405012480 | bytes 3260928 | tf_op jit(solution)/shard_map/transpose(jvp(vmap(hij,jhe->ihe)))/dot_general | solution.py:40
  119.8 2.9 %convolution_bitcast_fusion.3 = f32[128,128,16]{0,1,2:T(8,128)} fusion(f32[16,128]{1,0:T(8,128)S(1)} %get-tuple-element.37, bf16[4,16,136,128]{3,2,1,0:T(8,128)(2,1)S(1)} %bitcast.194, f32[16,1,128,128]{2,3,0,1:T(8,128)S(1)} %get-tuple-element.42, f32[16,128]{1,0:T(8,128)S(1)} %fusion.43, f32[16,128]{1,0:T(8,128)S(1)} %bitcast.206, f32[128]{0:T(128)S(1)} %dynamic_slice.10), kind=kOutput, calls=%fused_computation.19 | convolution fusion | flops 404226048 | bytes 3170816 | tf_op jit(solution)/shard_map/transpose(jvp(vmap(ihe,hef->ihf)))/dot_general | solution.py:41
  122.7 15.7 %collective-permute-start.4 = (f32[128]{0:T(128)S(1)}, f32[128]{0:T(128)S(1)}, u32[]{:S(2)}, u32[]{:S(2)}) collective-permute-start(f32[128]{0:T(128)S(1)} %fusion.19), channel_id=1, source_target_pairs={{0,16},{16,0},{32,48},{48,32},{64,80},{80,64},{96,112},{112,96},{1... | collective-permute-start | bytes 1544 | tf_op jit(solution)/shard_map/ppermute | solution.py:77
  138.5 2.6 %copy.54 = f32[128,128,16]{1,2,0:T(8,128)} copy(f32[128,128,16]{0,1,2:T(8,128)} %convolution_bitcast_fusion.3) | data formatting | bytes 2097152 | tf_op jit(solution)/shard_map/reshape.148
  141.1 2.3 convolution_bitcast_fusion
  143.4 1.4 fusion.8
  144.9 2.1 collective-permute-start.5
  149.3 3.3 %collective-permute-start.6 = (f32[128]{0:T(128)S(1)}, f32[128]{0:T(128)S(1)}, u32[]{:S(2)}, u32[]{:S(2)}) collective-permute-start(f32[128]{0:T(128)S(1)} %add.106), channel_id=1, source_target_pairs={{0,64},{16,80},{32,96},{48,112},{64,0},{80,16},{96,32},{112,48},{1... | collective-permute-start | bytes 1544 | tf_op jit(solution)/shard_map/ppermute | solution.py:77
  153.7 4.2 %collective-permute-start.7 = (f32[128]{0:T(128)S(1)}, f32[128]{0:T(128)S(1)}, u32[]{:S(2)}, u32[]{:S(2)}) collective-permute-start(f32[128]{0:T(128)S(1)} %add.107), channel_id=1, source_target_pairs={{0,128},{16,144},{32,160},{48,176},{64,192},{80,208},{96,224},{112... | collective-permute-start | bytes 1544 | tf_op jit(solution)/shard_map/ppermute | solution.py:77
  157.9 1.5 fusion.12
  159.5 6.8 %collective-permute-start.8 = (f32[128]{0:T(128)S(1)}, f32[128]{0:T(128)S(1)}, u32[]{:S(2)}, u32[]{:S(2)}) collective-permute-start(f32[128]{0:T(128)S(1)} %add.108), channel_id=1, source_target_pairs={{0,256},{16,272},{32,288},{48,304},{64,320},{80,336},{96,352},{112... | collective-permute-start | bytes 1544 | tf_op jit(solution)/shard_map/ppermute | solution.py:77
  168.0 1.6 copy.59
  169.5 3.7 %all-to-all-start.1 = ((bf16[4,16,136,128]{3,2,0,1:T(8,128)(2,1)}), bf16[4,16,136,128]{3,2,0,1:T(8,128)(2,1)S(1)}, u32[]{:S(2)}, u32[]{:S(2)}) async-start(bf16[4,16,136,128]{3,2,0,1:T(8,128)(2,1)} %copy.59), calls=%async_computation.1 | async-start | bytes 4456448 | tf_op jit(solution)/shard_map/all_to_all | solution.py:135
  173.3 53.2 %all-to-all-done.1 = bf16[4,16,136,128]{3,2,0,1:T(8,128)(2,1)S(1)} async-done(((bf16[4,16,136,128]{3,2,0,1:T(8,128)(2,1)}), bf16[4,16,136,128]{3,2,0,1:T(8,128)(2,1)S(1)}, u32[]{:S(2)}, u32[]{:S(2)}) %all-to-all-start.1) | async-done | bytes 2228256 | tf_op jit(solution)/shard_map/all_to_all | solution.py:135
  226.4 2.2 copy.60
  228.7 3.5 %reshape.664 = bf16[4,136,2048]{2,1,0:T(8,128)(2,1)S(1)} reshape(bf16[4,1,136,16,128]{4,3,2,0,1:T(8,128)(2,1)} %copy.60) | data formatting | bytes 4456448 | tf_op jit(solution)/shard_map/reshape | solution.py:136
  232.3 1.3 fusion.82
  (68 shorter events, 20.0 us)
Async XLA Ops:
  0.6 3.4 %copy-start.3 = (bf16[1,128,2048]{2,1,0:T(8,128)(2,1)S(1)}, bf16[1,128,2048]{2,1,0:T(8,128)(2,1)}, u32[]{:S(2)}) copy-start(bf16[1,128,2048]{2,1,0:T(8,128)(2,1)} %param.13) | copy-start | bytes 1572868
  0.6 3.7 %copy-start.4 = (bf16[1,128,2048]{2,1,0:T(8,128)(2,1)S(1)}, bf16[1,128,2048]{2,1,0:T(8,128)(2,1)}, u32[]{:S(2)}) copy-start(bf16[1,128,2048]{2,1,0:T(8,128)(2,1)} %param.17) | copy-start | bytes 1572868
  13.2 14.4 %copy-start.5 = (s32[16]{0:T(128)S(1)}, s32[16]{0:T(128)}, u32[]{:S(2)}) copy-start(s32[16]{0:T(128)} %param.15) | copy-start | bytes 196
  13.2 59.1 %all-to-all-start = ((bf16[4,136,16,128]{3,1,0,2:T(8,128)(2,1)}), bf16[4,136,16,128]{3,1,0,2:T(8,128)(2,1)}, u32[]{:S(2)}, u32[]{:S(2)}) async-start(bf16[4,136,16,128]{3,1,0,2:T(8,128)(2,1)} %copy.44), calls=%async_computation | async-start | bytes 4456448 | tf_op jit(solution)/shard_map/all_to_all | solution.py:110
  81.8 6.3 %collective-permute-start = (f32[2,2048]{1,0:T(2,128)S(1)}, f32[2,2048]{1,0:T(2,128)S(1)}, u32[]{:S(2)}, u32[]{:S(2)}) collective-permute-start(f32[2,2048]{1,0:T(2,128)S(1)} %pad_maximum_fusion.1), channel_id=1, source_target_pairs={{0,1},{1,0},{2,3},{3,2},{4,5},{5,4},{6,7},{7,6},{8,9},{9,8},{10,11... | collective-permute-start | bytes 49160 | tf_op jit(solution)/shard_map/ppermute | solution.py:77
  88.1 9.9 %collective-permute-start.1 = (f32[2,2048]{1,0:T(2,128)S(1)}, f32[2,2048]{1,0:T(2,128)S(1)}, u32[]{:S(2)}, u32[]{:S(2)}) collective-permute-start(f32[2,2048]{1,0:T(2,128)S(1)} %fusion.77), channel_id=1, source_target_pairs={{0,2},{1,3},{2,0},{3,1},{4,6},{5,7},{6,4},{7,5},{8,10},{9,11},{10,... | collective-permute-start | bytes 49160 | tf_op jit(solution)/shard_map/ppermute | solution.py:77
  98.0 4.5 %collective-permute-start.2 = (f32[2,2048]{1,0:T(2,128)S(1)}, f32[2,2048]{1,0:T(2,128)S(1)}, u32[]{:S(2)}, u32[]{:S(2)}) collective-permute-start(f32[2,2048]{1,0:T(2,128)S(1)} %fusion.88), channel_id=1, source_target_pairs={{0,4},{1,5},{2,6},{3,7},{4,0},{5,1},{6,2},{7,3},{8,12},{9,13},{10,... | collective-permute-start | bytes 49160 | tf_op jit(solution)/shard_map/ppermute | solution.py:77
  102.5 6.4 %collective-permute-start.3 = (f32[2,2048]{1,0:T(2,128)S(1)}, f32[2,2048]{1,0:T(2,128)S(1)}, u32[]{:S(2)}, u32[]{:S(2)}) collective-permute-start(f32[2,2048]{1,0:T(2,128)S(1)} %add.101), channel_id=1, source_target_pairs={{0,8},{1,9},{2,10},{3,11},{4,12},{5,13},{6,14},{7,15},{8,0},{9,1},... | collective-permute-start | bytes 49160 | tf_op jit(solution)/shard_map/ppermute | solution.py:77
  122.7 22.1 %collective-permute-start.4 = (f32[128]{0:T(128)S(1)}, f32[128]{0:T(128)S(1)}, u32[]{:S(2)}, u32[]{:S(2)}) collective-permute-start(f32[128]{0:T(128)S(1)} %fusion.19), channel_id=1, source_target_pairs={{0,16},{16,0},{32,48},{48,32},{64,80},{80,64},{96,112},{112,96},{1... | collective-permute-start | bytes 1544 | tf_op jit(solution)/shard_map/ppermute | solution.py:77
  141.1 5.9 %copy-start = (f32[16,128,128]{2,1,0:T(8,128)S(1)}, f32[16,128,128]{2,1,0:T(8,128)}, u32[]{:S(2)}) copy-start(f32[16,128,128]{2,1,0:T(8,128)} %select_multiply_fusion) | copy-start | bytes 3145732
  144.9 13.1 %copy-start.2 = (f32[16,128,128]{1,2,0:T(8,128)S(1)}, f32[16,128,128]{1,2,0:T(8,128)}, u32[]{:S(2)}) copy-start(f32[16,128,128]{1,2,0:T(8,128)} %fusion.22) | copy-start | bytes 3145732
  144.9 4.4 %collective-permute-start.5 = (f32[128]{0:T(128)S(1)}, f32[128]{0:T(128)S(1)}, u32[]{:S(2)}, u32[]{:S(2)}) collective-permute-start(f32[128]{0:T(128)S(1)} %add.105), channel_id=1, source_target_pairs={{0,32},{16,48},{32,0},{48,16},{64,96},{80,112},{96,64},{112,80},{1... | collective-permute-start | bytes 1544 | tf_op jit(solution)/shard_map/ppermute | solution.py:77
  149.3 17.0 %copy-start.1 = (f32[16,128,128]{2,1,0:T(8,128)S(1)}, f32[16,128,128]{2,1,0:T(8,128)}, u32[]{:S(2)}) copy-start(f32[16,128,128]{2,1,0:T(8,128)} %fusion.26) | copy-start | bytes 3145732
  149.3 4.4 %collective-permute-start.6 = (f32[128]{0:T(128)S(1)}, f32[128]{0:T(128)S(1)}, u32[]{:S(2)}, u32[]{:S(2)}) collective-permute-start(f32[128]{0:T(128)S(1)} %add.106), channel_id=1, source_target_pairs={{0,64},{16,80},{32,96},{48,112},{64,0},{80,16},{96,32},{112,48},{1... | collective-permute-start | bytes 1544 | tf_op jit(solution)/shard_map/ppermute | solution.py:77
  153.7 5.8 %collective-permute-start.7 = (f32[128]{0:T(128)S(1)}, f32[128]{0:T(128)S(1)}, u32[]{:S(2)}, u32[]{:S(2)}) collective-permute-start(f32[128]{0:T(128)S(1)} %add.107), channel_id=1, source_target_pairs={{0,128},{16,144},{32,160},{48,176},{64,192},{80,208},{96,224},{112... | collective-permute-start | bytes 1544 | tf_op jit(solution)/shard_map/ppermute | solution.py:77
  159.5 8.2 %collective-permute-start.8 = (f32[128]{0:T(128)S(1)}, f32[128]{0:T(128)S(1)}, u32[]{:S(2)}, u32[]{:S(2)}) collective-permute-start(f32[128]{0:T(128)S(1)} %add.108), channel_id=1, source_target_pairs={{0,256},{16,272},{32,288},{48,304},{64,320},{80,336},{96,352},{112... | collective-permute-start | bytes 1544 | tf_op jit(solution)/shard_map/ppermute | solution.py:77
  169.5 56.9 %all-to-all-start.1 = ((bf16[4,16,136,128]{3,2,0,1:T(8,128)(2,1)}), bf16[4,16,136,128]{3,2,0,1:T(8,128)(2,1)S(1)}, u32[]{:S(2)}, u32[]{:S(2)}) async-start(bf16[4,16,136,128]{3,2,0,1:T(8,128)(2,1)} %copy.59), calls=%async_computation.1 | async-start | bytes 4456448 | tf_op jit(solution)/shard_map/all_to_all | solution.py:135

commit v4 on v3

--- a/solution.py
+++ b/solution.py
@@ -101,16 +101,17 @@
 
     mark_rows = local_tokens // width
     extra = -(-max(mark_rows, 1) // 8) * 8
-    stacked = jnp.stack([query_rows[0], key_rows[0], value_rows[0], cotangent[0]])
-    stacked = stacked.reshape(4, local_tokens, count, width)
-    side = jnp.zeros((4, extra, count, width), jnp.bfloat16)
-    side = side.at[0, :mark_rows].set(
-        jnp.broadcast_to(doc_starts[0].astype(jnp.bfloat16).reshape(mark_rows, 1, width), (mark_rows, count, width))
+    side = jnp.zeros((count, extra, width), jnp.bfloat16)
+    side = side.at[:, :mark_rows].set(
+        jnp.broadcast_to(doc_starts[0].astype(jnp.bfloat16).reshape(1, mark_rows, width), (count, mark_rows, width))
     )
-    moved = lax.all_to_all(jnp.concatenate([stacked, side], axis=1), "seq", 2, 1, tiled=True)
-    moved = moved.reshape(4, count, local_tokens + extra, width)
-    marks = moved[0, :, local_tokens:local_tokens + mark_rows].reshape(tokens).astype(jnp.int32)
-    moved = moved[:, :, :local_tokens].reshape(4, tokens, heads, E)
+    pieces = [rows[0].reshape(local_tokens, count, width).transpose(1, 0, 2)
+              for rows in (query_rows, key_rows, value_rows, cotangent)]
+    moved = lax.all_to_all(jnp.concatenate(pieces + [side], axis=1), "seq", 0, 0, tiled=True)
+    span = 4 * local_tokens
+    marks = moved[:, span:span + mark_rows].reshape(tokens).astype(jnp.int32)
+    moved = moved[:, :span].reshape(count, 4, local_tokens, heads, E).transpose(1, 0, 2, 3, 4)
+    moved = moved.reshape(4, tokens, heads, E)
 
     query_seq, key_seq, value_seq = (moved[i].astype(jnp.float32) for i in range(3))
     grad_rows = moved[3].astype(jnp.float32).reshape(tokens, width)
@@ -126,18 +127,17 @@
     gain_total = butterfly_sum(gain_part, "dp")
     grad_q, grad_k, grad_v = back(grad_attn)
 
-    outs = jnp.stack(
-        [normed, grad_q.reshape(tokens, width), grad_k.reshape(tokens, width), grad_v.reshape(tokens, width)]
-    ).astype(jnp.bfloat16)
-    outs = outs.reshape(4, count, local_tokens, width)
-    tail = jnp.zeros((4, count, 8, width), jnp.bfloat16)
-    tail = tail.at[:3, :, 0].set(jnp.broadcast_to(exact_pieces(gain_total)[:, None], (3, count, width)))
-    returned = lax.all_to_all(jnp.concatenate([outs, tail], axis=2), "seq", 1, 3, tiled=True)
-    returned = returned.reshape(4, local_tokens + 8, features)
-    gain_all = jnp.sum(returned[:3, local_tokens].astype(jnp.float32), axis=0)
+    outs = [part.reshape(count, local_tokens, width).astype(jnp.bfloat16)
+            for part in (normed, grad_q, grad_k, grad_v)]
+    tail = jnp.zeros((count, 8, width), jnp.bfloat16)
+    tail = tail.at[:, :3].set(jnp.broadcast_to(exact_pieces(gain_total)[None], (count, 3, width)))
+    returned = lax.all_to_all(jnp.concatenate(outs + [tail], axis=1), "seq", 0, 0, tiled=True)
+    span = 4 * local_tokens
+    gain_all = jnp.sum(returned[:, span:span + 3].astype(jnp.float32), axis=1).reshape(features)
+    results = returned[:, :span].reshape(count, 4, local_tokens, width).transpose(1, 2, 0, 3)
+    results = results.reshape(4, 1, local_tokens, features)
     share = features // lax.axis_size("dp")
     grad_gain = lax.dynamic_slice_in_dim(gain_all, lax.axis_index("dp") * share, share)
-    results = returned[:, None, :local_tokens]
     return (results[0], results[1], results[2], results[3], grad_gain)
 
 

time: 236 us -> 223 us (0.945)
  waiting for transfers between devices: 103 us -> 96.1 us
  local copies, waits for them, and re-layouts: 25.2 us -> 21.5 us
    unnamed x16 -> x19, local copies, waits for them, and re-layouts: 3.19 us -> 8.24 us
    all_to_all x2, waiting for transfers between devices: 95.2 us -> 90.4 us  [the longest x1 51 us: per_device(): lax.all_to_all(jnp.concatenate(outs + [tail], axis=1), 'seq', 0, 0, tiled...]
    all_to_all x2 -> x0, local copies, waits for them, and re-layouts: 4.08 us -> none  [the longest x1 2.25 us: per_device(): lax.all_to_all(jnp.concatenate([outs, tail], axis=2), 'seq', 1, 3, tiled=...]
    concatenate x2 -> x3, local copies, waits for them, and re-layouts: 7.37 us -> 3.38 us  [the longest x2 2.75 us: per_device(): jnp.concatenate(pieces + [side], axis=1)]
    squeeze x0 -> x4, local copies, waits for them, and re-layouts: none -> 3.72 us  [per_device(): return (results[0], results[1], results[2], results[3], grad_gain)]
    reshape x1, local copies, waits for them, and re-layouts: 3.54 us -> 0.14 us  [per_device(): moved[:, :span].reshape(count, 4, local_tokens, heads, E)]
    concatenate x2 -> x0, other arithmetic: 2.58 us -> none  [the longest x1 2.34 us: per_device(): jnp.concatenate([stacked, side], axis=1)]
  transfers between devices with their start and end apart: 11 -> 11, of which waited for: 9 -> 6; matrix products, arithmetic and copies ran while one was open for 5% -> 7% of each run, Pallas kernels for 0% -> 0%
where the time goes in v4:
time: 223 us; the launch traced here: 221 us
  waiting for transfers between devices  96.1 us (43%)
  starting transfers between devices  71.6 us (32%)
  matrix products  25.9 us (12%)
  local copies, waits for them, and re-layouts  21.5 us (10%)
  other arithmetic  4.5 us (2%)
    ppermute x9, starting transfers between devices, butterfly_sum(): lax.ppermute(part, axis, [(i, i ^ distance) for i in range(count)])  53.5 us
    all_to_all x1, waiting for transfers between devices, per_device(): lax.all_to_all(jnp.concatenate(outs + [tail], axis=1), 'seq', 0, 0, tiled...  51 us
    all_to_all x1, waiting for transfers between devices, per_device(): lax.all_to_all(jnp.concatenate(pieces + [side], axis=1), 'seq', 0, 0, til...  39.4 us
    all_to_all x1, starting transfers between devices, per_device(): lax.all_to_all(jnp.concatenate(pieces + [side], axis=1), 'seq', 0, 0, til...  13.6 us
    unnamed x19, local copies, waits for them, and re-layouts  8.24 us
    dot_general x3, matrix products, out_sum(): jnp.einsum('ihe,hef->ihf', query_block, state_in, precision=highest)  6.83 us
    dot_general x3, matrix products, out_sum(): inner = jnp.einsum('hij,jhe->ihe', scores, value_block, precision=highest)  6.22 us
    ppermute x9, waiting for transfers between devices, butterfly_sum(): lax.ppermute(part, axis, [(i, i ^ distance) for i in range(count)])  5.73 us
  transfers between devices with their start and end apart: 11, of which 6 were waited for; matrix products, arithmetic and copies ran while one was open for 7% of the time, Pallas kernels for 0%

profile of v4, /device:TPU:1, one launch (start us, length us, event | category | flops | bytes accessed | tf_op | source)
XLA Modules:
  0.0 221.3 jit_solution(3622590201087756438)
XLA Ops:
  1.4 2.0 copy.89
  3.4 2.0 copy.90
  6.8 1.2 constant_dynamic-update-slice_fusion.3
  8.0 1.2 constant_dynamic-update-slice_fusion.2
  9.8 2.5 %copy.93 = bf16[16,520,128]{2,1,0:T(8,128)(2,1)} copy(bf16[16,520,128]{1,2,0:T(8,128)(2,1)S(1)} %pad_dynamic-update-slice_fusion) | data formatting | bytes 4259840 | tf_op jit(solution)/shard_map/concatenate | solution.py:110
  12.4 13.6 %all-to-all-start = ((bf16[16,520,128]{2,1,0:T(8,128)(2,1)}), bf16[16,520,128]{2,1,0:T(8,128)(2,1)S(1)}, u32[]{:S(2)}, u32[]{:S(2)}) async-start(bf16[16,520,128]{2,1,0:T(8,128)(2,1)} %copy.93), calls=%async_computation | async-start | bytes 4259840 | tf_op jit(solution)/shard_map/all_to_all | solution.py:110
  29.4 39.4 %all-to-all-done = bf16[16,520,128]{2,1,0:T(8,128)(2,1)S(1)} async-done(((bf16[16,520,128]{2,1,0:T(8,128)(2,1)}), bf16[16,520,128]{2,1,0:T(8,128)(2,1)S(1)}, u32[]{:S(2)}, u32[]{:S(2)}) %all-to-all-start) | async-done | bytes 2129952 | tf_op jit(solution)/shard_map/all_to_all | solution.py:110
  70.7 1.3 fusion.28
  72.6 1.6 convolution_bitcast_fusion.1
  75.3 1.2 fusion.26
  76.5 5.5 %collective-permute-start = (f32[2,2048]{1,0:T(2,128)S(1)}, f32[2,2048]{1,0:T(2,128)S(1)}, u32[]{:S(2)}, u32[]{:S(2)}) collective-permute-start(f32[2,2048]{1,0:T(2,128)S(1)} %pad_maximum_fusion), channel_id=1, source_target_pairs={{0,1},{1,0},{2,3},{3,2},{4,5},{5,4},{6,7},{7,6},{8,9},{9,8},{10,11... | collective-permute-start | bytes 49160 | tf_op jit(solution)/shard_map/ppermute | solution.py:77
  83.2 8.8 %collective-permute-start.1 = (f32[2,2048]{1,0:T(2,128)S(1)}, f32[2,2048]{1,0:T(2,128)S(1)}, u32[]{:S(2)}, u32[]{:S(2)}) collective-permute-start(f32[2,2048]{1,0:T(2,128)S(1)} %fusion.74), channel_id=1, source_target_pairs={{0,2},{1,3},{2,0},{3,1},{4,6},{5,7},{6,4},{7,5},{8,10},{9,11},{10,... | collective-permute-start | bytes 49160 | tf_op jit(solution)/shard_map/ppermute | solution.py:77
  93.1 1.9 collective-permute-start.2
  95.0 2.6 %collective-permute-done.2 = f32[2,2048]{1,0:T(2,128)S(1)} collective-permute-done((f32[2,2048]{1,0:T(2,128)S(1)}, f32[2,2048]{1,0:T(2,128)S(1)}, u32[]{:S(2)}, u32[]{:S(2)}) %collective-permute-start.2) | collective-permute-done | bytes 16416 | tf_op jit(solution)/shard_map/ppermute | solution.py:77
  97.6 5.0 %collective-permute-start.3 = (f32[2,2048]{1,0:T(2,128)S(1)}, f32[2,2048]{1,0:T(2,128)S(1)}, u32[]{:S(2)}, u32[]{:S(2)}) collective-permute-start(f32[2,2048]{1,0:T(2,128)S(1)} %add.99), channel_id=1, source_target_pairs={{0,8},{1,9},{2,10},{3,11},{4,12},{5,13},{6,14},{7,15},{8,0},{9,1},... | collective-permute-start | bytes 49160 | tf_op jit(solution)/shard_map/ppermute | solution.py:77
  103.6 3.5 %fusion.20 = f32[16,128,128]{1,2,0:T(8,128)} fusion(f32[16,128,128]{2,1,0:T(8,128)S(1)} %select_multiply_fusion.1, f32[16,1,128,128]{2,3,0,1:T(8,128)S(1)} %get-tuple-element.42, f32[16,128]{1,0:T(8,128)S(1)} %fusion.41, f32[16,128]{1,0:T(8,128)S(1)} %bitcast.240, f32[128]{0:T(128)S(1)} %dynamic_slice.10, bf16[4,16,128,1,128]{4,2,1,3,0:T(8,128)(2,1)S(1)} %bitcast.220), kind=kOutput, calls=%fused_computation.37 | convolution fusion | flops 403963904 | bytes 3686912 | tf_op jit(solution)/shard_map/transpose(jvp(vmap(hij,jhe->ihe)))/dot_general | solution.py:40
  107.1 2.8 %fusion.24 = f32[16,128,128]{2,1,0:T(8,128)S(1)} fusion(f32[16,128,128]{2,0,1:T(8,128)S(1)} %convolution_bitcast_fusion.1, f32[16,128]{1,0:T(8,128)S(1)} %get-tuple-element.37, f32[16,1,128,128]{2,3,0,1:T(8,128)S(1)} %get-tuple-element.42, f32[16,128]{1,0:T(8,128)S(1)} %fusion.41, f32[16,128]{1,0:T(8,128)S(1)} %bitcast.241, f32[128]{0:T(128)S(1)} %dynamic_slice.10, ...), kind=kOutput, calls=%fused_computation.41 | convolution fusion | flops 404226048 | bytes 3695104 | tf_op jit(solution)/shard_map/transpose(jvp(vmap(ihe,hef->ihf)))/dot_general | solution.py:41
  110.3 1.5 select_multiply_fusion
  111.8 2.9 %convolution_bitcast_fusion.3 = f32[128,128,16]{0,1,2:T(8,128)} fusion(f32[16,128]{1,0:T(8,128)S(1)} %get-tuple-element.37, bf16[4,16,128,1,128]{4,2,1,3,0:T(8,128)(2,1)S(1)} %bitcast.224, f32[16,1,128,128]{2,3,0,1:T(8,128)S(1)} %get-tuple-element.42, f32[16,128]{1,0:T(8,128)S(1)} %fusion.41, f32[16,128]{1,0:T(8,128)S(1)} %bitcast.244, ...), kind=kOutput, calls=%fused_computation.12 | convolution fusion | flops 404226048 | bytes 3170816 | tf_op jit(solution)/shard_map/transpose(jvp(vmap(ihe,hef->ihf)))/dot_general | solution.py:41
  116.0 16.4 %collective-permute-start.4 = (f32[128]{0:T(128)S(1)}, f32[128]{0:T(128)S(1)}, u32[]{:S(2)}, u32[]{:S(2)}) collective-permute-start(f32[128]{0:T(128)S(1)} %fusion.17), channel_id=1, source_target_pairs={{0,16},{16,0},{32,48},{48,32},{64,80},{80,64},{96,112},{112,96},{1... | collective-permute-start | bytes 1544 | tf_op jit(solution)/shard_map/ppermute | solution.py:77
  132.4 1.5 fusion.8
  133.9 2.6 %copy.104 = f32[128,128,16]{1,2,0:T(8,128)} copy(f32[128,128,16]{0,1,2:T(8,128)} %convolution_bitcast_fusion.3) | data formatting | bytes 2097152 | tf_op jit(solution)/shard_map/reshape.138
  136.5 2.1 collective-permute-start.5
  138.6 2.3 %convolution_bitcast_fusion = f32[16,128,128]{2,0,1:T(8,128)S(1)} fusion(f32[128,128,16]{1,2,0:T(8,128)} %copy.104, f32[]{:T(128)S(6)} %mul.235, s32[16]{0:T(128)S(1)} %reduce.9, s32[16]{0:T(128)S(1)} %compare_select_fusion.2), kind=kOutput, calls=%fused_computation.8 | convolution fusion | flops 50334464 | bytes 2097284 | tf_op jit(solution)/shard_map/transpose(jvp(hcd,dhef->chef))/dot_general | solution.py:66
  140.9 3.2 %collective-permute-start.6 = (f32[128]{0:T(128)S(1)}, f32[128]{0:T(128)S(1)}, u32[]{:S(2)}, u32[]{:S(2)}) collective-permute-start(f32[128]{0:T(128)S(1)} %add.104), channel_id=1, source_target_pairs={{0,64},{16,80},{32,96},{48,112},{64,0},{80,16},{96,32},{112,48},{1... | collective-permute-start | bytes 1544 | tf_op jit(solution)/shard_map/ppermute | solution.py:77
  144.1 1.4 fusion.4
  145.6 4.4 %collective-permute-start.7 = (f32[128]{0:T(128)S(1)}, f32[128]{0:T(128)S(1)}, u32[]{:S(2)}, u32[]{:S(2)}) collective-permute-start(f32[128]{0:T(128)S(1)} %add.105), channel_id=1, source_target_pairs={{0,128},{16,144},{32,160},{48,176},{64,192},{80,208},{96,224},{112... | collective-permute-start | bytes 1544 | tf_op jit(solution)/shard_map/ppermute | solution.py:77
  149.9 1.9 fusion.12
  151.8 6.2 %collective-permute-start.8 = (f32[128]{0:T(128)S(1)}, f32[128]{0:T(128)S(1)}, u32[]{:S(2)}, u32[]{:S(2)}) collective-permute-start(f32[128]{0:T(128)S(1)} %add.106), channel_id=1, source_target_pairs={{0,256},{16,272},{32,288},{48,304},{64,320},{80,336},{96,352},{112... | collective-permute-start | bytes 1544 | tf_op jit(solution)/shard_map/ppermute | solution.py:77
  158.0 2.3 %fusion.10 = bf16[16,520,128]{2,1,0:T(8,128)(2,1)} fusion(bf16[16,520,128]{2,1,0:T(8,128)(2,1)} %fusion.12, f32[16,128,128]{1,2,0:T(8,128)S(1)} %copy-done, f32[16,128,128]{2,0,1:T(8,128)S(1)} %convolution_bitcast_fusion, f32[16,128]{1,0:T(8,128)S(1)} %get-tuple-element.38, bf16[4,16,128,1,128]{4,2,1,3,0:T(8,128)(2,1)S(1)} %bitcast.228), kind=kOutput, calls=%fused_computation.26 | convolution fusion | flops 403701760 | bytes 3153920 | tf_op jit(solution)/shard_map/transpose(jvp(vmap(jhe,jhf->hef)))/dot_general | solution.py:35
  161.1 4.5 %all-to-all-start.1 = ((bf16[16,520,128]{2,1,0:T(8,128)(2,1)}), bf16[16,520,128]{2,1,0:T(8,128)(2,1)S(1)}, u32[]{:S(2)}, u32[]{:S(2)}) async-start(bf16[16,520,128]{2,1,0:T(8,128)(2,1)} %pad_dynamic-update-slice_fusion.1), calls=%async_computation.1 | async-start | bytes 4259840 | tf_op jit(solution)/shard_map/all_to_all | solution.py:134
  165.6 51.0 %all-to-all-done.1 = bf16[16,520,128]{2,1,0:T(8,128)(2,1)S(1)} async-done(((bf16[16,520,128]{2,1,0:T(8,128)(2,1)}), bf16[16,520,128]{2,1,0:T(8,128)(2,1)S(1)}, u32[]{:S(2)}, u32[]{:S(2)}) %all-to-all-start.1) | async-done | bytes 2129952 | tf_op jit(solution)/shard_map/all_to_all | solution.py:134
  (73 shorter events, 19.2 us)
Async XLA Ops:
  0.6 4.8 %copy-start.2 = (bf16[1,128,2048]{2,1,0:T(8,128)(2,1)S(1)}, bf16[1,128,2048]{2,1,0:T(8,128)(2,1)}, u32[]{:S(2)}) copy-start(bf16[1,128,2048]{2,1,0:T(8,128)(2,1)} %param.13) | copy-start | bytes 1572868
  0.6 5.8 %copy-start.3 = (bf16[1,128,2048]{2,1,0:T(8,128)(2,1)S(1)}, bf16[1,128,2048]{2,1,0:T(8,128)(2,1)}, u32[]{:S(2)}) copy-start(bf16[1,128,2048]{2,1,0:T(8,128)(2,1)} %param.17) | copy-start | bytes 1572868
  6.8 2.4 %copy-start.1 = (bf16[1,128,2048]{1,2,0:T(8,128)(2,1)S(1)}, bf16[1,128,2048]{1,2,0:T(8,128)(2,1)}, u32[]{:S(2)}) copy-start(bf16[1,128,2048]{1,2,0:T(8,128)(2,1)} %copy.91) | copy-start | bytes 1572868
  12.4 14.3 %copy-start.4 = (s32[16]{0:T(128)S(1)}, s32[16]{0:T(128)}, u32[]{:S(2)}) copy-start(s32[16]{0:T(128)} %param.15) | copy-start | bytes 196
  12.4 56.4 %all-to-all-start = ((bf16[16,520,128]{2,1,0:T(8,128)(2,1)}), bf16[16,520,128]{2,1,0:T(8,128)(2,1)S(1)}, u32[]{:S(2)}, u32[]{:S(2)}) async-start(bf16[16,520,128]{2,1,0:T(8,128)(2,1)} %copy.93), calls=%async_computation | async-start | bytes 4259840 | tf_op jit(solution)/shard_map/all_to_all | solution.py:110
  76.5 6.6 %collective-permute-start = (f32[2,2048]{1,0:T(2,128)S(1)}, f32[2,2048]{1,0:T(2,128)S(1)}, u32[]{:S(2)}, u32[]{:S(2)}) collective-permute-start(f32[2,2048]{1,0:T(2,128)S(1)} %pad_maximum_fusion), channel_id=1, source_target_pairs={{0,1},{1,0},{2,3},{3,2},{4,5},{5,4},{6,7},{7,6},{8,9},{9,8},{10,11... | collective-permute-start | bytes 49160 | tf_op jit(solution)/shard_map/ppermute | solution.py:77
  83.2 9.9 %collective-permute-start.1 = (f32[2,2048]{1,0:T(2,128)S(1)}, f32[2,2048]{1,0:T(2,128)S(1)}, u32[]{:S(2)}, u32[]{:S(2)}) collective-permute-start(f32[2,2048]{1,0:T(2,128)S(1)} %fusion.74), channel_id=1, source_target_pairs={{0,2},{1,3},{2,0},{3,1},{4,6},{5,7},{6,4},{7,5},{8,10},{9,11},{10,... | collective-permute-start | bytes 49160 | tf_op jit(solution)/shard_map/ppermute | solution.py:77
  93.1 4.5 %collective-permute-start.2 = (f32[2,2048]{1,0:T(2,128)S(1)}, f32[2,2048]{1,0:T(2,128)S(1)}, u32[]{:S(2)}, u32[]{:S(2)}) collective-permute-start(f32[2,2048]{1,0:T(2,128)S(1)} %fusion.84), channel_id=1, source_target_pairs={{0,4},{1,5},{2,6},{3,7},{4,0},{5,1},{6,2},{7,3},{8,12},{9,13},{10,... | collective-permute-start | bytes 49160 | tf_op jit(solution)/shard_map/ppermute | solution.py:77
  97.6 6.0 %collective-permute-start.3 = (f32[2,2048]{1,0:T(2,128)S(1)}, f32[2,2048]{1,0:T(2,128)S(1)}, u32[]{:S(2)}, u32[]{:S(2)}) collective-permute-start(f32[2,2048]{1,0:T(2,128)S(1)} %add.99), channel_id=1, source_target_pairs={{0,8},{1,9},{2,10},{3,11},{4,12},{5,13},{6,14},{7,15},{8,0},{9,1},... | collective-permute-start | bytes 49160 | tf_op jit(solution)/shard_map/ppermute | solution.py:77
  116.0 20.5 %collective-permute-start.4 = (f32[128]{0:T(128)S(1)}, f32[128]{0:T(128)S(1)}, u32[]{:S(2)}, u32[]{:S(2)}) collective-permute-start(f32[128]{0:T(128)S(1)} %fusion.17), channel_id=1, source_target_pairs={{0,16},{16,0},{32,48},{48,32},{64,80},{80,64},{96,112},{112,96},{1... | collective-permute-start | bytes 1544 | tf_op jit(solution)/shard_map/ppermute | solution.py:77
  136.5 4.4 %collective-permute-start.5 = (f32[128]{0:T(128)S(1)}, f32[128]{0:T(128)S(1)}, u32[]{:S(2)}, u32[]{:S(2)}) collective-permute-start(f32[128]{0:T(128)S(1)} %add.103), channel_id=1, source_target_pairs={{0,32},{16,48},{32,0},{48,16},{64,96},{80,112},{96,64},{112,80},{1... | collective-permute-start | bytes 1544 | tf_op jit(solution)/shard_map/ppermute | solution.py:77
  140.9 4.7 %collective-permute-start.6 = (f32[128]{0:T(128)S(1)}, f32[128]{0:T(128)S(1)}, u32[]{:S(2)}, u32[]{:S(2)}) collective-permute-start(f32[128]{0:T(128)S(1)} %add.104), channel_id=1, source_target_pairs={{0,64},{16,80},{32,96},{48,112},{64,0},{80,16},{96,32},{112,48},{1... | collective-permute-start | bytes 1544 | tf_op jit(solution)/shard_map/ppermute | solution.py:77
  145.5 12.5 %copy-start = (f32[16,128,128]{1,2,0:T(8,128)S(1)}, f32[16,128,128]{1,2,0:T(8,128)}, u32[]{:S(2)}) copy-start(f32[16,128,128]{1,2,0:T(8,128)} %fusion.20) | copy-start | bytes 3145732
  145.6 6.2 %collective-permute-start.7 = (f32[128]{0:T(128)S(1)}, f32[128]{0:T(128)S(1)}, u32[]{:S(2)}, u32[]{:S(2)}) collective-permute-start(f32[128]{0:T(128)S(1)} %add.105), channel_id=1, source_target_pairs={{0,128},{16,144},{32,160},{48,176},{64,192},{80,208},{96,224},{112... | collective-permute-start | bytes 1544 | tf_op jit(solution)/shard_map/ppermute | solution.py:77
  151.8 8.6 %collective-permute-start.8 = (f32[128]{0:T(128)S(1)}, f32[128]{0:T(128)S(1)}, u32[]{:S(2)}, u32[]{:S(2)}) collective-permute-start(f32[128]{0:T(128)S(1)} %add.106), channel_id=1, source_target_pairs={{0,256},{16,272},{32,288},{48,304},{64,320},{80,336},{96,352},{112... | collective-permute-start | bytes 1544 | tf_op jit(solution)/shard_map/ppermute | solution.py:77
  161.1 55.5 %all-to-all-start.1 = ((bf16[16,520,128]{2,1,0:T(8,128)(2,1)}), bf16[16,520,128]{2,1,0:T(8,128)(2,1)S(1)}, u32[]{:S(2)}, u32[]{:S(2)}) async-start(bf16[16,520,128]{2,1,0:T(8,128)(2,1)} %pad_dynamic-update-slice_fusion.1), calls=%async_computation.1 | async-start | bytes 4259840 | tf_op jit(solution)/shard_map/all_to_all | solution.py:134

commit v5 on v4

--- a/solution.py
+++ b/solution.py
@@ -79,6 +79,15 @@
     return part
 
 
+def token_sum(stats, count):
+    kinds, tokens = stats.shape
+    blocks = stats.reshape(kinds, count, tokens // count).transpose(1, 0, 2)
+    own = jnp.sum(lax.all_to_all(blocks, "seq", 0, 0, tiled=True), axis=0)
+    spread = jnp.broadcast_to(own[None], (count,) + own.shape)
+    gathered = lax.all_to_all(spread, "seq", 0, 0, tiled=True)
+    return gathered.transpose(1, 0, 2).reshape(kinds, tokens)
+
+
 def exact_pieces(values):
     pieces = []
     rest = values
@@ -119,25 +128,25 @@
         lambda q, k, v: local_attention(q, k, v, marks, log_decay), query_seq, key_seq, value_seq
     )
     stats = jnp.stack([jnp.sum(attn * attn, axis=-1), jnp.sum(attn * gain * grad_rows, axis=-1)])
-    totals = butterfly_sum(stats, "seq")
+    totals = token_sum(stats, count)
     scale = lax.rsqrt(totals[0] / features + epsilon)[:, None]
     normed = attn * scale * gain
     grad_attn = gain * grad_rows * scale - attn * (scale**3 * (totals[1] / features)[:, None])
     gain_part = jnp.sum(grad_rows * attn * scale, axis=0)
-    gain_total = butterfly_sum(gain_part, "dp")
     grad_q, grad_k, grad_v = back(grad_attn)
 
     outs = [part.reshape(count, local_tokens, width).astype(jnp.bfloat16)
             for part in (normed, grad_q, grad_k, grad_v)]
     tail = jnp.zeros((count, 8, width), jnp.bfloat16)
-    tail = tail.at[:, :3].set(jnp.broadcast_to(exact_pieces(gain_total)[None], (count, 3, width)))
+    tail = tail.at[:, :3].set(jnp.broadcast_to(exact_pieces(gain_part)[None], (count, 3, width)))
     returned = lax.all_to_all(jnp.concatenate(outs + [tail], axis=1), "seq", 0, 0, tiled=True)
     span = 4 * local_tokens
     gain_all = jnp.sum(returned[:, span:span + 3].astype(jnp.float32), axis=1).reshape(features)
     results = returned[:, :span].reshape(count, 4, local_tokens, width).transpose(1, 2, 0, 3)
     results = results.reshape(4, 1, local_tokens, features)
-    share = features // lax.axis_size("dp")
-    grad_gain = lax.dynamic_slice_in_dim(gain_all, lax.axis_index("dp") * share, share)
+    groups = lax.axis_size("dp")
+    spread = lax.all_to_all(gain_all.reshape(groups, features // groups), "dp", 0, 0, tiled=True)
+    grad_gain = jnp.sum(spread, axis=0)
     return (results[0], results[1], results[2], results[3], grad_gain)
 
 

time: 223 us -> 209 us (0.937)
  blocking collectives: 0 us -> 71.9 us
  waiting for transfers between devices: 96.1 us -> 43.1 us
  starting transfers between devices: 71.6 us -> 39.2 us
    all_to_all x0 -> x3, blocking collectives: none -> 71.9 us  [the longest x1 39.3 us: per_device(): lax.all_to_all(jnp.concatenate(outs + [tail], axis=1), 'seq', 0, 0, tiled...]
    ppermute x9 -> x0, starting transfers between devices: 53.5 us -> none  [butterfly_sum(): lax.ppermute(part, axis, [(i, i ^ distance) for i in range(count)])]
    all_to_all x1, waiting for transfers between devices: 51 us -> 3.63 us  [per_device(): lax.all_to_all(gain_all.reshape(groups, features // groups), 'dp', 0, 0,...]
    all_to_all x1, starting transfers between devices: 4.51 us -> 25.6 us  [per_device(): lax.all_to_all(gain_all.reshape(groups, features // groups), 'dp', 0, 0,...]
    ppermute x9 -> x0, waiting for transfers between devices: 5.73 us -> none  [butterfly_sum(): lax.ppermute(part, axis, [(i, i ^ distance) for i in range(count)])]
    dot_general x3, matrix products: 6.22 us -> 8.78 us  [out_sum(): inner = jnp.einsum('hij,jhe->ihe', scores, value_block, precision=highest)]
    unnamed x19 -> x31, local copies, waits for them, and re-layouts: 8.24 us -> 9.3 us
  transfers between devices with their start and end apart: 11 -> 2, of which waited for: 6 -> 2; matrix products, arithmetic and copies ran while one was open for 7% -> 3% of each run, Pallas kernels for 0% -> 0%
where the time goes in v5:
time: 209 us; the launch traced here: 208 us
  blocking collectives  71.9 us (34%)
  waiting for transfers between devices  43.1 us (21%)
  starting transfers between devices  39.2 us (19%)
  matrix products  26.1 us (12%)
  local copies, waits for them, and re-layouts  21.2 us (10%)
  other arithmetic  5.01 us (2%)
    all_to_all x1, waiting for transfers between devices, per_device(): lax.all_to_all(jnp.concatenate(pieces + [side], axis=1), 'seq', 0, 0, til...  39.4 us
    all_to_all x1, blocking collectives, per_device(): lax.all_to_all(jnp.concatenate(outs + [tail], axis=1), 'seq', 0, 0, tiled...  39.3 us
    all_to_all x1, starting transfers between devices, per_device(): lax.all_to_all(gain_all.reshape(groups, features // groups), 'dp', 0, 0,...  25.6 us
    all_to_all x1, blocking collectives, token_sum(): own = jnp.sum(lax.all_to_all(blocks, 'seq', 0, 0, tiled=True), axis=0)  21 us
    all_to_all x1, starting transfers between devices, per_device(): lax.all_to_all(jnp.concatenate(pieces + [side], axis=1), 'seq', 0, 0, til...  13.6 us
    all_to_all x1, blocking collectives, token_sum(): gathered = lax.all_to_all(spread, 'seq', 0, 0, tiled=True)  11.5 us
    unnamed x31, local copies, waits for them, and re-layouts  9.3 us
    dot_general x3, matrix products, out_sum(): inner = jnp.einsum('hij,jhe->ihe', scores, value_block, precision=highest)  8.78 us
  transfers between devices with their start and end apart: 2, of which 2 were waited for; matrix products, arithmetic and copies ran while one was open for 3% of the time, Pallas kernels for 0%

profile of v5, /device:TPU:1, one launch (start us, length us, event | category | flops | bytes accessed | tf_op | source)
XLA Modules:
  0.0 208.1 jit_solution(2665644540100412067)
XLA Ops:
  1.4 2.0 copy.89
  3.4 2.0 copy.90
  5.5 1.0 copy.91
  6.8 1.2 constant_dynamic-update-slice_fusion.3
  8.0 1.2 constant_dynamic-update-slice_fusion.2
  9.8 2.5 %copy.93 = bf16[16,520,128]{2,1,0:T(8,128)(2,1)} copy(bf16[16,520,128]{1,2,0:T(8,128)(2,1)S(1)} %pad_dynamic-update-slice_fusion) | data formatting | bytes 4259840 | tf_op jit(solution)/shard_map/concatenate | solution.py:119
  12.4 13.6 %all-to-all-start = ((bf16[16,520,128]{2,1,0:T(8,128)(2,1)}), bf16[16,520,128]{2,1,0:T(8,128)(2,1)S(1)}, u32[]{:S(2)}, u32[]{:S(2)}) async-start(bf16[16,520,128]{2,1,0:T(8,128)(2,1)} %copy.93), calls=%async_computation | async-start | bytes 4259840 | tf_op jit(solution)/shard_map/all_to_all | solution.py:119
  29.4 39.4 %all-to-all-done = bf16[16,520,128]{2,1,0:T(8,128)(2,1)S(1)} async-done(((bf16[16,520,128]{2,1,0:T(8,128)(2,1)}), bf16[16,520,128]{2,1,0:T(8,128)(2,1)S(1)}, u32[]{:S(2)}, u32[]{:S(2)}) %all-to-all-start) | async-done | bytes 2129952 | tf_op jit(solution)/shard_map/all_to_all | solution.py:119
  70.7 1.3 fusion.28
  72.6 1.6 convolution_bitcast_fusion.1
  74.2 1.0 copy-done
  75.2 1.1 fusion.1
  76.3 1.2 fusion.26
  77.6 21.0 %all_to_all.29 = f32[16,2,128]{2,1,0:T(2,128)S(1)} all-to-all(f32[16,2,128]{2,1,0:T(2,128)S(1)} %maximum_bitcast_fusion), channel_id=1, replica_groups=mesh['dp'=32,'seq'=16] {'seq'}, dimensions={0} | all-to-all | bytes 32768 | tf_op jit(solution)/shard_map/all_to_all | solution.py:85
  98.7 11.5 %all_to_all.30 = f32[16,2,128]{2,1,0:T(2,128)S(1)} all-to-all(f32[16,2,128]{2,1,0:T(2,128)S(1)} %broadcast_in_dim.22), channel_id=1, replica_groups=mesh['dp'=32,'seq'=16] {'seq'}, dimensions={0} | all-to-all | bytes 32768 | tf_op jit(solution)/shard_map/all_to_all | solution.py:87
  110.2 4.6 %fusion.20 = f32[16,128,128]{1,2,0:T(8,128)} fusion(f32[16,128,128]{2,1,0:T(8,128)} %copy-done.5, f32[16,1,128,128]{2,3,0,1:T(8,128)S(1)} %get-tuple-element.42, f32[16,128]{1,0:T(8,128)S(1)} %fusion.41, f32[16,128]{1,0:T(8,128)S(1)} %rsqrt_bitcast_fusion, f32[128]{0:T(128)S(1)} %dynamic_slice.7, bf16[4,16,128,1,128]{4,2,1,3,0:T(8,128)(2,1)S(1)} %bitcast.228), kind=kOutput, calls=%fused_computation.37 | convolution fusion | flops 403963904 | bytes 3686912 | tf_op jit(solution)/shard_map/transpose(jvp(vmap(hij,jhe->ihe)))/dot_general | solution.py:40
  114.9 3.9 %fusion.24 = f32[16,128,128]{2,1,0:T(8,128)} fusion(f32[16,128,128]{2,0,1:T(8,128)S(1)} %copy-done.1, f32[16,128]{1,0:T(8,128)S(1)} %get-tuple-element.37, f32[16,1,128,128]{2,3,0,1:T(8,128)S(1)} %get-tuple-element.42, f32[16,128]{1,0:T(8,128)S(1)} %fusion.41, f32[16,128]{1,0:T(8,128)S(1)} %rsqrt_bitcast_fusion, f32[128]{0:T(128)S(1)} %dynamic_slice.7, ...), kind=kOutput, calls=%fused_computation.41 | convolution fusion | flops 404226048 | bytes 3695104 | tf_op jit(solution)/shard_map/transpose(jvp(vmap(ihe,hef->ihf)))/dot_general | solution.py:41
  119.2 2.9 %select_multiply_fusion = f32[16,128,128]{2,1,0:T(8,128)} fusion(f32[128,128]{1,0:T(8,128)S(1)} %multiply_exponential_fusion, s32[16,128]{1,0:T(8,128)S(1)} %reduce_window_sum.18, pred[128,128]{1,0:T(8,128)(4,1)S(1)} %fusion.40, bf16[4,16,128,1,128]{4,2,1,3,0:T(8,128)(2,1)S(1)} %bitcast.231, f32[16,1,128,128]{2,3,0,1:T(8,128)S(1)} %get-tuple-element.42, ...), kind=kOutput, calls=%fused_computation.5 | convolution fusion | flops 405012480 | bytes 3260928 | tf_op jit(solution)/shard_map/transpose(jvp(vmap(hij,jhe->ihe)))/dot_general | solution.py:40
  122.1 2.9 %convolution_bitcast_fusion.3 = f32[128,128,16]{0,1,2:T(8,128)} fusion(f32[16,128]{1,0:T(8,128)S(1)} %get-tuple-element.37, bf16[4,16,128,1,128]{4,2,1,3,0:T(8,128)(2,1)S(1)} %bitcast.232, f32[16,1,128,128]{2,3,0,1:T(8,128)S(1)} %get-tuple-element.42, f32[16,128]{1,0:T(8,128)S(1)} %fusion.41, f32[16,128]{1,0:T(8,128)S(1)} %rsqrt_bitcast_fusion, ...), kind=kOutput, calls=%fused_computation.12 | convolution fusion | flops 404226048 | bytes 3170816 | tf_op jit(solution)/shard_map/transpose(jvp(vmap(ihe,hef->ihf)))/dot_general | solution.py:41
  125.0 1.2 fusion.35
  126.2 1.7 copy.106
  127.9 1.0 convolution_bitcast_fusion
  129.0 1.4 fusion.4
  131.2 1.1 fusion.12
  132.4 1.6 fusion.10
  134.1 39.3 %all_to_all.31 = bf16[16,520,128]{2,1,0:T(8,128)(2,1)S(1)} all-to-all(bf16[16,520,128]{2,1,0:T(8,128)(2,1)S(1)} %pad_dynamic-update-slice_fusion.1), channel_id=1, replica_groups=mesh['dp'=32,'seq'=16] {'seq'}, dimensions={0} | all-to-all | bytes 4259840 | tf_op jit(solution)/shard_map/all_to_all | solution.py:142
  174.1 25.6 %all-to-all-start.4 = ((f32[32,1,64]{2,1,0:T(1,128)}), f32[32,1,64]{2,1,0:T(1,128)S(1)}, u32[]{:S(2)}, u32[]{:S(2)}) async-start(f32[32,1,64]{2,1,0:T(1,128)} %all_to_all.22), calls=%async_computation.4 | async-start | bytes 32768 | tf_op jit(solution)/shard_map/all_to_all | solution.py:148
  200.2 0.9 copy.146
  201.1 0.9 copy.147
  202.0 0.9 copy.148
  203.0 0.9 copy.149
  203.9 3.6 %all-to-all-done.4 = f32[32,1,64]{2,1,0:T(1,128)S(1)} async-done(((f32[32,1,64]{2,1,0:T(1,128)}), f32[32,1,64]{2,1,0:T(1,128)S(1)}, u32[]{:S(2)}, u32[]{:S(2)}) %all-to-all-start.4) | async-done | bytes 8224 | tf_op jit(solution)/shard_map/all_to_all | solution.py:148
  (67 shorter events, 9.9 us)
Async XLA Ops:
  0.6 4.8 %copy-start.8 = (bf16[1,128,2048]{2,1,0:T(8,128)(2,1)S(1)}, bf16[1,128,2048]{2,1,0:T(8,128)(2,1)}, u32[]{:S(2)}) copy-start(bf16[1,128,2048]{2,1,0:T(8,128)(2,1)} %param.13) | copy-start | bytes 1572868
  0.6 5.8 %copy-start.9 = (bf16[1,128,2048]{2,1,0:T(8,128)(2,1)S(1)}, bf16[1,128,2048]{2,1,0:T(8,128)(2,1)}, u32[]{:S(2)}) copy-start(bf16[1,128,2048]{2,1,0:T(8,128)(2,1)} %param.17) | copy-start | bytes 1572868
  6.8 2.4 %copy-start.7 = (bf16[1,128,2048]{1,2,0:T(8,128)(2,1)S(1)}, bf16[1,128,2048]{1,2,0:T(8,128)(2,1)}, u32[]{:S(2)}) copy-start(bf16[1,128,2048]{1,2,0:T(8,128)(2,1)} %copy.91) | copy-start | bytes 1572868
  12.4 14.3 %copy-start.10 = (s32[16]{0:T(128)S(1)}, s32[16]{0:T(128)}, u32[]{:S(2)}) copy-start(s32[16]{0:T(128)} %param.15) | copy-start | bytes 196
  12.4 56.4 %all-to-all-start = ((bf16[16,520,128]{2,1,0:T(8,128)(2,1)}), bf16[16,520,128]{2,1,0:T(8,128)(2,1)S(1)}, u32[]{:S(2)}, u32[]{:S(2)}) async-start(bf16[16,520,128]{2,1,0:T(8,128)(2,1)} %copy.93), calls=%async_computation | async-start | bytes 4259840 | tf_op jit(solution)/shard_map/all_to_all | solution.py:119
  72.6 3.7 %copy-start.5 = (f32[16,128,128]{2,1,0:T(8,128)}, f32[16,128,128]{2,1,0:T(8,128)S(1)}, u32[]{:S(2)}) copy-start(f32[16,128,128]{2,1,0:T(8,128)S(1)} %select_multiply_fusion.1) | copy-start | bytes 3145732
  74.2 1.0 copy-start
  98.6 16.2 %copy-start.1 = (f32[16,128,128]{2,0,1:T(8,128)S(1)}, f32[16,128,128]{2,0,1:T(8,128)}, u32[]{:S(2)}) copy-start(f32[16,128,128]{2,0,1:T(8,128)} %copy-done) | copy-start | bytes 3145732
  127.9 2.5 %copy-start.2 = (f32[16,128,128]{2,1,0:T(8,128)S(1)}, f32[16,128,128]{2,1,0:T(8,128)}, u32[]{:S(2)}) copy-start(f32[16,128,128]{2,1,0:T(8,128)} %select_multiply_fusion) | copy-start | bytes 3145732
  127.9 2.5 %copy-start.4 = (f32[16,128,128]{2,1,0:T(8,128)S(1)}, f32[16,128,128]{2,1,0:T(8,128)}, u32[]{:S(2)}) copy-start(f32[16,128,128]{2,1,0:T(8,128)} %fusion.24) | copy-start | bytes 3145732
  127.9 2.5 %copy-start.6 = (bf16[16,520,128]{2,1,0:T(8,128)(2,1)S(1)}, bf16[16,520,128]{2,1,0:T(8,128)(2,1)}, u32[]{:S(2)}) copy-start(bf16[16,520,128]{2,1,0:T(8,128)(2,1)} %fusion.35) | copy-start | bytes 6389764
  131.2 1.2 copy-start.3
  174.1 33.4 %all-to-all-start.4 = ((f32[32,1,64]{2,1,0:T(1,128)}), f32[32,1,64]{2,1,0:T(1,128)S(1)}, u32[]{:S(2)}, u32[]{:S(2)}) async-start(f32[32,1,64]{2,1,0:T(1,128)} %all_to_all.22), calls=%async_computation.4 | async-start | bytes 32768 | tf_op jit(solution)/shard_map/all_to_all | solution.py:148

commit v6 on v4

--- a/solution.py
+++ b/solution.py
@@ -79,6 +79,12 @@
     return part
 
 
+def gathered_sum(part, axis):
+    count = lax.axis_size(axis)
+    spread = jnp.broadcast_to(part[None], (count,) + part.shape)
+    return jnp.sum(lax.all_to_all(spread, axis, 0, 0, tiled=True), axis=0)
+
+
 def exact_pieces(values):
     pieces = []
     rest = values
@@ -96,9 +102,6 @@
     tokens = local_tokens * count
     heads = features // E // count
     width = heads * E
-    log_decay = lax.dynamic_slice_in_dim(-decay_rates.astype(jnp.float32) / tokens, place * heads, heads)
-    gain = lax.dynamic_slice_in_dim(out_gain, place * width, width)
-
     mark_rows = local_tokens // width
     extra = -(-max(mark_rows, 1) // 8) * 8
     side = jnp.zeros((count, extra, width), jnp.bfloat16)
@@ -108,10 +111,13 @@
     pieces = [rows[0].reshape(local_tokens, count, width).transpose(1, 0, 2)
               for rows in (query_rows, key_rows, value_rows, cotangent)]
     moved = lax.all_to_all(jnp.concatenate(pieces + [side], axis=1), "seq", 0, 0, tiled=True)
+    moved, decay_rates, out_gain = lax.optimization_barrier((moved, decay_rates, out_gain))
     span = 4 * local_tokens
     marks = moved[:, span:span + mark_rows].reshape(tokens).astype(jnp.int32)
     moved = moved[:, :span].reshape(count, 4, local_tokens, heads, E).transpose(1, 0, 2, 3, 4)
     moved = moved.reshape(4, tokens, heads, E)
+    log_decay = lax.dynamic_slice_in_dim(-decay_rates.astype(jnp.float32) / tokens, place * heads, heads)
+    gain = lax.dynamic_slice_in_dim(out_gain, place * width, width)
 
     query_seq, key_seq, value_seq = (moved[i].astype(jnp.float32) for i in range(3))
     grad_rows = moved[3].astype(jnp.float32).reshape(tokens, width)
@@ -119,12 +125,12 @@
         lambda q, k, v: local_attention(q, k, v, marks, log_decay), query_seq, key_seq, value_seq
     )
     stats = jnp.stack([jnp.sum(attn * attn, axis=-1), jnp.sum(attn * gain * grad_rows, axis=-1)])
-    totals = butterfly_sum(stats, "seq")
+    totals = gathered_sum(stats, "seq")
     scale = lax.rsqrt(totals[0] / features + epsilon)[:, None]
     normed = attn * scale * gain
     grad_attn = gain * grad_rows * scale - attn * (scale**3 * (totals[1] / features)[:, None])
     gain_part = jnp.sum(grad_rows * attn * scale, axis=0)
-    gain_total = butterfly_sum(gain_part, "dp")
+    gain_total = gathered_sum(gain_part, "dp")
     grad_q, grad_k, grad_v = back(grad_attn)
 
     outs = [part.reshape(count, local_tokens, width).astype(jnp.bfloat16)

time: 223 us -> 212 us (0.951)
  the two profiles are of different devices: /device:TPU:1 before, /device:TPU:8 now
where the time goes in v6:
time: 212 us; the launch traced here: 211 us
  waiting for transfers between devices  109 us (51%)
  matrix products  28.4 us (13%)
  starting transfers between devices  26.2 us (12%)
  local copies, waits for them, and re-layouts  25.6 us (12%)
  blocking collectives  15.5 us (7%)
  other arithmetic  4.53 us (2%)
    all_to_all x1, waiting for transfers between devices, per_device(): lax.all_to_all(jnp.concatenate(outs + [tail], axis=1), 'seq', 0, 0, tiled...  54.8 us
    all_to_all x1, waiting for transfers between devices, per_device(): lax.all_to_all(jnp.concatenate(pieces + [side], axis=1), 'seq', 0, 0, til...  54.3 us
    all_to_all x1, blocking collectives, gathered_sum(): return jnp.sum(lax.all_to_all(spread, axis, 0, 0, tiled=True), axis=0)  15.5 us
    all_to_all x1, starting transfers between devices, per_device(): lax.all_to_all(jnp.concatenate(pieces + [side], axis=1), 'seq', 0, 0, til...  13 us
    all_to_all x1, starting transfers between devices, gathered_sum(): return jnp.sum(lax.all_to_all(spread, axis, 0, 0, tiled=True), axis=0)  9.49 us
    unnamed x29, local copies, waits for them, and re-layouts  9.24 us
    dot_general x3, matrix products, out_sum(): inner = jnp.einsum('hij,jhe->ihe', scores, value_block, precision=highest)  8.86 us
    dot_general x3, matrix products, out_sum(): jnp.einsum('ihe,hef->ihf', query_block, state_in, precision=highest)  7.93 us
  transfers between devices with their start and end apart: 3, of which 2 were waited for; matrix products, arithmetic and copies ran while one was open for 5% of the time, Pallas kernels for 0%

profile of v6, /device:TPU:8, one launch (start us, length us, event | category | flops | bytes accessed | tf_op | source)
XLA Modules:
  0.0 211.0 jit_solution(16341831398184598036)
XLA Ops:
  1.4 2.0 copy.137
  3.4 2.0 copy.138
  5.5 1.0 copy.139
  6.8 1.2 constant_dynamic-update-slice_fusion.3
  8.0 1.2 constant_dynamic-update-slice_fusion.2
  9.8 2.5 %copy.141 = bf16[16,520,128]{2,1,0:T(8,128)(2,1)} copy(bf16[16,520,128]{1,2,0:T(8,128)(2,1)S(1)} %pad_dynamic-update-slice_fusion) | data formatting | bytes 4259840 | tf_op jit(solution)/shard_map/concatenate | solution.py:113
  12.4 13.0 %all-to-all-start = ((bf16[16,520,128]{2,1,0:T(8,128)(2,1)}), bf16[16,520,128]{2,1,0:T(8,128)(2,1)S(1)}, u32[]{:S(2)}, u32[]{:S(2)}) async-start(bf16[16,520,128]{2,1,0:T(8,128)(2,1)} %copy.141), calls=%async_computation | async-start | bytes 4259840 | tf_op jit(solution)/shard_map/all_to_all | solution.py:113
  25.4 54.3 %all-to-all-done = bf16[16,520,128]{2,1,0:T(8,128)(2,1)S(1)} async-done(((bf16[16,520,128]{2,1,0:T(8,128)(2,1)}), bf16[16,520,128]{2,1,0:T(8,128)(2,1)S(1)}, u32[]{:S(2)}, u32[]{:S(2)}) %all-to-all-start) | async-done | bytes 2129952 | tf_op jit(solution)/shard_map/all_to_all | solution.py:113
  81.7 1.6 slice.97
  84.3 1.7 copy.192
  88.2 1.3 fusion.28
  90.1 1.6 convolution_bitcast_fusion.1
  91.7 1.0 copy-done
  92.7 1.1 fusion.1
  93.8 1.2 fusion.26
  95.2 15.5 %all_to_all.21 = f32[16,2,2048]{2,1,0:T(2,128)S(1)} all-to-all(f32[16,2,2048]{2,1,0:T(2,128)S(1)} %broadcast_in_dim.26), channel_id=1, replica_groups=mesh['dp'=32,'seq'=16] {'seq'}, dimensions={0} | all-to-all | bytes 524288 | tf_op jit(solution)/shard_map/all_to_all | solution.py:85
  110.9 4.7 %fusion.20 = f32[16,128,128]{1,2,0:T(8,128)} fusion(f32[16,128,128]{2,1,0:T(8,128)} %copy-done.5, f32[16,1,128,128]{2,3,0,1:T(8,128)S(1)} %get-tuple-element.48, f32[16,128]{1,0:T(8,128)S(1)} %fusion.41, f32[16,128]{1,0:T(8,128)S(1)} %bitcast.242, f32[128]{0:T(128)S(1)} %dynamic_slice.10, bf16[4,16,128,1,128]{4,2,1,3,0:T(8,128)(2,1)S(1)} %bitcast.222), kind=kOutput, calls=%fused_computation.37 | convolution fusion | flops 403963904 | bytes 3686912 | tf_op jit(solution)/shard_map/transpose(jvp(vmap(hij,jhe->ihe)))/dot_general | solution.py:40
  115.6 3.9 %fusion.24 = f32[16,128,128]{2,1,0:T(8,128)} fusion(f32[16,128,128]{2,0,1:T(8,128)S(1)} %copy-done.1, f32[16,128]{1,0:T(8,128)S(1)} %get-tuple-element.43, f32[16,1,128,128]{2,3,0,1:T(8,128)S(1)} %get-tuple-element.48, f32[16,128]{1,0:T(8,128)S(1)} %fusion.41, f32[16,128]{1,0:T(8,128)S(1)} %bitcast.243, f32[128]{0:T(128)S(1)} %dynamic_slice.10, ...), kind=kOutput, calls=%fused_computation.41 | convolution fusion | flops 404226048 | bytes 3695104 | tf_op jit(solution)/shard_map/transpose(jvp(vmap(ihe,hef->ihf)))/dot_general | solution.py:41
  119.9 2.9 %select_multiply_fusion = f32[16,128,128]{2,1,0:T(8,128)} fusion(f32[128,128]{1,0:T(8,128)S(1)} %multiply_exponential_fusion, s32[16,128]{1,0:T(8,128)S(1)} %reduce_window_sum.18, pred[128,128]{1,0:T(8,128)(4,1)S(1)} %fusion.40, bf16[4,16,128,1,128]{4,2,1,3,0:T(8,128)(2,1)S(1)} %bitcast.225, f32[16,1,128,128]{2,3,0,1:T(8,128)S(1)} %get-tuple-element.48, ...), kind=kOutput, calls=%fused_computation.5 | convolution fusion | flops 405012480 | bytes 3260928 | tf_op jit(solution)/shard_map/transpose(jvp(vmap(hij,jhe->ihe)))/dot_general | solution.py:40
  122.8 2.9 %convolution_bitcast_fusion.3 = f32[128,128,16]{0,1,2:T(8,128)} fusion(f32[16,128]{1,0:T(8,128)S(1)} %get-tuple-element.43, bf16[4,16,128,1,128]{4,2,1,3,0:T(8,128)(2,1)S(1)} %bitcast.226, f32[16,1,128,128]{2,3,0,1:T(8,128)S(1)} %get-tuple-element.48, f32[16,128]{1,0:T(8,128)S(1)} %fusion.41, f32[16,128]{1,0:T(8,128)S(1)} %bitcast.246, ...), kind=kOutput, calls=%fused_computation.12 | convolution fusion | flops 404226048 | bytes 3170816 | tf_op jit(solution)/shard_map/transpose(jvp(vmap(ihe,hef->ihf)))/dot_general | solution.py:41
  125.7 1.2 fusion.35
  127.5 9.5 %all-to-all-start.2 = ((f32[32,1,128]{2,1,0:T(1,128)}), f32[32,1,128]{2,1,0:T(1,128)S(1)}, u32[]{:S(2)}, u32[]{:S(2)}) async-start(f32[32,1,128]{2,1,0:T(1,128)} %broadcast_in_dim.27), calls=%async_computation.2 | async-start | bytes 32768 | tf_op jit(solution)/shard_map/all_to_all | solution.py:85
  137.0 1.7 copy.153
  138.7 1.0 convolution_bitcast_fusion
  139.8 1.4 fusion.4
  141.2 1.5 fusion.8
  142.7 1.8 fusion.12
  144.6 2.3 %fusion.10 = bf16[16,520,128]{2,1,0:T(8,128)(2,1)} fusion(bf16[16,520,128]{2,1,0:T(8,128)(2,1)} %fusion.12, f32[16,128,128]{1,2,0:T(8,128)S(1)} %copy-done.3, f32[16,128,128]{2,0,1:T(8,128)S(1)} %convolution_bitcast_fusion, f32[16,128]{1,0:T(8,128)S(1)} %get-tuple-element.44, bf16[4,16,128,1,128]{4,2,1,3,0:T(8,128)(2,1)S(1)} %bitcast.230), kind=kOutput, calls=%fused_computation.26 | convolution fusion | flops 403701760 | bytes 3153920 | tf_op jit(solution)/shard_map/transpose(jvp(vmap(jhe,jhf->hef)))/dot_general | solution.py:35
  147.6 3.7 %all-to-all-start.3 = ((bf16[16,520,128]{2,1,0:T(8,128)(2,1)}), bf16[16,520,128]{2,1,0:T(8,128)(2,1)S(1)}, u32[]{:S(2)}, u32[]{:S(2)}) async-start(bf16[16,520,128]{2,1,0:T(8,128)(2,1)} %pad_dynamic-update-slice_fusion.1), calls=%async_computation.3 | async-start | bytes 4259840 | tf_op jit(solution)/shard_map/all_to_all | solution.py:140
  151.3 54.8 %all-to-all-done.3 = bf16[16,520,128]{2,1,0:T(8,128)(2,1)S(1)} async-done(((bf16[16,520,128]{2,1,0:T(8,128)(2,1)}), bf16[16,520,128]{2,1,0:T(8,128)(2,1)S(1)}, u32[]{:S(2)}, u32[]{:S(2)}) %all-to-all-start.3) | async-done | bytes 2129952 | tf_op jit(solution)/shard_map/all_to_all | solution.py:140
  206.6 0.9 copy.193
  207.6 0.9 copy.194
  (64 shorter events, 11.6 us)
Async XLA Ops:
  0.6 4.8 %copy-start.7 = (bf16[1,128,2048]{2,1,0:T(8,128)(2,1)S(1)}, bf16[1,128,2048]{2,1,0:T(8,128)(2,1)}, u32[]{:S(2)}) copy-start(bf16[1,128,2048]{2,1,0:T(8,128)(2,1)} %param.13) | copy-start | bytes 1572868
  0.6 5.8 %copy-start.8 = (bf16[1,128,2048]{2,1,0:T(8,128)(2,1)S(1)}, bf16[1,128,2048]{2,1,0:T(8,128)(2,1)}, u32[]{:S(2)}) copy-start(bf16[1,128,2048]{2,1,0:T(8,128)(2,1)} %param.17) | copy-start | bytes 1572868
  6.8 2.4 %copy-start.6 = (bf16[1,128,2048]{1,2,0:T(8,128)(2,1)S(1)}, bf16[1,128,2048]{1,2,0:T(8,128)(2,1)}, u32[]{:S(2)}) copy-start(bf16[1,128,2048]{1,2,0:T(8,128)(2,1)} %copy.139) | copy-start | bytes 1572868
  12.4 67.4 %copy-start.9 = (s32[16]{0:T(128)S(1)}, s32[16]{0:T(128)}, u32[]{:S(2)}) copy-start(s32[16]{0:T(128)} %param.15) | copy-start | bytes 196
  12.4 67.4 %all-to-all-start = ((bf16[16,520,128]{2,1,0:T(8,128)(2,1)}), bf16[16,520,128]{2,1,0:T(8,128)(2,1)S(1)}, u32[]{:S(2)}, u32[]{:S(2)}) async-start(bf16[16,520,128]{2,1,0:T(8,128)(2,1)} %copy.141), calls=%async_computation | async-start | bytes 4259840 | tf_op jit(solution)/shard_map/all_to_all | solution.py:113
  90.1 3.7 %copy-start.5 = (f32[16,128,128]{2,1,0:T(8,128)}, f32[16,128,128]{2,1,0:T(8,128)S(1)}, u32[]{:S(2)}) copy-start(f32[16,128,128]{2,1,0:T(8,128)S(1)} %select_multiply_fusion.1) | copy-start | bytes 3145732
  91.7 1.0 copy-start
  110.8 4.7 %copy-start.1 = (f32[16,128,128]{2,0,1:T(8,128)S(1)}, f32[16,128,128]{2,0,1:T(8,128)}, u32[]{:S(2)}) copy-start(f32[16,128,128]{2,0,1:T(8,128)} %copy-done) | copy-start | bytes 3145732
  127.5 19.4 %all-to-all-start.2 = ((f32[32,1,128]{2,1,0:T(1,128)}), f32[32,1,128]{2,1,0:T(1,128)S(1)}, u32[]{:S(2)}, u32[]{:S(2)}) async-start(f32[32,1,128]{2,1,0:T(1,128)} %broadcast_in_dim.27), calls=%async_computation.2 | async-start | bytes 32768 | tf_op jit(solution)/shard_map/all_to_all | solution.py:85
  138.7 2.5 %copy-start.2 = (f32[16,128,128]{2,1,0:T(8,128)S(1)}, f32[16,128,128]{2,1,0:T(8,128)}, u32[]{:S(2)}) copy-start(f32[16,128,128]{2,1,0:T(8,128)} %select_multiply_fusion) | copy-start | bytes 3145732
  138.7 2.5 %copy-start.4 = (f32[16,128,128]{2,1,0:T(8,128)S(1)}, f32[16,128,128]{2,1,0:T(8,128)}, u32[]{:S(2)}) copy-start(f32[16,128,128]{2,1,0:T(8,128)} %fusion.24) | copy-start | bytes 3145732
  142.7 1.8 copy-start.3
  147.6 58.6 %all-to-all-start.3 = ((bf16[16,520,128]{2,1,0:T(8,128)(2,1)}), bf16[16,520,128]{2,1,0:T(8,128)(2,1)S(1)}, u32[]{:S(2)}, u32[]{:S(2)}) async-start(bf16[16,520,128]{2,1,0:T(8,128)(2,1)} %pad_dynamic-update-slice_fusion.1), calls=%async_computation.3 | async-start | bytes 4259840 | tf_op jit(solution)/shard_map/all_to_all | solution.py:140

commit v7 on v6

--- a/solution.py
+++ b/solution.py
@@ -102,6 +102,9 @@
     tokens = local_tokens * count
     heads = features // E // count
     width = heads * E
+    log_decay = lax.dynamic_slice_in_dim(-decay_rates.astype(jnp.float32) / tokens, place * heads, heads)
+    gain = lax.dynamic_slice_in_dim(out_gain, place * width, width)
+
     mark_rows = local_tokens // width
     extra = -(-max(mark_rows, 1) // 8) * 8
     side = jnp.zeros((count, extra, width), jnp.bfloat16)
@@ -111,13 +114,10 @@
     pieces = [rows[0].reshape(local_tokens, count, width).transpose(1, 0, 2)
               for rows in (query_rows, key_rows, value_rows, cotangent)]
     moved = lax.all_to_all(jnp.concatenate(pieces + [side], axis=1), "seq", 0, 0, tiled=True)
-    moved, decay_rates, out_gain = lax.optimization_barrier((moved, decay_rates, out_gain))
     span = 4 * local_tokens
     marks = moved[:, span:span + mark_rows].reshape(tokens).astype(jnp.int32)
     moved = moved[:, :span].reshape(count, 4, local_tokens, heads, E).transpose(1, 0, 2, 3, 4)
     moved = moved.reshape(4, tokens, heads, E)
-    log_decay = lax.dynamic_slice_in_dim(-decay_rates.astype(jnp.float32) / tokens, place * heads, heads)
-    gain = lax.dynamic_slice_in_dim(out_gain, place * width, width)
 
     query_seq, key_seq, value_seq = (moved[i].astype(jnp.float32) for i in range(3))
     grad_rows = moved[3].astype(jnp.float32).reshape(tokens, width)
@@ -130,20 +130,20 @@
     normed = attn * scale * gain
     grad_attn = gain * grad_rows * scale - attn * (scale**3 * (totals[1] / features)[:, None])
     gain_part = jnp.sum(grad_rows * attn * scale, axis=0)
-    gain_total = gathered_sum(gain_part, "dp")
     grad_q, grad_k, grad_v = back(grad_attn)
 
     outs = [part.reshape(count, local_tokens, width).astype(jnp.bfloat16)
             for part in (normed, grad_q, grad_k, grad_v)]
     tail = jnp.zeros((count, 8, width), jnp.bfloat16)
-    tail = tail.at[:, :3].set(jnp.broadcast_to(exact_pieces(gain_total)[None], (count, 3, width)))
+    tail = tail.at[:, :3].set(jnp.broadcast_to(exact_pieces(gain_part)[None], (count, 3, width)))
     returned = lax.all_to_all(jnp.concatenate(outs + [tail], axis=1), "seq", 0, 0, tiled=True)
     span = 4 * local_tokens
     gain_all = jnp.sum(returned[:, span:span + 3].astype(jnp.float32), axis=1).reshape(features)
     results = returned[:, :span].reshape(count, 4, local_tokens, width).transpose(1, 2, 0, 3)
     results = results.reshape(4, 1, local_tokens, features)
-    share = features // lax.axis_size("dp")
-    grad_gain = lax.dynamic_slice_in_dim(gain_all, lax.axis_index("dp") * share, share)
+    groups = lax.axis_size("dp")
+    spread = lax.all_to_all(gain_all.reshape(groups, features // groups), "dp", 0, 0, tiled=True)
+    grad_gain = jnp.sum(spread, axis=0)
     return (results[0], results[1], results[2], results[3], grad_gain)
 
 

time: 212 us -> 199 us (0.939)
  the two profiles are of different devices: /device:TPU:8 before, /device:TPU:1 now
where the time goes in v7:
time: 199 us
  blocking collectives  62.6 us (31%)
  waiting for transfers between devices  43.1 us (22%)
  starting transfers between devices  38.8 us (19%)
  matrix products  26.2 us (13%)
  local copies, waits for them, and re-layouts  21.3 us (11%)
  other arithmetic  5.07 us (3%)
    all_to_all x1, blocking collectives, per_device(): lax.all_to_all(jnp.concatenate(outs + [tail], axis=1), 'seq', 0, 0, tiled...  39.7 us
    all_to_all x1, waiting for transfers between devices, per_device(): lax.all_to_all(jnp.concatenate(pieces + [side], axis=1), 'seq', 0, 0, til...  39.4 us
    all_to_all x1, starting transfers between devices, per_device(): lax.all_to_all(gain_all.reshape(groups, features // groups), 'dp', 0, 0,...  25.2 us
    all_to_all x1, blocking collectives, gathered_sum(): return jnp.sum(lax.all_to_all(spread, axis, 0, 0, tiled=True), axis=0)  22.9 us
    all_to_all x1, starting transfers between devices, per_device(): lax.all_to_all(jnp.concatenate(pieces + [side], axis=1), 'seq', 0, 0, til...  13.6 us
    unnamed x31, local copies, waits for them, and re-layouts  9.3 us
    dot_general x3, matrix products, out_sum(): inner = jnp.einsum('hij,jhe->ihe', scores, value_block, precision=highest)  8.86 us
    dot_general x3, matrix products, out_sum(): jnp.einsum('ihe,hef->ihf', query_block, state_in, precision=highest)  7.92 us
  transfers between devices with their start and end apart: 2, of which 2 were waited for; matrix products, arithmetic and copies ran while one was open for 3% of the time, Pallas kernels for 0%

profile of v7, /device:TPU:1, one launch (start us, length us, event | category | flops | bytes accessed | tf_op | source)
XLA Modules:
  0.0 198.6 jit_solution(17188227998592136419)
XLA Ops:
  1.4 2.0 %copy.137 = bf16[1,128,2048]{1,2,0:T(8,128)(2,1)} copy(bf16[1,128,2048]{2,1,0:T(8,128)(2,1)} %param.11) | data formatting | bytes 1048576 | tf_op args[0]
  3.4 2.0 %copy.138 = bf16[1,128,2048]{1,2,0:T(8,128)(2,1)} copy(bf16[1,128,2048]{2,1,0:T(8,128)(2,1)} %param.12) | data formatting | bytes 1048576 | tf_op args[1]
  5.5 1.0 copy.139
  6.8 1.2 constant_dynamic-update-slice_fusion.3
  8.0 1.2 constant_dynamic-update-slice_fusion.2
  9.8 2.5 %copy.141 = bf16[16,520,128]{2,1,0:T(8,128)(2,1)} copy(bf16[16,520,128]{1,2,0:T(8,128)(2,1)S(1)} %pad_dynamic-update-slice_fusion) | data formatting | bytes 4259840 | tf_op jit(solution)/shard_map/concatenate | solution.py:116
  12.4 13.6 %all-to-all-start = ((bf16[16,520,128]{2,1,0:T(8,128)(2,1)}), bf16[16,520,128]{2,1,0:T(8,128)(2,1)S(1)}, u32[]{:S(2)}, u32[]{:S(2)}) async-start(bf16[16,520,128]{2,1,0:T(8,128)(2,1)} %copy.141), calls=%async_computation | async-start | bytes 4259840 | tf_op jit(solution)/shard_map/all_to_all | solution.py:116
  29.4 39.4 %all-to-all-done = bf16[16,520,128]{2,1,0:T(8,128)(2,1)S(1)} async-done(((bf16[16,520,128]{2,1,0:T(8,128)(2,1)}), bf16[16,520,128]{2,1,0:T(8,128)(2,1)S(1)}, u32[]{:S(2)}, u32[]{:S(2)}) %all-to-all-start) | async-done | bytes 2129952 | tf_op jit(solution)/shard_map/all_to_all | solution.py:116
  70.7 1.3 fusion.28
  72.6 1.6 convolution_bitcast_fusion.1
  74.2 1.0 copy-done
  75.2 1.1 fusion.1
  76.3 1.2 fusion.26
  77.7 22.9 %all_to_all.24 = f32[16,2,2048]{2,1,0:T(2,128)S(1)} all-to-all(f32[16,2,2048]{2,1,0:T(2,128)S(1)} %broadcast_in_dim.22), channel_id=1, replica_groups=mesh['dp'=32,'seq'=16] {'seq'}, dimensions={0} | all-to-all | bytes 524288 | tf_op jit(solution)/shard_map/all_to_all | solution.py:85
  100.7 4.7 %fusion.20 = f32[16,128,128]{1,2,0:T(8,128)} fusion(f32[16,128,128]{2,1,0:T(8,128)} %copy-done.5, f32[16,1,128,128]{2,3,0,1:T(8,128)S(1)} %get-tuple-element.42, f32[16,128]{1,0:T(8,128)S(1)} %fusion.41, f32[16,128]{1,0:T(8,128)S(1)} %bitcast.240, f32[128]{0:T(128)S(1)} %dynamic_slice.7, bf16[4,16,128,1,128]{4,2,1,3,0:T(8,128)(2,1)S(1)} %bitcast.220), kind=kOutput, calls=%fused_computation.37 | convolution fusion | flops 403963904 | bytes 3686912 | tf_op jit(solution)/shard_map/transpose(jvp(vmap(hij,jhe->ihe)))/dot_general | solution.py:40
  105.4 3.9 %fusion.24 = f32[16,128,128]{2,1,0:T(8,128)} fusion(f32[16,128,128]{2,0,1:T(8,128)S(1)} %copy-done.1, f32[16,128]{1,0:T(8,128)S(1)} %get-tuple-element.37, f32[16,1,128,128]{2,3,0,1:T(8,128)S(1)} %get-tuple-element.42, f32[16,128]{1,0:T(8,128)S(1)} %fusion.41, f32[16,128]{1,0:T(8,128)S(1)} %bitcast.241, f32[128]{0:T(128)S(1)} %dynamic_slice.7, ...), kind=kOutput, calls=%fused_computation.41 | convolution fusion | flops 404226048 | bytes 3695104 | tf_op jit(solution)/shard_map/transpose(jvp(vmap(ihe,hef->ihf)))/dot_general | solution.py:41
  109.7 2.9 %select_multiply_fusion = f32[16,128,128]{2,1,0:T(8,128)} fusion(f32[128,128]{1,0:T(8,128)S(1)} %multiply_exponential_fusion, s32[16,128]{1,0:T(8,128)S(1)} %reduce_window_sum.18, pred[128,128]{1,0:T(8,128)(4,1)S(1)} %fusion.40, bf16[4,16,128,1,128]{4,2,1,3,0:T(8,128)(2,1)S(1)} %bitcast.223, f32[16,1,128,128]{2,3,0,1:T(8,128)S(1)} %get-tuple-element.42, ...), kind=kOutput, calls=%fused_computation.5 | convolution fusion | flops 405012480 | bytes 3260928 | tf_op jit(solution)/shard_map/transpose(jvp(vmap(hij,jhe->ihe)))/dot_general | solution.py:40
  112.6 2.9 %convolution_bitcast_fusion.3 = f32[128,128,16]{0,1,2:T(8,128)} fusion(f32[16,128]{1,0:T(8,128)S(1)} %get-tuple-element.37, bf16[4,16,128,1,128]{4,2,1,3,0:T(8,128)(2,1)S(1)} %bitcast.224, f32[16,1,128,128]{2,3,0,1:T(8,128)S(1)} %get-tuple-element.42, f32[16,128]{1,0:T(8,128)S(1)} %fusion.41, f32[16,128]{1,0:T(8,128)S(1)} %bitcast.244, f32[128]{0:T(128)S(1)} %dynamic_slice.7), kind=kOutput, calls=%fused_computation.12 | convolution fusion | flops 404226048 | bytes 3170816 | tf_op jit(solution)/shard_map/transpose(jvp(vmap(ihe,hef->ihf)))/dot_general | solution.py:41
  115.6 1.2 fusion.35
  116.7 1.7 copy.153
  118.5 1.0 convolution_bitcast_fusion
  119.5 1.4 fusion.4
  121.0 0.8 fusion.8
  121.8 1.2 fusion.12
  123.0 1.6 fusion.10
  124.6 39.7 %all_to_all.25 = bf16[16,520,128]{2,1,0:T(8,128)(2,1)S(1)} all-to-all(bf16[16,520,128]{2,1,0:T(8,128)(2,1)S(1)} %pad_dynamic-update-slice_fusion.1), channel_id=1, replica_groups=mesh['dp'=32,'seq'=16] {'seq'}, dimensions={0} | all-to-all | bytes 4259840 | tf_op jit(solution)/shard_map/all_to_all | solution.py:139
  165.0 25.2 %all-to-all-start.3 = ((f32[32,1,64]{2,1,0:T(1,128)}), f32[32,1,64]{2,1,0:T(1,128)S(1)}, u32[]{:S(2)}, u32[]{:S(2)}) async-start(f32[32,1,64]{2,1,0:T(1,128)} %all_to_all.18), calls=%async_computation.3 | async-start | bytes 32768 | tf_op jit(solution)/shard_map/all_to_all | solution.py:145
  190.7 0.9 copy.195
  191.6 0.9 copy.196
  192.6 0.9 copy.197
  193.5 0.9 copy.198
  194.4 3.6 %all-to-all-done.3 = f32[32,1,64]{2,1,0:T(1,128)S(1)} async-done(((f32[32,1,64]{2,1,0:T(1,128)}), f32[32,1,64]{2,1,0:T(1,128)S(1)}, u32[]{:S(2)}, u32[]{:S(2)}) %all-to-all-start.3) | async-done | bytes 8224 | tf_op jit(solution)/shard_map/all_to_all | solution.py:145
  (64 shorter events, 9.3 us)
Async XLA Ops:
  0.6 4.8 %copy-start.8 = (bf16[1,128,2048]{2,1,0:T(8,128)(2,1)S(1)}, bf16[1,128,2048]{2,1,0:T(8,128)(2,1)}, u32[]{:S(2)}) copy-start(bf16[1,128,2048]{2,1,0:T(8,128)(2,1)} %param.13) | copy-start | bytes 1572868
  0.6 5.8 %copy-start.9 = (bf16[1,128,2048]{2,1,0:T(8,128)(2,1)S(1)}, bf16[1,128,2048]{2,1,0:T(8,128)(2,1)}, u32[]{:S(2)}) copy-start(bf16[1,128,2048]{2,1,0:T(8,128)(2,1)} %param.17) | copy-start | bytes 1572868
  6.8 2.4 %copy-start.7 = (bf16[1,128,2048]{1,2,0:T(8,128)(2,1)S(1)}, bf16[1,128,2048]{1,2,0:T(8,128)(2,1)}, u32[]{:S(2)}) copy-start(bf16[1,128,2048]{1,2,0:T(8,128)(2,1)} %copy.139) | copy-start | bytes 1572868
  12.4 14.3 %copy-start.10 = (s32[16]{0:T(128)S(1)}, s32[16]{0:T(128)}, u32[]{:S(2)}) copy-start(s32[16]{0:T(128)} %param.15) | copy-start | bytes 196
  12.4 56.4 %all-to-all-start = ((bf16[16,520,128]{2,1,0:T(8,128)(2,1)}), bf16[16,520,128]{2,1,0:T(8,128)(2,1)S(1)}, u32[]{:S(2)}, u32[]{:S(2)}) async-start(bf16[16,520,128]{2,1,0:T(8,128)(2,1)} %copy.141), calls=%async_computation | async-start | bytes 4259840 | tf_op jit(solution)/shard_map/all_to_all | solution.py:116
  72.6 3.7 %copy-start.5 = (f32[16,128,128]{2,1,0:T(8,128)}, f32[16,128,128]{2,1,0:T(8,128)S(1)}, u32[]{:S(2)}) copy-start(f32[16,128,128]{2,1,0:T(8,128)S(1)} %select_multiply_fusion.1) | copy-start | bytes 3145732
  74.2 1.0 copy-start
  100.6 4.7 %copy-start.1 = (f32[16,128,128]{2,0,1:T(8,128)S(1)}, f32[16,128,128]{2,0,1:T(8,128)}, u32[]{:S(2)}) copy-start(f32[16,128,128]{2,0,1:T(8,128)} %copy-done) | copy-start | bytes 3145732
  118.4 2.5 %copy-start.2 = (f32[16,128,128]{2,1,0:T(8,128)S(1)}, f32[16,128,128]{2,1,0:T(8,128)}, u32[]{:S(2)}) copy-start(f32[16,128,128]{2,1,0:T(8,128)} %select_multiply_fusion) | copy-start | bytes 3145732
  118.4 2.5 %copy-start.4 = (f32[16,128,128]{2,1,0:T(8,128)S(1)}, f32[16,128,128]{2,1,0:T(8,128)}, u32[]{:S(2)}) copy-start(f32[16,128,128]{2,1,0:T(8,128)} %fusion.24) | copy-start | bytes 3145732
  118.5 2.5 %copy-start.6 = (bf16[16,520,128]{2,1,0:T(8,128)(2,1)S(1)}, bf16[16,520,128]{2,1,0:T(8,128)(2,1)}, u32[]{:S(2)}) copy-start(bf16[16,520,128]{2,1,0:T(8,128)(2,1)} %fusion.35) | copy-start | bytes 6389764
  121.7 1.2 copy-start.3
  165.0 33.1 %all-to-all-start.3 = ((f32[32,1,64]{2,1,0:T(1,128)}), f32[32,1,64]{2,1,0:T(1,128)S(1)}, u32[]{:S(2)}, u32[]{:S(2)}) async-start(f32[32,1,64]{2,1,0:T(1,128)} %all_to_all.18), calls=%async_computation.3 | async-start | bytes 32768 | tf_op jit(solution)/shard_map/all_to_all | solution.py:145

commit v8 on v7

--- a/solution.py
+++ b/solution.py
@@ -1,6 +1,7 @@
 import jax
 import jax.numpy as jnp
 from jax import lax
+from jax.experimental import pallas as pl
 from jax.sharding import PartitionSpec as P
 
 E = 128
@@ -95,6 +96,28 @@
     return jnp.stack(pieces).astype(jnp.bfloat16)
 
 
+def pack_kernel(query_ref, key_ref, value_ref, grad_ref, marks_ref, out_ref):
+    rows = query_ref.shape[1]
+    for plane, ref in enumerate((query_ref, key_ref, value_ref, grad_ref)):
+        out_ref[0, plane * rows:(plane + 1) * rows, :] = ref[0]
+    side = out_ref.shape[1] - 4 * rows
+    out_ref[0, 4 * rows:, :] = jnp.zeros((side, out_ref.shape[2]), out_ref.dtype)
+    out_ref[0, 4 * rows:4 * rows + 1, :] = marks_ref[...].astype(jnp.float32).astype(out_ref.dtype)
+
+
+def pack_payload(query_rows, key_rows, value_rows, cotangent, doc_starts, count, width):
+    local_tokens = query_rows.shape[1]
+    block = pl.BlockSpec((1, local_tokens, width), lambda j: (0, 0, j))
+    return pl.pallas_call(
+        pack_kernel,
+        grid=(count,),
+        in_specs=[block, block, block, block, pl.BlockSpec((1, local_tokens), lambda j: (0, 0))],
+        out_specs=pl.BlockSpec((1, 4 * local_tokens + 8, width), lambda j: (j, 0, 0)),
+        out_shape=jax.ShapeDtypeStruct((count, 4 * local_tokens + 8, width), jnp.bfloat16),
+        cost_estimate=pl.CostEstimate(flops=0, transcendentals=0, bytes_accessed=2 * 2 * 4 * local_tokens * width * count),
+    )(query_rows, key_rows, value_rows, cotangent, doc_starts)
+
+
 def per_device(query_rows, key_rows, value_rows, doc_starts, decay_rates, out_gain, cotangent):
     count = lax.axis_size("seq")
     place = lax.axis_index("seq")
@@ -105,15 +128,9 @@
     log_decay = lax.dynamic_slice_in_dim(-decay_rates.astype(jnp.float32) / tokens, place * heads, heads)
     gain = lax.dynamic_slice_in_dim(out_gain, place * width, width)
 
-    mark_rows = local_tokens // width
-    extra = -(-max(mark_rows, 1) // 8) * 8
-    side = jnp.zeros((count, extra, width), jnp.bfloat16)
-    side = side.at[:, :mark_rows].set(
-        jnp.broadcast_to(doc_starts[0].astype(jnp.bfloat16).reshape(1, mark_rows, width), (count, mark_rows, width))
-    )
-    pieces = [rows[0].reshape(local_tokens, count, width).transpose(1, 0, 2)
-              for rows in (query_rows, key_rows, value_rows, cotangent)]
-    moved = lax.all_to_all(jnp.concatenate(pieces + [side], axis=1), "seq", 0, 0, tiled=True)
+    mark_rows = 1
+    payload = pack_payload(query_rows, key_rows, value_rows, cotangent, doc_starts, count, width)
+    moved = lax.all_to_all(payload, "seq", 0, 0, tiled=True)
     span = 4 * local_tokens
     marks = moved[:, span:span + mark_rows].reshape(tokens).astype(jnp.int32)
     moved = moved[:, :span].reshape(count, 4, local_tokens, heads, E).transpose(1, 0, 2, 3, 4)

time: 199 us -> 198 us (level)
  local copies, waits for them, and re-layouts: 21.3 us -> 10.4 us
  Pallas kernels: 0 us -> 8.9 us
    pallas_call x0 -> x1, Pallas kernels: none -> 8.9 us  [pack_payload(): pl.pallas_call(pack_kernel, grid=(count,), in_specs=[block, block, block,...]
    unnamed x31 -> x19, local copies, waits for them, and re-layouts: 9.3 us -> 1.31 us
    concatenate x2 -> x0, local copies, waits for them, and re-layouts: 2.75 us -> none  [per_device(): jnp.concatenate(pieces + [side], axis=1)]
  transfers between devices with their start and end apart: 2 -> 2, of which waited for: 2 -> 2; matrix products, arithmetic and copies ran while one was open for 3% -> 4% of each run, Pallas kernels for 0% -> 0%
where the time goes in v8:
time: 198 us; the launch traced here: 197 us
  blocking collectives  64 us (32%)
  waiting for transfers between devices  43.1 us (22%)
  starting transfers between devices  37.3 us (19%)
  matrix products  26.2 us (13%)
  local copies, waits for them, and re-layouts  10.4 us (5%)
  Pallas kernels  8.9 us (4%)
  other arithmetic  5.35 us (3%)
    all_to_all x1, blocking collectives, per_device(): lax.all_to_all(jnp.concatenate(outs + [tail], axis=1), 'seq', 0, 0, tiled...  41.2 us
    all_to_all x1, waiting for transfers between devices, per_device(): moved = lax.all_to_all(payload, 'seq', 0, 0, tiled=True)  39.4 us
    all_to_all x1, starting transfers between devices, per_device(): lax.all_to_all(gain_all.reshape(groups, features // groups), 'dp', 0, 0,...  23.8 us
    all_to_all x1, blocking collectives, gathered_sum(): return jnp.sum(lax.all_to_all(spread, axis, 0, 0, tiled=True), axis=0)  22.9 us
    all_to_all x1, starting transfers between devices, per_device(): moved = lax.all_to_all(payload, 'seq', 0, 0, tiled=True)  13.6 us
    pallas_call x1, Pallas kernels, pack_payload(): pl.pallas_call(pack_kernel, grid=(count,), in_specs=[block, block, block,...  8.9 us
    dot_general x3, matrix products, out_sum(): inner = jnp.einsum('hij,jhe->ihe', scores, value_block, precision=highest)  8.87 us
    dot_general x3, matrix products, out_sum(): jnp.einsum('ihe,hef->ihf', query_block, state_in, precision=highest)  7.93 us
  transfers between devices with their start and end apart: 2, of which 2 were waited for; matrix products, arithmetic and copies ran while one was open for 4% of the time, Pallas kernels for 0%

profile of v8, /device:TPU:1, one launch (start us, length us, event | category | flops | bytes accessed | tf_op | source)
XLA Modules:
  0.0 196.8 jit_solution(14249382524330993079)
XLA Ops:
  0.6 8.9 %shard_map.110 = bf16[16,520,128]{2,1,0:T(8,128)(2,1)} custom-call(bf16[1,128,2048]{2,1,0:T(8,128)(2,1)} %query_ref.1, bf16[1,128,2048]{2,1,0:T(8,128)(2,1)} %key_ref.1, bf16[1,128,2048]{2,1,0:T(8,128)(2,1)} %value_ref.1, bf16[1,128,2048]{2,1,0:T(8,128)(2,1)} %grad_ref.1, s32[1,128]{1,0:T(1,128)} %marks_ref.1), custom_call_target="tpu_custom_call" | custom-call | bytes 4194304 | tf_op jit(solution)/shard_map/pallas_call | solution.py:111
  9.5 13.6 %all-to-all-start = ((bf16[16,520,128]{2,1,0:T(8,128)(2,1)}), bf16[16,520,128]{2,1,0:T(8,128)(2,1)S(1)}, u32[]{:S(2)}, u32[]{:S(2)}) async-start(bf16[16,520,128]{2,1,0:T(8,128)(2,1)} %shard_map.110), calls=%async_computation | async-start | bytes 4259840 | tf_op jit(solution)/shard_map/all_to_all | solution.py:133
  23.1 0.8 dynamic_slice.7
  25.8 0.7 multiply_exponential_fusion
  26.5 39.4 %all-to-all-done = bf16[16,520,128]{2,1,0:T(8,128)(2,1)S(1)} async-done(((bf16[16,520,128]{2,1,0:T(8,128)(2,1)}), bf16[16,520,128]{2,1,0:T(8,128)(2,1)S(1)}, u32[]{:S(2)}, u32[]{:S(2)}) %all-to-all-start) | async-done | bytes 2129952 | tf_op jit(solution)/shard_map/all_to_all | solution.py:133
  66.6 0.7 gather_fusion
  67.6 0.8 slice_convert_fusion
  68.9 1.3 fusion.28
  70.8 1.6 convolution_bitcast_fusion.1
  72.4 1.0 copy-done
  73.4 1.1 fusion.1
  74.5 1.3 fusion.26
  75.9 22.9 %all_to_all.24 = f32[16,2,2048]{2,1,0:T(2,128)S(1)} all-to-all(f32[16,2,2048]{2,1,0:T(2,128)S(1)} %broadcast_in_dim.24), channel_id=1, replica_groups=mesh['dp'=32,'seq'=16] {'seq'}, dimensions={0} | all-to-all | bytes 524288 | tf_op jit(solution)/shard_map/all_to_all | solution.py:86
  98.9 4.7 %fusion.20 = f32[16,128,128]{1,2,0:T(8,128)} fusion(f32[16,128,128]{2,1,0:T(8,128)} %copy-done.6, f32[16,1,128,128]{2,3,0,1:T(8,128)S(1)} %get-tuple-element.30, f32[16,128]{1,0:T(8,128)S(1)} %fusion.41, f32[16,128]{1,0:T(8,128)S(1)} %bitcast.221, f32[128]{0:T(128)S(1)} %dynamic_slice.7, bf16[4,16,128,1,128]{4,2,1,3,0:T(8,128)(2,1)S(1)} %bitcast.205), kind=kOutput, calls=%fused_computation.37 | convolution fusion | flops 403963904 | bytes 3686912 | tf_op jit(solution)/shard_map/transpose(jvp(vmap(hij,jhe->ihe)))/dot_general | solution.py:41
  103.6 3.9 %fusion.24 = f32[16,128,128]{2,1,0:T(8,128)} fusion(f32[16,128,128]{2,0,1:T(8,128)S(1)} %copy-done.1, f32[16,128]{1,0:T(8,128)S(1)} %get-tuple-element.25, f32[16,1,128,128]{2,3,0,1:T(8,128)S(1)} %get-tuple-element.30, f32[16,128]{1,0:T(8,128)S(1)} %fusion.41, f32[16,128]{1,0:T(8,128)S(1)} %bitcast.222, f32[128]{0:T(128)S(1)} %dynamic_slice.7, ...), kind=kOutput, calls=%fused_computation.41 | convolution fusion | flops 404226048 | bytes 3695104 | tf_op jit(solution)/shard_map/transpose(jvp(vmap(ihe,hef->ihf)))/dot_general | solution.py:42
  107.9 2.9 %select_multiply_fusion = f32[16,128,128]{2,1,0:T(8,128)} fusion(f32[128,128]{1,0:T(8,128)S(1)} %multiply_exponential_fusion, s32[16,128]{1,0:T(8,128)S(1)} %reduce_window_sum.18, pred[128,128]{1,0:T(8,128)(4,1)S(1)} %fusion.40, bf16[4,16,128,1,128]{4,2,1,3,0:T(8,128)(2,1)S(1)} %bitcast.208, f32[16,1,128,128]{2,3,0,1:T(8,128)S(1)} %get-tuple-element.30, ...), kind=kOutput, calls=%fused_computation.5 | convolution fusion | flops 405012480 | bytes 3260928 | tf_op jit(solution)/shard_map/transpose(jvp(vmap(hij,jhe->ihe)))/dot_general | solution.py:41
  110.8 2.9 %convolution_bitcast_fusion.3 = f32[128,128,16]{0,1,2:T(8,128)} fusion(f32[16,128]{1,0:T(8,128)S(1)} %get-tuple-element.25, bf16[4,16,128,1,128]{4,2,1,3,0:T(8,128)(2,1)S(1)} %bitcast.209, f32[16,1,128,128]{2,3,0,1:T(8,128)S(1)} %get-tuple-element.30, f32[16,128]{1,0:T(8,128)S(1)} %fusion.41, f32[16,128]{1,0:T(8,128)S(1)} %bitcast.225, f32[128]{0:T(128)S(1)} %dynamic_slice.7), kind=kOutput, calls=%fused_computation.12 | convolution fusion | flops 404226048 | bytes 3170816 | tf_op jit(solution)/shard_map/transpose(jvp(vmap(ihe,hef->ihf)))/dot_general | solution.py:42
  113.8 1.2 fusion.35
  115.0 1.7 copy.90
  116.7 1.0 convolution_bitcast_fusion
  117.7 1.4 fusion.4
  119.2 0.8 fusion.8
  120.0 1.2 fusion.12
  121.2 1.6 fusion.10
  122.8 41.2 %all_to_all.25 = bf16[16,520,128]{2,1,0:T(8,128)(2,1)S(1)} all-to-all(bf16[16,520,128]{2,1,0:T(8,128)(2,1)S(1)} %pad_dynamic-update-slice_fusion), channel_id=1, replica_groups=mesh['dp'=32,'seq'=16] {'seq'}, dimensions={0} | all-to-all | bytes 4259840 | tf_op jit(solution)/shard_map/all_to_all | solution.py:156
  164.0 0.7 all_to_all.18
  164.7 23.8 %all-to-all-start.3 = ((f32[32,1,64]{2,1,0:T(1,128)}), f32[32,1,64]{2,1,0:T(1,128)S(1)}, u32[]{:S(2)}, u32[]{:S(2)}) async-start(f32[32,1,64]{2,1,0:T(1,128)} %all_to_all.18), calls=%async_computation.3 | async-start | bytes 32768 | tf_op jit(solution)/shard_map/all_to_all | solution.py:162
  188.9 0.9 copy.129
  189.9 0.9 copy.130
  190.8 0.9 copy.131
  191.7 0.9 copy.132
  192.7 3.6 %all-to-all-done.3 = f32[32,1,64]{2,1,0:T(1,128)S(1)} async-done(((f32[32,1,64]{2,1,0:T(1,128)}), f32[32,1,64]{2,1,0:T(1,128)S(1)}, u32[]{:S(2)}, u32[]{:S(2)}) %all-to-all-start.3) | async-done | bytes 8224 | tf_op jit(solution)/shard_map/all_to_all | solution.py:162
  (48 shorter events, 5.1 us)
Async XLA Ops:
  9.5 14.3 %copy-start.8 = (s32[16]{0:T(128)S(1)}, s32[16]{0:T(128)}, u32[]{:S(2)}) copy-start(s32[16]{0:T(128)} %param.13) | copy-start | bytes 196
  9.5 56.4 %all-to-all-start = ((bf16[16,520,128]{2,1,0:T(8,128)(2,1)}), bf16[16,520,128]{2,1,0:T(8,128)(2,1)S(1)}, u32[]{:S(2)}, u32[]{:S(2)}) async-start(bf16[16,520,128]{2,1,0:T(8,128)(2,1)} %shard_map.110), calls=%async_computation | async-start | bytes 4259840 | tf_op jit(solution)/shard_map/all_to_all | solution.py:133
  65.9 1.5 copy-start.2
  70.8 3.7 %copy-start.6 = (f32[16,128,128]{2,1,0:T(8,128)}, f32[16,128,128]{2,1,0:T(8,128)S(1)}, u32[]{:S(2)}) copy-start(f32[16,128,128]{2,1,0:T(8,128)S(1)} %select_multiply_fusion.1) | copy-start | bytes 3145732
  72.4 1.0 copy-start
  98.9 4.7 %copy-start.1 = (f32[16,128,128]{2,0,1:T(8,128)S(1)}, f32[16,128,128]{2,0,1:T(8,128)}, u32[]{:S(2)}) copy-start(f32[16,128,128]{2,0,1:T(8,128)} %copy-done) | copy-start | bytes 3145732
  116.7 2.5 %copy-start.3 = (f32[16,128,128]{2,1,0:T(8,128)S(1)}, f32[16,128,128]{2,1,0:T(8,128)}, u32[]{:S(2)}) copy-start(f32[16,128,128]{2,1,0:T(8,128)} %select_multiply_fusion) | copy-start | bytes 3145732
  116.7 2.5 %copy-start.5 = (f32[16,128,128]{2,1,0:T(8,128)S(1)}, f32[16,128,128]{2,1,0:T(8,128)}, u32[]{:S(2)}) copy-start(f32[16,128,128]{2,1,0:T(8,128)} %fusion.24) | copy-start | bytes 3145732
  116.7 2.5 %copy-start.7 = (bf16[16,520,128]{2,1,0:T(8,128)(2,1)S(1)}, bf16[16,520,128]{2,1,0:T(8,128)(2,1)}, u32[]{:S(2)}) copy-start(bf16[16,520,128]{2,1,0:T(8,128)(2,1)} %fusion.35) | copy-start | bytes 6389764
  120.0 1.2 copy-start.4
  164.7 31.6 %all-to-all-start.3 = ((f32[32,1,64]{2,1,0:T(1,128)}), f32[32,1,64]{2,1,0:T(1,128)S(1)}, u32[]{:S(2)}, u32[]{:S(2)}) async-start(f32[32,1,64]{2,1,0:T(1,128)} %all_to_all.18), calls=%async_computation.3 | async-start | bytes 32768 | tf_op jit(solution)/shard_map/all_to_all | solution.py:162

commit v9 on v8

--- a/solution.py
+++ b/solution.py
@@ -98,21 +98,25 @@
 
 def pack_kernel(query_ref, key_ref, value_ref, grad_ref, marks_ref, out_ref):
     rows = query_ref.shape[1]
-    for plane, ref in enumerate((query_ref, key_ref, value_ref, grad_ref)):
-        out_ref[0, plane * rows:(plane + 1) * rows, :] = ref[0]
-    side = out_ref.shape[1] - 4 * rows
-    out_ref[0, 4 * rows:, :] = jnp.zeros((side, out_ref.shape[2]), out_ref.dtype)
-    out_ref[0, 4 * rows:4 * rows + 1, :] = marks_ref[...].astype(jnp.float32).astype(out_ref.dtype)
+    group, depth, width = out_ref.shape
+    side = depth - 4 * rows
+    for dest in range(group):
+        columns = slice(dest * width, (dest + 1) * width)
+        for plane, ref in enumerate((query_ref, key_ref, value_ref, grad_ref)):
+            out_ref[dest, plane * rows:(plane + 1) * rows, :] = ref[0, :, columns]
+        out_ref[dest, 4 * rows:, :] = jnp.zeros((side, width), out_ref.dtype)
+        out_ref[dest, 4 * rows:4 * rows + 1, :] = marks_ref[...].astype(jnp.float32).astype(out_ref.dtype)
 
 
 def pack_payload(query_rows, key_rows, value_rows, cotangent, doc_starts, count, width):
     local_tokens = query_rows.shape[1]
-    block = pl.BlockSpec((1, local_tokens, width), lambda j: (0, 0, j))
+    group = 4 if count % 4 == 0 else 1
+    block = pl.BlockSpec((1, local_tokens, group * width), lambda j: (0, 0, j))
     return pl.pallas_call(
         pack_kernel,
-        grid=(count,),
+        grid=(count // group,),
         in_specs=[block, block, block, block, pl.BlockSpec((1, local_tokens), lambda j: (0, 0))],
-        out_specs=pl.BlockSpec((1, 4 * local_tokens + 8, width), lambda j: (j, 0, 0)),
+        out_specs=pl.BlockSpec((group, 4 * local_tokens + 8, width), lambda j: (j, 0, 0)),
         out_shape=jax.ShapeDtypeStruct((count, 4 * local_tokens + 8, width), jnp.bfloat16),
         cost_estimate=pl.CostEstimate(flops=0, transcendentals=0, bytes_accessed=2 * 2 * 4 * local_tokens * width * count),
     )(query_rows, key_rows, value_rows, cotangent, doc_starts)

time: 198 us -> 193 us (0.975)
  Pallas kernels: 8.9 us -> 3.97 us
    pallas_call x1, Pallas kernels: 8.9 us -> 3.97 us  [pack_payload(): pl.pallas_call(pack_kernel, grid=(count // group,), in_specs=[block, bloc...]
where the time goes in v9:
time: 193 us; the launch traced here: 192 us
  blocking collectives  62.6 us (32%)
  waiting for transfers between devices  43.1 us (22%)
  starting transfers between devices  38.8 us (20%)
  matrix products  26.2 us (14%)
  local copies, waits for them, and re-layouts  10.4 us (5%)
  other arithmetic  5.35 us (3%)
  Pallas kernels  3.97 us (2%)
    all_to_all x1, blocking collectives, per_device(): lax.all_to_all(jnp.concatenate(outs + [tail], axis=1), 'seq', 0, 0, tiled...  39.7 us
    all_to_all x1, waiting for transfers between devices, per_device(): moved = lax.all_to_all(payload, 'seq', 0, 0, tiled=True)  39.4 us
    all_to_all x1, starting transfers between devices, per_device(): lax.all_to_all(gain_all.reshape(groups, features // groups), 'dp', 0, 0,...  25.3 us
    all_to_all x1, blocking collectives, gathered_sum(): return jnp.sum(lax.all_to_all(spread, axis, 0, 0, tiled=True), axis=0)  22.9 us
    all_to_all x1, starting transfers between devices, per_device(): moved = lax.all_to_all(payload, 'seq', 0, 0, tiled=True)  13.6 us
    dot_general x3, matrix products, out_sum(): inner = jnp.einsum('hij,jhe->ihe', scores, value_block, precision=highest)  8.87 us
    dot_general x3, matrix products, out_sum(): jnp.einsum('ihe,hef->ihf', query_block, state_in, precision=highest)  7.93 us
    dot_general x3, matrix products, state_sum(): jnp.einsum('jhe,jhf->hef', key_block * tail[:, :, None], value_block, pre...  4.32 us
  transfers between devices with their start and end apart: 2, of which 2 were waited for; matrix products, arithmetic and copies ran while one was open for 4% of the time, Pallas kernels for 0%

profile of v9, /device:TPU:1, one launch (start us, length us, event | category | flops | bytes accessed | tf_op | source)
XLA Modules:
  0.0 192.0 jit_solution(3894701381326309516)
XLA Ops:
  0.6 4.0 %shard_map.110 = bf16[16,520,128]{2,1,0:T(8,128)(2,1)} custom-call(bf16[1,128,2048]{2,1,0:T(8,128)(2,1)} %query_ref.1, bf16[1,128,2048]{2,1,0:T(8,128)(2,1)} %key_ref.1, bf16[1,128,2048]{2,1,0:T(8,128)(2,1)} %value_ref.1, bf16[1,128,2048]{2,1,0:T(8,128)(2,1)} %grad_ref.1, s32[1,128]{1,0:T(1,128)} %marks_ref.1), custom_call_target="tpu_custom_call" | custom-call | bytes 4194304 | tf_op jit(solution)/shard_map/pallas_call | solution.py:115
  4.6 13.6 %all-to-all-start = ((bf16[16,520,128]{2,1,0:T(8,128)(2,1)}), bf16[16,520,128]{2,1,0:T(8,128)(2,1)S(1)}, u32[]{:S(2)}, u32[]{:S(2)}) async-start(bf16[16,520,128]{2,1,0:T(8,128)(2,1)} %shard_map.110), calls=%async_computation | async-start | bytes 4259840 | tf_op jit(solution)/shard_map/all_to_all | solution.py:137
  18.2 0.8 dynamic_slice.7
  20.9 0.7 multiply_exponential_fusion
  21.6 39.4 %all-to-all-done = bf16[16,520,128]{2,1,0:T(8,128)(2,1)S(1)} async-done(((bf16[16,520,128]{2,1,0:T(8,128)(2,1)}), bf16[16,520,128]{2,1,0:T(8,128)(2,1)S(1)}, u32[]{:S(2)}, u32[]{:S(2)}) %all-to-all-start) | async-done | bytes 2129952 | tf_op jit(solution)/shard_map/all_to_all | solution.py:137
  61.6 0.7 gather_fusion
  62.7 0.8 slice_convert_fusion
  64.0 1.3 fusion.28
  65.9 1.6 convolution_bitcast_fusion.1
  67.5 1.0 copy-done
  68.5 1.1 fusion.1
  69.6 1.3 fusion.26
  71.0 22.9 %all_to_all.24 = f32[16,2,2048]{2,1,0:T(2,128)S(1)} all-to-all(f32[16,2,2048]{2,1,0:T(2,128)S(1)} %broadcast_in_dim.24), channel_id=1, replica_groups=mesh['dp'=32,'seq'=16] {'seq'}, dimensions={0} | all-to-all | bytes 524288 | tf_op jit(solution)/shard_map/all_to_all | solution.py:86
  94.0 4.7 %fusion.20 = f32[16,128,128]{1,2,0:T(8,128)} fusion(f32[16,128,128]{2,1,0:T(8,128)} %copy-done.6, f32[16,1,128,128]{2,3,0,1:T(8,128)S(1)} %get-tuple-element.30, f32[16,128]{1,0:T(8,128)S(1)} %fusion.41, f32[16,128]{1,0:T(8,128)S(1)} %bitcast.221, f32[128]{0:T(128)S(1)} %dynamic_slice.7, bf16[4,16,128,1,128]{4,2,1,3,0:T(8,128)(2,1)S(1)} %bitcast.205), kind=kOutput, calls=%fused_computation.37 | convolution fusion | flops 403963904 | bytes 3686912 | tf_op jit(solution)/shard_map/transpose(jvp(vmap(hij,jhe->ihe)))/dot_general | solution.py:41
  98.7 3.9 %fusion.24 = f32[16,128,128]{2,1,0:T(8,128)} fusion(f32[16,128,128]{2,0,1:T(8,128)S(1)} %copy-done.1, f32[16,128]{1,0:T(8,128)S(1)} %get-tuple-element.25, f32[16,1,128,128]{2,3,0,1:T(8,128)S(1)} %get-tuple-element.30, f32[16,128]{1,0:T(8,128)S(1)} %fusion.41, f32[16,128]{1,0:T(8,128)S(1)} %bitcast.222, f32[128]{0:T(128)S(1)} %dynamic_slice.7, ...), kind=kOutput, calls=%fused_computation.41 | convolution fusion | flops 404226048 | bytes 3695104 | tf_op jit(solution)/shard_map/transpose(jvp(vmap(ihe,hef->ihf)))/dot_general | solution.py:42
  103.0 2.9 %select_multiply_fusion = f32[16,128,128]{2,1,0:T(8,128)} fusion(f32[128,128]{1,0:T(8,128)S(1)} %multiply_exponential_fusion, s32[16,128]{1,0:T(8,128)S(1)} %reduce_window_sum.18, pred[128,128]{1,0:T(8,128)(4,1)S(1)} %fusion.40, bf16[4,16,128,1,128]{4,2,1,3,0:T(8,128)(2,1)S(1)} %bitcast.208, f32[16,1,128,128]{2,3,0,1:T(8,128)S(1)} %get-tuple-element.30, ...), kind=kOutput, calls=%fused_computation.5 | convolution fusion | flops 405012480 | bytes 3260928 | tf_op jit(solution)/shard_map/transpose(jvp(vmap(hij,jhe->ihe)))/dot_general | solution.py:41
  105.9 2.9 %convolution_bitcast_fusion.3 = f32[128,128,16]{0,1,2:T(8,128)} fusion(f32[16,128]{1,0:T(8,128)S(1)} %get-tuple-element.25, bf16[4,16,128,1,128]{4,2,1,3,0:T(8,128)(2,1)S(1)} %bitcast.209, f32[16,1,128,128]{2,3,0,1:T(8,128)S(1)} %get-tuple-element.30, f32[16,128]{1,0:T(8,128)S(1)} %fusion.41, f32[16,128]{1,0:T(8,128)S(1)} %bitcast.225, f32[128]{0:T(128)S(1)} %dynamic_slice.7), kind=kOutput, calls=%fused_computation.12 | convolution fusion | flops 404226048 | bytes 3170816 | tf_op jit(solution)/shard_map/transpose(jvp(vmap(ihe,hef->ihf)))/dot_general | solution.py:42
  108.8 1.2 fusion.35
  110.0 1.7 copy.90
  111.8 1.0 convolution_bitcast_fusion
  112.8 1.4 fusion.4
  114.3 0.8 fusion.8
  115.1 1.2 fusion.12
  116.3 1.6 fusion.10
  117.9 39.7 %all_to_all.25 = bf16[16,520,128]{2,1,0:T(8,128)(2,1)S(1)} all-to-all(bf16[16,520,128]{2,1,0:T(8,128)(2,1)S(1)} %pad_dynamic-update-slice_fusion), channel_id=1, replica_groups=mesh['dp'=32,'seq'=16] {'seq'}, dimensions={0} | all-to-all | bytes 4259840 | tf_op jit(solution)/shard_map/all_to_all | solution.py:160
  157.6 0.7 all_to_all.18
  158.3 25.3 %all-to-all-start.3 = ((f32[32,1,64]{2,1,0:T(1,128)}), f32[32,1,64]{2,1,0:T(1,128)S(1)}, u32[]{:S(2)}, u32[]{:S(2)}) async-start(f32[32,1,64]{2,1,0:T(1,128)} %all_to_all.18), calls=%async_computation.3 | async-start | bytes 32768 | tf_op jit(solution)/shard_map/all_to_all | solution.py:166
  184.1 0.9 copy.129
  185.0 0.9 copy.130
  185.9 0.9 copy.131
  186.9 0.9 copy.132
  187.8 3.6 %all-to-all-done.3 = f32[32,1,64]{2,1,0:T(1,128)S(1)} async-done(((f32[32,1,64]{2,1,0:T(1,128)}), f32[32,1,64]{2,1,0:T(1,128)S(1)}, u32[]{:S(2)}, u32[]{:S(2)}) %all-to-all-start.3) | async-done | bytes 8224 | tf_op jit(solution)/shard_map/all_to_all | solution.py:166
  (48 shorter events, 5.1 us)
Async XLA Ops:
  4.6 14.3 %copy-start.8 = (s32[16]{0:T(128)S(1)}, s32[16]{0:T(128)}, u32[]{:S(2)}) copy-start(s32[16]{0:T(128)} %param.13) | copy-start | bytes 196
  4.6 56.4 %all-to-all-start = ((bf16[16,520,128]{2,1,0:T(8,128)(2,1)}), bf16[16,520,128]{2,1,0:T(8,128)(2,1)S(1)}, u32[]{:S(2)}, u32[]{:S(2)}) async-start(bf16[16,520,128]{2,1,0:T(8,128)(2,1)} %shard_map.110), calls=%async_computation | async-start | bytes 4259840 | tf_op jit(solution)/shard_map/all_to_all | solution.py:137
  61.0 1.5 copy-start.2
  65.8 3.7 %copy-start.6 = (f32[16,128,128]{2,1,0:T(8,128)}, f32[16,128,128]{2,1,0:T(8,128)S(1)}, u32[]{:S(2)}) copy-start(f32[16,128,128]{2,1,0:T(8,128)S(1)} %select_multiply_fusion.1) | copy-start | bytes 3145732
  67.5 1.0 copy-start
  93.9 4.7 %copy-start.1 = (f32[16,128,128]{2,0,1:T(8,128)S(1)}, f32[16,128,128]{2,0,1:T(8,128)}, u32[]{:S(2)}) copy-start(f32[16,128,128]{2,0,1:T(8,128)} %copy-done) | copy-start | bytes 3145732
  111.7 2.5 %copy-start.3 = (f32[16,128,128]{2,1,0:T(8,128)S(1)}, f32[16,128,128]{2,1,0:T(8,128)}, u32[]{:S(2)}) copy-start(f32[16,128,128]{2,1,0:T(8,128)} %select_multiply_fusion) | copy-start | bytes 3145732
  111.7 2.5 %copy-start.5 = (f32[16,128,128]{2,1,0:T(8,128)S(1)}, f32[16,128,128]{2,1,0:T(8,128)}, u32[]{:S(2)}) copy-start(f32[16,128,128]{2,1,0:T(8,128)} %fusion.24) | copy-start | bytes 3145732
  111.7 2.5 %copy-start.7 = (bf16[16,520,128]{2,1,0:T(8,128)(2,1)S(1)}, bf16[16,520,128]{2,1,0:T(8,128)(2,1)}, u32[]{:S(2)}) copy-start(bf16[16,520,128]{2,1,0:T(8,128)(2,1)} %fusion.35) | copy-start | bytes 6389764
  115.1 1.2 copy-start.4
  158.3 33.1 %all-to-all-start.3 = ((f32[32,1,64]{2,1,0:T(1,128)}), f32[32,1,64]{2,1,0:T(1,128)S(1)}, u32[]{:S(2)}, u32[]{:S(2)}) async-start(f32[32,1,64]{2,1,0:T(1,128)} %all_to_all.18), calls=%async_computation.3 | async-start | bytes 32768 | tf_op jit(solution)/shard_map/all_to_all | solution.py:166

commit v10 on v9

--- a/solution.py
+++ b/solution.py
@@ -151,20 +151,21 @@
     normed = attn * scale * gain
     grad_attn = gain * grad_rows * scale - attn * (scale**3 * (totals[1] / features)[:, None])
     gain_part = jnp.sum(grad_rows * attn * scale, axis=0)
+    gain_total = gathered_sum(gain_part, "dp")
     grad_q, grad_k, grad_v = back(grad_attn)
 
     outs = [part.reshape(count, local_tokens, width).astype(jnp.bfloat16)
             for part in (normed, grad_q, grad_k, grad_v)]
     tail = jnp.zeros((count, 8, width), jnp.bfloat16)
-    tail = tail.at[:, :3].set(jnp.broadcast_to(exact_pieces(gain_part)[None], (count, 3, width)))
-    returned = lax.all_to_all(jnp.concatenate(outs + [tail], axis=1), "seq", 0, 0, tiled=True)
+    tail = tail.at[:, :3].set(jnp.broadcast_to(exact_pieces(gain_total)[None], (count, 3, width)))
+    share = features // lax.axis_size("dp")
+    payload, offset = lax.optimization_barrier((jnp.concatenate(outs + [tail], axis=1), lax.axis_index("dp") * share))
+    returned = lax.all_to_all(payload, "seq", 0, 0, tiled=True)
     span = 4 * local_tokens
     gain_all = jnp.sum(returned[:, span:span + 3].astype(jnp.float32), axis=1).reshape(features)
     results = returned[:, :span].reshape(count, 4, local_tokens, width).transpose(1, 2, 0, 3)
     results = results.reshape(4, 1, local_tokens, features)
-    groups = lax.axis_size("dp")
-    spread = lax.all_to_all(gain_all.reshape(groups, features // groups), "dp", 0, 0, tiled=True)
-    grad_gain = jnp.sum(spread, axis=0)
+    grad_gain = lax.dynamic_slice_in_dim(gain_all, offset, share)
     return (results[0], results[1], results[2], results[3], grad_gain)
 
 

time: 193 us -> 200 us (1.036)
  the two profiles are of different devices: /device:TPU:1 before, /device:TPU:8 now
where the time goes in v10:
time: 200 us; the launch traced here: 199 us
  waiting for transfers between devices  118 us (59%)
  starting transfers between devices  30.1 us (15%)
  matrix products  28.4 us (14%)
  local copies, waits for them, and re-layouts  12.2 us (6%)
  other arithmetic  4.81 us (2%)
  Pallas kernels  3.97 us (2%)
    all_to_all x1, waiting for transfers between devices, per_device(): returned = lax.all_to_all(payload, 'seq', 0, 0, tiled=True)  55 us
    all_to_all x1, waiting for transfers between devices, per_device(): moved = lax.all_to_all(payload, 'seq', 0, 0, tiled=True)  50.9 us
    all_to_all x2, starting transfers between devices, gathered_sum(): return jnp.sum(lax.all_to_all(spread, axis, 0, 0, tiled=True), axis=0)  13.3 us
    all_to_all x1, starting transfers between devices, per_device(): moved = lax.all_to_all(payload, 'seq', 0, 0, tiled=True)  13 us
    all_to_all x2, waiting for transfers between devices, gathered_sum(): return jnp.sum(lax.all_to_all(spread, axis, 0, 0, tiled=True), axis=0)  12.1 us
    dot_general x3, matrix products, out_sum(): inner = jnp.einsum('hij,jhe->ihe', scores, value_block, precision=highest)  8.87 us
    dot_general x3, matrix products, out_sum(): jnp.einsum('ihe,hef->ihf', query_block, state_in, precision=highest)  7.92 us
    dot_general x3, matrix products, state_sum(): jnp.einsum('jhe,jhf->hef', key_block * tail[:, :, None], value_block, pre...  5.06 us
  transfers between devices with their start and end apart: 4, of which 3 were waited for; matrix products, arithmetic and copies ran while one was open for 6% of the time, Pallas kernels for 0%

profile of v10, /device:TPU:8, one launch (start us, length us, event | category | flops | bytes accessed | tf_op | source)
XLA Modules:
  0.0 199.0 jit_solution(5803406180998390389)
XLA Ops:
  0.6 4.0 %shard_map.110 = bf16[16,520,128]{2,1,0:T(8,128)(2,1)} custom-call(bf16[1,128,2048]{2,1,0:T(8,128)(2,1)} %query_ref.1, bf16[1,128,2048]{2,1,0:T(8,128)(2,1)} %key_ref.1, bf16[1,128,2048]{2,1,0:T(8,128)(2,1)} %value_ref.1, bf16[1,128,2048]{2,1,0:T(8,128)(2,1)} %grad_ref.1, s32[1,128]{1,0:T(1,128)} %marks_ref.1), custom_call_target="tpu_custom_call" | custom-call | bytes 4194304 | tf_op jit(solution)/shard_map/pallas_call | solution.py:115
  4.6 13.0 %all-to-all-start = ((bf16[16,520,128]{2,1,0:T(8,128)(2,1)}), bf16[16,520,128]{2,1,0:T(8,128)(2,1)S(1)}, u32[]{:S(2)}, u32[]{:S(2)}) async-start(bf16[16,520,128]{2,1,0:T(8,128)(2,1)} %shard_map.110), calls=%async_computation | async-start | bytes 4259840 | tf_op jit(solution)/shard_map/all_to_all | solution.py:137
  17.6 0.8 dynamic_slice.10
  20.4 0.7 multiply_exponential_fusion
  21.0 50.9 %all-to-all-done = bf16[16,520,128]{2,1,0:T(8,128)(2,1)S(1)} async-done(((bf16[16,520,128]{2,1,0:T(8,128)(2,1)}), bf16[16,520,128]{2,1,0:T(8,128)(2,1)S(1)}, u32[]{:S(2)}, u32[]{:S(2)}) %all-to-all-start) | async-done | bytes 2129952 | tf_op jit(solution)/shard_map/all_to_all | solution.py:137
  73.6 0.8 slice_convert_fusion
  75.0 1.3 fusion.28
  76.8 1.6 convolution_bitcast_fusion.1
  78.5 1.0 copy-done
  79.5 1.1 fusion.1
  80.5 1.3 fusion.26
  81.8 0.8 broadcast_in_dim.26
  82.6 3.7 %all-to-all-start.1 = ((f32[16,2,2048]{2,1,0:T(2,128)}), f32[16,2,2048]{2,1,0:T(2,128)S(1)}, u32[]{:S(2)}, u32[]{:S(2)}) async-start(f32[16,2,2048]{2,1,0:T(2,128)} %broadcast_in_dim.26), calls=%async_computation.1 | async-start | bytes 524288 | tf_op jit(solution)/shard_map/all_to_all | solution.py:86
  86.4 12.1 %all-to-all-done.1 = f32[16,2,2048]{2,1,0:T(2,128)S(1)} async-done(((f32[16,2,2048]{2,1,0:T(2,128)}), f32[16,2,2048]{2,1,0:T(2,128)S(1)}, u32[]{:S(2)}, u32[]{:S(2)}) %all-to-all-start.1) | async-done | bytes 262176 | tf_op jit(solution)/shard_map/all_to_all | solution.py:86
  98.6 4.7 %fusion.20 = f32[16,128,128]{1,2,0:T(8,128)} fusion(f32[16,128,128]{2,1,0:T(8,128)} %copy-done.6, f32[16,1,128,128]{2,3,0,1:T(8,128)S(1)} %get-tuple-element.34, f32[16,128]{1,0:T(8,128)S(1)} %fusion.41, f32[16,128]{1,0:T(8,128)S(1)} %bitcast.223, f32[128]{0:T(128)S(1)} %dynamic_slice.10, bf16[4,16,128,1,128]{4,2,1,3,0:T(8,128)(2,1)S(1)} %bitcast.207), kind=kOutput, calls=%fused_computation.37 | convolution fusion | flops 403963904 | bytes 3686912 | tf_op jit(solution)/shard_map/transpose(jvp(vmap(hij,jhe->ihe)))/dot_general | solution.py:41
  103.3 3.9 %fusion.24 = f32[16,128,128]{2,1,0:T(8,128)} fusion(f32[16,128,128]{2,0,1:T(8,128)S(1)} %copy-done.1, f32[16,128]{1,0:T(8,128)S(1)} %get-tuple-element.29, f32[16,1,128,128]{2,3,0,1:T(8,128)S(1)} %get-tuple-element.34, f32[16,128]{1,0:T(8,128)S(1)} %fusion.41, f32[16,128]{1,0:T(8,128)S(1)} %bitcast.224, f32[128]{0:T(128)S(1)} %dynamic_slice.10, ...), kind=kOutput, calls=%fused_computation.41 | convolution fusion | flops 404226048 | bytes 3695104 | tf_op jit(solution)/shard_map/transpose(jvp(vmap(ihe,hef->ihf)))/dot_general | solution.py:42
  107.6 2.9 %select_multiply_fusion = f32[16,128,128]{2,1,0:T(8,128)} fusion(f32[128,128]{1,0:T(8,128)S(1)} %multiply_exponential_fusion, s32[16,128]{1,0:T(8,128)S(1)} %reduce_window_sum.18, pred[128,128]{1,0:T(8,128)(4,1)S(1)} %fusion.40, bf16[4,16,128,1,128]{4,2,1,3,0:T(8,128)(2,1)S(1)} %bitcast.210, f32[16,1,128,128]{2,3,0,1:T(8,128)S(1)} %get-tuple-element.34, ...), kind=kOutput, calls=%fused_computation.5 | convolution fusion | flops 405012480 | bytes 3260928 | tf_op jit(solution)/shard_map/transpose(jvp(vmap(hij,jhe->ihe)))/dot_general | solution.py:41
  110.5 2.9 %convolution_bitcast_fusion.3 = f32[128,128,16]{0,1,2:T(8,128)} fusion(f32[16,128]{1,0:T(8,128)S(1)} %get-tuple-element.29, bf16[4,16,128,1,128]{4,2,1,3,0:T(8,128)(2,1)S(1)} %bitcast.211, f32[16,1,128,128]{2,3,0,1:T(8,128)S(1)} %get-tuple-element.34, f32[16,128]{1,0:T(8,128)S(1)} %fusion.41, f32[16,128]{1,0:T(8,128)S(1)} %bitcast.227, ...), kind=kOutput, calls=%fused_computation.12 | convolution fusion | flops 404226048 | bytes 3170816 | tf_op jit(solution)/shard_map/transpose(jvp(vmap(ihe,hef->ihf)))/dot_general | solution.py:42
  113.4 1.2 fusion.35
  115.2 9.6 %all-to-all-start.2 = ((f32[32,1,128]{2,1,0:T(1,128)}), f32[32,1,128]{2,1,0:T(1,128)S(1)}, u32[]{:S(2)}, u32[]{:S(2)}) async-start(f32[32,1,128]{2,1,0:T(1,128)} %broadcast_in_dim.28), calls=%async_computation.2 | async-start | bytes 32768 | tf_op jit(solution)/shard_map/all_to_all | solution.py:86
  124.9 1.7 copy.72
  126.6 1.0 convolution_bitcast_fusion
  127.6 1.4 fusion.4
  129.1 1.5 fusion.8
  130.6 1.9 fusion.12
  132.5 2.3 %fusion.10 = bf16[16,520,128]{2,1,0:T(8,128)(2,1)} fusion(bf16[16,520,128]{2,1,0:T(8,128)(2,1)} %fusion.12, f32[16,128,128]{1,2,0:T(8,128)S(1)} %copy-done.4, f32[16,128,128]{2,0,1:T(8,128)S(1)} %convolution_bitcast_fusion, f32[16,128]{1,0:T(8,128)S(1)} %get-tuple-element.30, bf16[4,16,128,1,128]{4,2,1,3,0:T(8,128)(2,1)S(1)} %bitcast.215), kind=kOutput, calls=%fused_computation.26 | convolution fusion | flops 403701760 | bytes 3153920 | tf_op jit(solution)/shard_map/transpose(jvp(vmap(jhe,jhf->hef)))/dot_general | solution.py:36
  135.5 3.7 %all-to-all-start.3 = ((bf16[16,520,128]{2,1,0:T(8,128)(2,1)}), bf16[16,520,128]{2,1,0:T(8,128)(2,1)S(1)}, u32[]{:S(2)}, u32[]{:S(2)}) async-start(bf16[16,520,128]{2,1,0:T(8,128)(2,1)} %pad_dynamic-update-slice_fusion), calls=%async_computation.3 | async-start | bytes 4259840 | tf_op jit(solution)/shard_map/all_to_all | solution.py:163
  139.2 55.0 %all-to-all-done.3 = bf16[16,520,128]{2,1,0:T(8,128)(2,1)S(1)} async-done(((bf16[16,520,128]{2,1,0:T(8,128)(2,1)}), bf16[16,520,128]{2,1,0:T(8,128)(2,1)S(1)}, u32[]{:S(2)}, u32[]{:S(2)}) %all-to-all-start.3) | async-done | bytes 2129952 | tf_op jit(solution)/shard_map/all_to_all | solution.py:163
  194.7 0.9 copy.112
  195.6 0.9 copy.113
  196.5 0.9 copy.114
  197.5 0.9 copy.115
  (49 shorter events, 6.9 us)
Async XLA Ops:
  4.6 13.8 %copy-start.7 = (s32[16]{0:T(128)S(1)}, s32[16]{0:T(128)}, u32[]{:S(2)}) copy-start(s32[16]{0:T(128)} %param.13) | copy-start | bytes 196
  4.6 67.4 %all-to-all-start = ((bf16[16,520,128]{2,1,0:T(8,128)(2,1)}), bf16[16,520,128]{2,1,0:T(8,128)(2,1)S(1)}, u32[]{:S(2)}, u32[]{:S(2)}) async-start(bf16[16,520,128]{2,1,0:T(8,128)(2,1)} %shard_map.110), calls=%async_computation | async-start | bytes 4259840 | tf_op jit(solution)/shard_map/all_to_all | solution.py:137
  72.0 1.5 copy-start.2
  76.8 3.7 %copy-start.6 = (f32[16,128,128]{2,1,0:T(8,128)}, f32[16,128,128]{2,1,0:T(8,128)S(1)}, u32[]{:S(2)}) copy-start(f32[16,128,128]{2,1,0:T(8,128)S(1)} %select_multiply_fusion.1) | copy-start | bytes 3145732
  78.5 1.0 copy-start
  82.6 15.8 %all-to-all-start.1 = ((f32[16,2,2048]{2,1,0:T(2,128)}), f32[16,2,2048]{2,1,0:T(2,128)S(1)}, u32[]{:S(2)}, u32[]{:S(2)}) async-start(f32[16,2,2048]{2,1,0:T(2,128)} %broadcast_in_dim.26), calls=%async_computation.1 | async-start | bytes 524288 | tf_op jit(solution)/shard_map/all_to_all | solution.py:86
  98.5 4.7 %copy-start.1 = (f32[16,128,128]{2,0,1:T(8,128)S(1)}, f32[16,128,128]{2,0,1:T(8,128)}, u32[]{:S(2)}) copy-start(f32[16,128,128]{2,0,1:T(8,128)} %copy-done) | copy-start | bytes 3145732
  115.2 19.5 %all-to-all-start.2 = ((f32[32,1,128]{2,1,0:T(1,128)}), f32[32,1,128]{2,1,0:T(1,128)S(1)}, u32[]{:S(2)}, u32[]{:S(2)}) async-start(f32[32,1,128]{2,1,0:T(1,128)} %broadcast_in_dim.28), calls=%async_computation.2 | async-start | bytes 32768 | tf_op jit(solution)/shard_map/all_to_all | solution.py:86
  126.6 2.5 %copy-start.3 = (f32[16,128,128]{2,1,0:T(8,128)S(1)}, f32[16,128,128]{2,1,0:T(8,128)}, u32[]{:S(2)}) copy-start(f32[16,128,128]{2,1,0:T(8,128)} %select_multiply_fusion) | copy-start | bytes 3145732
  126.6 2.5 %copy-start.5 = (f32[16,128,128]{2,1,0:T(8,128)S(1)}, f32[16,128,128]{2,1,0:T(8,128)}, u32[]{:S(2)}) copy-start(f32[16,128,128]{2,1,0:T(8,128)} %fusion.24) | copy-start | bytes 3145732
  130.6 1.9 copy-start.4
  135.5 58.7 %all-to-all-start.3 = ((bf16[16,520,128]{2,1,0:T(8,128)(2,1)}), bf16[16,520,128]{2,1,0:T(8,128)(2,1)S(1)}, u32[]{:S(2)}, u32[]{:S(2)}) async-start(bf16[16,520,128]{2,1,0:T(8,128)(2,1)} %pad_dynamic-update-slice_fusion), calls=%async_computation.3 | async-start | bytes 4259840 | tf_op jit(solution)/shard_map/all_to_all | solution.py:163

commit v11 on v9

--- a/solution.py
+++ b/solution.py
@@ -110,7 +110,7 @@
 
 def pack_payload(query_rows, key_rows, value_rows, cotangent, doc_starts, count, width):
     local_tokens = query_rows.shape[1]
-    group = 4 if count % 4 == 0 else 1
+    group = 8 if count % 8 == 0 else 1
     block = pl.BlockSpec((1, local_tokens, group * width), lambda j: (0, 0, j))
     return pl.pallas_call(
         pack_kernel,

time: 193 us -> 191 us (0.990)
  no operation moved by 1% of the time
where the time goes in v11:
time: 191 us
  blocking collectives  64 us (34%)
  waiting for transfers between devices  43.1 us (23%)
  starting transfers between devices  37.3 us (20%)
  matrix products  26.2 us (14%)
  local copies, waits for them, and re-layouts  10.4 us (5%)
  other arithmetic  5.35 us (3%)
  Pallas kernels  2.77 us (1%)
    all_to_all x1, blocking collectives, per_device(): lax.all_to_all(jnp.concatenate(outs + [tail], axis=1), 'seq', 0, 0, tiled...  41.2 us
    all_to_all x1, waiting for transfers between devices, per_device(): moved = lax.all_to_all(payload, 'seq', 0, 0, tiled=True)  39.4 us
    all_to_all x1, starting transfers between devices, per_device(): lax.all_to_all(gain_all.reshape(groups, features // groups), 'dp', 0, 0,...  23.8 us
    all_to_all x1, blocking collectives, gathered_sum(): return jnp.sum(lax.all_to_all(spread, axis, 0, 0, tiled=True), axis=0)  22.9 us
    all_to_all x1, starting transfers between devices, per_device(): moved = lax.all_to_all(payload, 'seq', 0, 0, tiled=True)  13.6 us
    dot_general x3, matrix products, out_sum(): inner = jnp.einsum('hij,jhe->ihe', scores, value_block, precision=highest)  8.87 us
    dot_general x3, matrix products, out_sum(): jnp.einsum('ihe,hef->ihf', query_block, state_in, precision=highest)  7.93 us
    dot_general x3, matrix products, state_sum(): jnp.einsum('jhe,jhf->hef', key_block * tail[:, :, None], value_block, pre...  4.33 us
  transfers between devices with their start and end apart: 2, of which 2 were waited for; matrix products, arithmetic and copies ran while one was open for 4% of the time, Pallas kernels for 0%

profile of v11, /device:TPU:1, one launch (start us, length us, event | category | flops | bytes accessed | tf_op | source)
XLA Modules:
  0.0 190.7 jit_solution(5078557959690785830)
XLA Ops:
  0.6 2.8 %shard_map.110 = bf16[16,520,128]{2,1,0:T(8,128)(2,1)} custom-call(bf16[1,128,2048]{2,1,0:T(8,128)(2,1)} %query_ref.1, bf16[1,128,2048]{2,1,0:T(8,128)(2,1)} %key_ref.1, bf16[1,128,2048]{2,1,0:T(8,128)(2,1)} %value_ref.1, bf16[1,128,2048]{2,1,0:T(8,128)(2,1)} %grad_ref.1, s32[1,128]{1,0:T(1,128)} %marks_ref.1), custom_call_target="tpu_custom_call" | custom-call | bytes 4194304 | tf_op jit(solution)/shard_map/pallas_call | solution.py:115
  3.4 13.6 %all-to-all-start = ((bf16[16,520,128]{2,1,0:T(8,128)(2,1)}), bf16[16,520,128]{2,1,0:T(8,128)(2,1)S(1)}, u32[]{:S(2)}, u32[]{:S(2)}) async-start(bf16[16,520,128]{2,1,0:T(8,128)(2,1)} %shard_map.110), calls=%async_computation | async-start | bytes 4259840 | tf_op jit(solution)/shard_map/all_to_all | solution.py:137
  17.0 0.8 dynamic_slice.7
  19.7 0.7 multiply_exponential_fusion
  20.4 39.4 %all-to-all-done = bf16[16,520,128]{2,1,0:T(8,128)(2,1)S(1)} async-done(((bf16[16,520,128]{2,1,0:T(8,128)(2,1)}), bf16[16,520,128]{2,1,0:T(8,128)(2,1)S(1)}, u32[]{:S(2)}, u32[]{:S(2)}) %all-to-all-start) | async-done | bytes 2129952 | tf_op jit(solution)/shard_map/all_to_all | solution.py:137
  60.4 0.7 gather_fusion
  61.5 0.8 slice_convert_fusion
  62.8 1.3 fusion.28
  64.7 1.6 convolution_bitcast_fusion.1
  66.3 1.0 copy-done
  67.3 1.1 fusion.1
  68.4 1.3 fusion.26
  69.8 22.9 %all_to_all.24 = f32[16,2,2048]{2,1,0:T(2,128)S(1)} all-to-all(f32[16,2,2048]{2,1,0:T(2,128)S(1)} %broadcast_in_dim.24), channel_id=1, replica_groups=mesh['dp'=32,'seq'=16] {'seq'}, dimensions={0} | all-to-all | bytes 524288 | tf_op jit(solution)/shard_map/all_to_all | solution.py:86
  92.8 4.7 %fusion.20 = f32[16,128,128]{1,2,0:T(8,128)} fusion(f32[16,128,128]{2,1,0:T(8,128)} %copy-done.6, f32[16,1,128,128]{2,3,0,1:T(8,128)S(1)} %get-tuple-element.30, f32[16,128]{1,0:T(8,128)S(1)} %fusion.41, f32[16,128]{1,0:T(8,128)S(1)} %bitcast.221, f32[128]{0:T(128)S(1)} %dynamic_slice.7, bf16[4,16,128,1,128]{4,2,1,3,0:T(8,128)(2,1)S(1)} %bitcast.205), kind=kOutput, calls=%fused_computation.37 | convolution fusion | flops 403963904 | bytes 3686912 | tf_op jit(solution)/shard_map/transpose(jvp(vmap(hij,jhe->ihe)))/dot_general | solution.py:41
  97.5 3.9 %fusion.24 = f32[16,128,128]{2,1,0:T(8,128)} fusion(f32[16,128,128]{2,0,1:T(8,128)S(1)} %copy-done.1, f32[16,128]{1,0:T(8,128)S(1)} %get-tuple-element.25, f32[16,1,128,128]{2,3,0,1:T(8,128)S(1)} %get-tuple-element.30, f32[16,128]{1,0:T(8,128)S(1)} %fusion.41, f32[16,128]{1,0:T(8,128)S(1)} %bitcast.222, f32[128]{0:T(128)S(1)} %dynamic_slice.7, ...), kind=kOutput, calls=%fused_computation.41 | convolution fusion | flops 404226048 | bytes 3695104 | tf_op jit(solution)/shard_map/transpose(jvp(vmap(ihe,hef->ihf)))/dot_general | solution.py:42
  101.8 2.9 %select_multiply_fusion = f32[16,128,128]{2,1,0:T(8,128)} fusion(f32[128,128]{1,0:T(8,128)S(1)} %multiply_exponential_fusion, s32[16,128]{1,0:T(8,128)S(1)} %reduce_window_sum.18, pred[128,128]{1,0:T(8,128)(4,1)S(1)} %fusion.40, bf16[4,16,128,1,128]{4,2,1,3,0:T(8,128)(2,1)S(1)} %bitcast.208, f32[16,1,128,128]{2,3,0,1:T(8,128)S(1)} %get-tuple-element.30, ...), kind=kOutput, calls=%fused_computation.5 | convolution fusion | flops 405012480 | bytes 3260928 | tf_op jit(solution)/shard_map/transpose(jvp(vmap(hij,jhe->ihe)))/dot_general | solution.py:41
  104.7 2.9 %convolution_bitcast_fusion.3 = f32[128,128,16]{0,1,2:T(8,128)} fusion(f32[16,128]{1,0:T(8,128)S(1)} %get-tuple-element.25, bf16[4,16,128,1,128]{4,2,1,3,0:T(8,128)(2,1)S(1)} %bitcast.209, f32[16,1,128,128]{2,3,0,1:T(8,128)S(1)} %get-tuple-element.30, f32[16,128]{1,0:T(8,128)S(1)} %fusion.41, f32[16,128]{1,0:T(8,128)S(1)} %bitcast.225, f32[128]{0:T(128)S(1)} %dynamic_slice.7), kind=kOutput, calls=%fused_computation.12 | convolution fusion | flops 404226048 | bytes 3170816 | tf_op jit(solution)/shard_map/transpose(jvp(vmap(ihe,hef->ihf)))/dot_general | solution.py:42
  107.7 1.2 fusion.35
  108.8 1.7 copy.90
  110.6 1.0 convolution_bitcast_fusion
  111.6 1.4 fusion.4
  113.1 0.8 fusion.8
  113.9 1.2 fusion.12
  115.1 1.6 fusion.10
  116.7 41.2 %all_to_all.25 = bf16[16,520,128]{2,1,0:T(8,128)(2,1)S(1)} all-to-all(bf16[16,520,128]{2,1,0:T(8,128)(2,1)S(1)} %pad_dynamic-update-slice_fusion), channel_id=1, replica_groups=mesh['dp'=32,'seq'=16] {'seq'}, dimensions={0} | all-to-all | bytes 4259840 | tf_op jit(solution)/shard_map/all_to_all | solution.py:160
  157.9 0.7 all_to_all.18
  158.6 23.8 %all-to-all-start.3 = ((f32[32,1,64]{2,1,0:T(1,128)}), f32[32,1,64]{2,1,0:T(1,128)S(1)}, u32[]{:S(2)}, u32[]{:S(2)}) async-start(f32[32,1,64]{2,1,0:T(1,128)} %all_to_all.18), calls=%async_computation.3 | async-start | bytes 32768 | tf_op jit(solution)/shard_map/all_to_all | solution.py:166
  182.8 0.9 copy.129
  183.7 0.9 copy.130
  184.7 0.9 copy.131
  185.6 0.9 copy.132
  186.5 3.6 %all-to-all-done.3 = f32[32,1,64]{2,1,0:T(1,128)S(1)} async-done(((f32[32,1,64]{2,1,0:T(1,128)}), f32[32,1,64]{2,1,0:T(1,128)S(1)}, u32[]{:S(2)}, u32[]{:S(2)}) %all-to-all-start.3) | async-done | bytes 8224 | tf_op jit(solution)/shard_map/all_to_all | solution.py:166
  (48 shorter events, 5.1 us)
Async XLA Ops:
  3.4 14.3 %copy-start.8 = (s32[16]{0:T(128)S(1)}, s32[16]{0:T(128)}, u32[]{:S(2)}) copy-start(s32[16]{0:T(128)} %param.13) | copy-start | bytes 196
  3.4 56.4 %all-to-all-start = ((bf16[16,520,128]{2,1,0:T(8,128)(2,1)}), bf16[16,520,128]{2,1,0:T(8,128)(2,1)S(1)}, u32[]{:S(2)}, u32[]{:S(2)}) async-start(bf16[16,520,128]{2,1,0:T(8,128)(2,1)} %shard_map.110), calls=%async_computation | async-start | bytes 4259840 | tf_op jit(solution)/shard_map/all_to_all | solution.py:137
  59.8 1.5 copy-start.2
  64.6 3.7 %copy-start.6 = (f32[16,128,128]{2,1,0:T(8,128)}, f32[16,128,128]{2,1,0:T(8,128)S(1)}, u32[]{:S(2)}) copy-start(f32[16,128,128]{2,1,0:T(8,128)S(1)} %select_multiply_fusion.1) | copy-start | bytes 3145732
  66.3 1.0 copy-start
  92.7 4.7 %copy-start.1 = (f32[16,128,128]{2,0,1:T(8,128)S(1)}, f32[16,128,128]{2,0,1:T(8,128)}, u32[]{:S(2)}) copy-start(f32[16,128,128]{2,0,1:T(8,128)} %copy-done) | copy-start | bytes 3145732
  110.5 2.5 %copy-start.3 = (f32[16,128,128]{2,1,0:T(8,128)S(1)}, f32[16,128,128]{2,1,0:T(8,128)}, u32[]{:S(2)}) copy-start(f32[16,128,128]{2,1,0:T(8,128)} %select_multiply_fusion) | copy-start | bytes 3145732
  110.5 2.5 %copy-start.5 = (f32[16,128,128]{2,1,0:T(8,128)S(1)}, f32[16,128,128]{2,1,0:T(8,128)}, u32[]{:S(2)}) copy-start(f32[16,128,128]{2,1,0:T(8,128)} %fusion.24) | copy-start | bytes 3145732
  110.6 2.5 %copy-start.7 = (bf16[16,520,128]{2,1,0:T(8,128)(2,1)S(1)}, bf16[16,520,128]{2,1,0:T(8,128)(2,1)}, u32[]{:S(2)}) copy-start(bf16[16,520,128]{2,1,0:T(8,128)(2,1)} %fusion.35) | copy-start | bytes 6389764
  113.9 1.2 copy-start.4
  158.6 31.6 %all-to-all-start.3 = ((f32[32,1,64]{2,1,0:T(1,128)}), f32[32,1,64]{2,1,0:T(1,128)S(1)}, u32[]{:S(2)}, u32[]{:S(2)}) async-start(f32[32,1,64]{2,1,0:T(1,128)} %all_to_all.18), calls=%async_computation.3 | async-start | bytes 32768 | tf_op jit(solution)/shard_map/all_to_all | solution.py:166
